TPU v7x, 32 devices: a whole 2x2x4 slice. The times are simulated.
32 devices in a mesh: groups: 2 (over y), sta: 4 (over z), band: 2 (over x), seg: 2 (over core).
Axes of the slice: x: 2, y: 2, z: 4, core: 2. Of those that a mesh axis runs over, the one named last changes fastest.
Arguments:
- spectra: float32 [8, 2, 512, 1024], P('seg', None, 'band', ('groups', 'sta')), parts along dimension 3, may hold values from -600 to 600, as said below
- plan: int32 [4], P('groups'), parts along dimension 0, may hold values from 0 to 3
- pair_mask: int32 [8, 4], P('groups'), parts along dimension 0, may hold values 0 or 1
Outputs:
- correlations: bfloat16 [2, 256, 128, 1024], P(None, 'band', 'seg', ('groups', 'sta')), parts along dimension 3
There are 2 independent parts, one for each index of `groups`. A program takes and returns all parts, laid end to end along the dimension named above; each array names one. Nothing has to cross between parts.
Inputs may be any that keep to these rules, and one draw needn't show every extreme that they name: spectra of the station records, real part first and imaginary part second.
All inputs are finite; a program needn't handle non-finite values.
Results may differ from a plain program's by a relative error of at most 0.0072.
Values may be sent and summed in bfloat16 or wider, within the bound.
No kernel may reach another device: no remote copies, remote signals or barrier semaphores. Data moves between devices by JAX's collectives and lax.ppermute only.
A program may use at most 128 MiB of HBM per device.

v0:
```python
import math

import jax
import jax.numpy as jnp
from jax import lax
from jax.sharding import PartitionSpec as P

SEGS = 8
STEPS = 2
SRC = 128
BLK_DEV = 1
BAND_BINS = 256
HALF = 64
LAGS = 128


EPSILON = 1e-06


def padded(cells, sides, width):
    for axis, dim in sides:
        count = lax.axis_size(axis)
        ends = count - 1
        head = lax.slice_in_dim(cells, 0, width, axis=dim)
        tail = lax.slice_in_dim(cells, cells.shape[dim] - width, cells.shape[dim], axis=dim)
        cells = jnp.concatenate(
            [
                lax.ppermute(tail, axis, [(i, (i + 1) % count) for i in range(ends)]),
                cells,
                lax.ppermute(head, axis, [((i + 1) % count, i) for i in range(ends)]),
            ],
            axis=dim,
        )
    return cells


def from_root(block, axis, source):
    block = jnp.where(lax.axis_index(axis) == source, block, jnp.zeros_like(block))
    return lax.psum(block, axis)


def lag_table(first_bin):
    bin_number = first_bin + jnp.arange(BAND_BINS, dtype=jnp.int32)
    lag_number = jnp.arange(LAGS, dtype=jnp.int32) - LAGS // 2
    phase_steps = jnp.remainder(lag_number[:, None] * bin_number[None, :], 2 * BAND_BINS)
    phases = phase_steps.astype(jnp.float32) * (math.pi / BAND_BINS)
    normalizer = 1.0 / math.sqrt(SEGS * BAND_BINS)
    weights = jnp.stack([jnp.cos(phases), -jnp.sin(phases)], axis=2) * normalizer
    return weights.astype(jnp.bfloat16).reshape(LAGS, 2 * BAND_BINS)


def cross_terms(sources, receivers):
    src_real = sources[:, 0]
    src_imag = sources[:, 1]
    left_stack = jnp.stack(
        [jnp.concatenate([src_real, src_imag], 0), jnp.concatenate([src_imag, -src_real], 0)], 0
    )
    right_stack = jnp.concatenate([receivers[:, 0], receivers[:, 1]], 0)
    cross_spectra = jnp.einsum(
        "ctfs,tfn->fcsn", left_stack, right_stack, preferred_element_type=jnp.float32
    )
    return cross_spectra.astype(jnp.bfloat16)


def local(spectra, plan, pair_mask):
    seg_local = spectra.shape[0]
    band_bins = spectra.shape[2]
    sta_local = spectra.shape[3]
    band_position = lax.axis_index("band")
    sta_position = lax.axis_index("sta")
    seg_position = lax.axis_index("seg")
    total_bins = band_bins * lax.axis_size("band")
    half_sources = SRC // lax.axis_size("seg")
    amplitude = jnp.sqrt(spectra[:, 0] ** 2 + spectra[:, 1] ** 2)
    extended = padded(amplitude, (("band", 1),), HALF)
    block_width = 2 * HALF
    block_count = band_bins // block_width
    lower_part = extended[:, : block_count * block_width].reshape(
        seg_local, block_count, block_width, sta_local
    )
    upper_part = extended[:, block_width:].reshape(seg_local, block_count, block_width, sta_local)
    windows = jnp.concatenate([lower_part, upper_part], axis=2)
    offsets = jnp.arange(2 * block_width, dtype=jnp.int32)[:, None]
    targets = jnp.arange(block_width, dtype=jnp.int32)[None, :]
    band_matrix = ((offsets >= targets) & (offsets <= targets + 2 * HALF)).astype(jnp.float32)
    window_sums = jnp.einsum("tbgn,gf->tbfn", windows, band_matrix, precision=lax.Precision.HIGHEST)
    window_sums = window_sums.reshape(seg_local, band_bins, sta_local)
    bin_number = band_position * band_bins + jnp.arange(band_bins, dtype=jnp.int32)
    in_range = (
        jnp.minimum(bin_number + HALF, total_bins - 1) - jnp.maximum(bin_number - HALF, 0) + 1
    ).astype(jnp.float32)
    smooth = window_sums / in_range[None, :, None]
    white = (spectra / (smooth[:, None] + EPSILON)).astype(jnp.bfloat16)
    receivers = lax.all_gather(white, "seg", axis=0, tiled=True)
    own_half = lax.all_to_all(white, "seg", split_axis=3, concat_axis=0, tiled=True)
    candidates = lax.all_gather(own_half, "sta", axis=0, tiled=False)
    blk_dev = sta_local // SRC
    lag_weights = lag_table(band_position * band_bins).reshape(LAGS, band_bins, 2)
    receiver_ids = sta_position * sta_local + jnp.arange(sta_local, dtype=jnp.int32)
    block_columns = jnp.arange(pair_mask.shape[1], dtype=jnp.int32)
    block_onehot = ((receiver_ids // SRC)[:, None] == block_columns[None, :]).astype(jnp.float32)
    results = []
    for step_number in range(STEPS):
        block_number = plan[step_number]
        owner_position = block_number // blk_dev
        held = lax.dynamic_index_in_dim(candidates, owner_position, 0, keepdims=False)
        sources = lax.dynamic_slice_in_dim(
            held, (block_number % blk_dev) * half_sources, half_sources, 3
        )
        cross_spectra = cross_terms(sources, receivers)
        correlated = lax.dot_general(
            lag_weights,
            cross_spectra,
            (((1, 2), (0, 1)), ((), ())),
            preferred_element_type=jnp.float32,
        )
        mask_row = pair_mask[block_number].astype(jnp.float32)
        allowed = jnp.sum(block_onehot * mask_row[None, :], axis=1)
        source_ids = (
            block_number * SRC
            + seg_position * half_sources
            + jnp.arange(half_sources, dtype=jnp.int32)
        )
        keep_pairs = (source_ids[:, None] != receiver_ids[None, :]).astype(jnp.float32) * allowed[
            None, :
        ]
        results.append((correlated * keep_pairs[None]).astype(jnp.bfloat16))
    return jnp.stack(results, 0)


def solution(mesh):
    return jax.shard_map(
        local,
        mesh=mesh,
        in_specs=(P("seg", None, "band", ("groups", "sta")), P("groups"), P("groups", None)),
        out_specs=P(None, "band", "seg", ("groups", "sta")),
        check_vma=False,
    )
```

profile of v0, /device:TPU:0, one launch (start us, length us, event | category | flops | bytes accessed | tf_op | source)
XLA Modules:
  0.0 115.3 jit_solution(5819262840081034191)
XLA Ops:
  6.5 1.4 %sqrt_bitcast_fusion = f32[4,256,128]{2,1,0:T(8,128)S(1)} fusion(f32[4,2,256,128]{3,2,1,0:T(8,128)} %param.3), kind=kLoop, calls=%fused_computation.37 | loop fusion | flops 393216 | bytes 1572864 | tf_op jit(solution)/shard_map/sqrt | solution.py:74
  7.9 4.9 %collective-permute-start = (f32[4,64,128]{2,1,0:T(8,128)S(1)}, f32[4,64,128]{2,1,0:T(8,128)S(1)}, u32[]{:S(2)}, u32[]{:S(2)}) collective-permute-start(f32[4,64,128]{2,1,0:T(8,128)S(1)} %get-tuple-element.21), channel_id=1, source_target_pairs={{0,2},{1,3},{4,6},{5,7},{8,10},{9,11},{12,14},{13,15},{16,18},{17,... | collective-permute-start | bytes 393224 | tf_op jit(solution)/shard_map/ppermute | solution.py:28
  12.8 1.3 %collective-permute-start.1 = (f32[4,64,128]{2,1,0:T(8,128)S(1)}, f32[4,64,128]{2,1,0:T(8,128)S(1)}, u32[]{:S(2)}, u32[]{:S(2)}) collective-permute-start(f32[4,64,128]{2,1,0:T(8,128)S(1)} %get-tuple-element.22), channel_id=1, source_target_pairs={{2,0},{3,1},{6,4},{7,5},{10,8},{11,9},{14,12},{15,13},{18,16},{19,... | collective-permute-start | bytes 393224 | tf_op jit(solution)/shard_map/ppermute | solution.py:30
  14.2 1.4 %collective-permute-done = f32[4,64,128]{2,1,0:T(8,128)S(1)} collective-permute-done((f32[4,64,128]{2,1,0:T(8,128)S(1)}, f32[4,64,128]{2,1,0:T(8,128)S(1)}, u32[]{:S(2)}, u32[]{:S(2)}) %collective-permute-start) | collective-permute-done | bytes 131104 | tf_op jit(solution)/shard_map/ppermute | solution.py:28
  15.6 4.1 %collective-permute-done.1 = f32[4,64,128]{2,1,0:T(8,128)S(1)} collective-permute-done((f32[4,64,128]{2,1,0:T(8,128)S(1)}, f32[4,64,128]{2,1,0:T(8,128)S(1)}, u32[]{:S(2)}, u32[]{:S(2)}) %collective-permute-start.1) | collective-permute-done | bytes 131104 | tf_op jit(solution)/shard_map/ppermute | solution.py:30
  20.5 0.9 divide_convert_fusion
  21.4 1.4 %copy.47 = bf16[4,2,256,128]{2,1,0,3:T(2,128)(2,1)S(1)} copy(bf16[4,2,256,128]{3,2,1,0:T(8,128)(2,1)} %divide_convert_fusion) | data formatting | bytes 1048576 | tf_op jit(solution)/shard_map/convert_element_type | solution.py:93
  22.9 4.2 %all_to_all.15 = bf16[4,2,256,128]{2,1,0,3:T(2,128)(2,1)S(1)} all-to-all(bf16[4,2,256,128]{2,1,0,3:T(2,128)(2,1)S(1)} %copy.47), channel_id=1, replica_groups=mesh['groups'=2,'sta'=4,'band'=2,'seg'=2] {'seg'}, dimensions={3} | all-to-all | bytes 1048576 | tf_op jit(solution)/shard_map/all_to_all | solution.py:95
  27.1 0.8 copy.49
  28.0 0.6 fusion.54
  34.0 0.7 compare_select_fusion.1
  34.7 1.3 %fusion.36 = (f32[128,256,1]{1,0,2:T(8,128)S(1)}, f32[128,256,1]{1,0,2:T(8,128)}) fusion(s32[256]{0:T(256)S(1)} %get-tuple-element.36, s32[128]{0:T(128)S(1)} %iota_add_fusion.5), kind=kLoop, calls=%fused_computation.55 | loop fusion | flops 491520 | bytes 263680 | tf_op jit(solution)/shard_map/cos | solution.py:48
  36.0 1.3 %fusion.50 = (bf16[8,1,256,128]{3,2,1,0:T(8,128)(2,1)S(1)}, bf16[8,1,256,128]{3,2,1,0:T(8,128)(2,1)S(1)}) fusion(bf16[8,2,256,128]{3,2,1,0:T(8,128)(2,1)} %all-gather.5.cloned.1.call-done), kind=kLoop, calls=%fused_computation.87 | loop fusion | bytes 2097152 | tf_op jit(solution)/shard_map/slice | solution.py:58
  37.9 41.4 %all-gather.3.cloned.1.call-done = bf16[4,8,2,256,64]{3,4,2,1,0:T(8,128)(2,1)} async-done(((bf16[1,8,2,256,64]{3,4,2,1,0:T(8,128)(2,1)}), bf16[4,8,2,256,64]{3,4,2,1,0:T(8,128)(2,1)}) %all-gather.3.cloned.1.call-update) | async-done | bytes 2097168 | tf_op jit(solution)/shard_map/all_gather | solution.py:96
  79.3 1.3 %dynamic-slice_bitcast_fusion.1 = (bf16[8,2,256,64]{2,3,1,0:T(8,128)(2,1)S(1)}, bf16[8,2,256,64]{2,3,1,0:T(8,128)(2,1)S(1)}) fusion(bf16[4,8,2,256,64]{3,4,2,1,0:T(8,128)(2,1)} %all-gather.3.cloned.1.call-done, s32[]{:T(128)S(6)} %select_n.50, s32[]{:T(128)S(6)} %select_n.53), kind=kLoop, calls=%fused_computation.36 | loop fusion | bytes 2097160 | tf_op jit(solution)/shard_map/jit(dynamic_index_in_dim)/squeeze | solution.py:106
  81.4 0.7 fusion.51
  82.1 2.0 %copy.66 = bf16[8,1,256,64]{3,0,2,1:T(8,128)(2,1)} copy(bf16[8,1,256,64]{2,3,1,0:T(8,128)(2,1)} %get-tuple-element.13) | data formatting | bytes 524288
  84.9 0.6 copy-done.2
  85.6 1.4 %maximum_bitcast_fusion = (bf16[1,16,256,64]{3,1,0,2:T(8,128)(2,1)S(1)}, bf16[1,16,256,64]{3,1,0,2:T(8,128)(2,1)}) fusion(bf16[8,256,64]{2,0,1:T(8,128)(2,1)S(1)} %bitcast.88, bf16[8,256,64]{2,0,1:T(8,128)(2,1)S(1)} %bitcast.86, bf16[8,256,64]{2,0,1:T(8,128)(2,1)S(1)} %bitcast_negate_fusion.1), kind=kLoop, calls=%fused_computation.23 | loop fusion | flops 2097152 | bytes 1835008 | tf_op jit(solution)/shard_map/stack | solution.py:55
  86.9 2.6 %convolution_convert_fusion = bf16[256,2,64,128]{3,2,1,0:T(8,128)(2,1)S(1)} fusion(bf16[1,16,256,64]{3,1,0,2:T(8,128)(2,1)S(1)} %get-tuple-element.16, bf16[1,16,256,64]{3,1,0,2:T(8,128)(2,1)S(1)} %get-tuple-element.15, bf16[8,256,128]{2,0,1:T(8,128)(2,1)S(1)} %bitcast.81, bf16[8,256,128]{2,0,1:T(8,128)(2,1)S(1)} %bitcast.83), kind=kOutput, calls=%fused_computation.4 | convolution fusion | flops 141033472 | bytes 10485760 | tf_op jit(solution)/shard_map/ctfs,tfn->fcsn/dot_general | solution.py:59
  89.6 2.8 %convolution_convert_fusion.1 = bf16[256,2,64,128]{3,2,1,0:T(8,128)(2,1)S(1)} fusion(bf16[1,16,256,64]{3,1,0,2:T(8,128)(2,1)S(1)} %copy-done.1, bf16[1,16,256,64]{3,1,0,2:T(8,128)(2,1)S(1)} %get-tuple-element.11, bf16[8,256,128]{2,0,1:T(8,128)(2,1)S(1)} %bitcast.82, bf16[8,256,128]{2,0,1:T(8,128)(2,1)S(1)} %bitcast.84), kind=kOutput, calls=%fused_computation.5 | convolution fusion | flops 141033472 | bytes 10485760 | tf_op jit(solution)/shard_map/ctfs,tfn->fcsn/dot_general | solution.py:59
  92.5 5.4 %fusion.19 = bf16[1,128,64,128]{3,1,2,0:T(8,128)(2,1)S(1)} fusion(f32[64,128]{1,0:T(8,128)S(1)} %copy-done.5, bf16[256,2,64,128]{3,2,1,0:T(8,128)(2,1)S(1)} %convolution_convert_fusion, f32[128,256,1]{1,0,2:T(8,128)S(1)} %copy-done.3, f32[128,256,1]{1,0,2:T(8,128)S(1)} %get-tuple-element.25), kind=kOutput, calls=%fused_computation.18 | convolution fusion | flops 1076035584 | bytes 10780672 | tf_op jit(solution)/shard_map/dot_general | solution.py:111
  97.9 5.4 %fusion.16 = bf16[1,128,64,128]{3,1,2,0:T(8,128)(2,1)S(1)} fusion(f32[64,128]{1,0:T(8,128)S(1)} %copy-done.4, bf16[256,2,64,128]{3,2,1,0:T(8,128)(2,1)S(1)} %convolution_convert_fusion.1, f32[128,256,1]{1,0,2:T(8,128)S(1)} %copy-done.3, f32[128,256,1]{1,0,2:T(8,128)S(1)} %get-tuple-element.25), kind=kOutput, calls=%fused_computation.17 | convolution fusion | flops 1076035584 | bytes 10780672 | tf_op jit(solution)/shard_map/dot_general | solution.py:111
  103.7 4.7 %copy.60 = bf16[2,128,64,128]{3,2,1,0:T(8,128)(2,1)} copy(bf16[2,128,64,128]{3,1,2,0:T(8,128)(2,1)S(1)} %pad_maximum_fusion) | data formatting | bytes 8388608 | tf_op jit(solution)/shard_map/stack | solution.py:128
  (42 shorter events, 3.7 us)
Async XLA Ops:
  6.5 29.4 %all-gather.5.cloned.1.call-start = ((), (), s32[]{:S(2)}) async-start(), calls=%async_computation.2 | async-start | bytes 1572864 | tf_op jit(solution)/shard_map/all_gather | solution.py:94
  7.9 7.6 %collective-permute-start = (f32[4,64,128]{2,1,0:T(8,128)S(1)}, f32[4,64,128]{2,1,0:T(8,128)S(1)}, u32[]{:S(2)}, u32[]{:S(2)}) collective-permute-start(f32[4,64,128]{2,1,0:T(8,128)S(1)} %get-tuple-element.21), channel_id=1, source_target_pairs={{0,2},{1,3},{4,6},{5,7},{8,10},{9,11},{12,14},{13,15},{16,18},{17,... | collective-permute-start | bytes 393224 | tf_op jit(solution)/shard_map/ppermute | solution.py:28
  12.8 6.9 %collective-permute-start.1 = (f32[4,64,128]{2,1,0:T(8,128)S(1)}, f32[4,64,128]{2,1,0:T(8,128)S(1)}, u32[]{:S(2)}, u32[]{:S(2)}) collective-permute-start(f32[4,64,128]{2,1,0:T(8,128)S(1)} %get-tuple-element.22), channel_id=1, source_target_pairs={{2,0},{3,1},{6,4},{7,5},{10,8},{11,9},{14,12},{15,13},{18,16},{19,... | collective-permute-start | bytes 393224 | tf_op jit(solution)/shard_map/ppermute | solution.py:30
  14.2 6.3 %copy-start = (f32[4,2,256,128]{3,2,1,0:T(8,128)S(1)}, f32[4,2,256,128]{3,2,1,0:T(8,128)}, u32[]{:S(2)}) copy-start(f32[4,2,256,128]{3,2,1,0:T(8,128)} %param.3) | copy-start | bytes 3145732
  21.4 57.9 %all-gather.3.cloned.1.call-start = ((), (), s32[]{:S(2)}) async-start(), calls=%async_computation.1 | async-start | bytes 2621440 | tf_op jit(solution)/shard_map/all_gather | solution.py:96
  22.8 5.1 %copy-start.6 = (s32[2]{0:T(128)S(1)}, s32[2]{0:T(128)}, u32[]{:S(2)}) copy-start(s32[2]{0:T(128)} %param.4) | copy-start | bytes 28
  22.8 11.0 %copy-start.7 = (s32[4,4]{1,0:T(4,128)S(1)}, s32[4,4]{1,0:T(4,128)}, u32[]{:S(2)}) copy-start(s32[4,4]{1,0:T(4,128)} %param.5) | copy-start | bytes 196
  84.5 1.0 copy-start.2
  86.9 2.6 %copy-start.1 = (bf16[1,16,256,64]{3,1,0,2:T(8,128)(2,1)S(1)}, bf16[1,16,256,64]{3,1,0,2:T(8,128)(2,1)}, u32[]{:S(2)}) copy-start(bf16[1,16,256,64]{3,1,0,2:T(8,128)(2,1)} %get-tuple-element.12) | copy-start | bytes 1572868
  89.6 2.9 %copy-start.3 = (f32[128,256,1]{1,0,2:T(8,128)S(1)}, f32[128,256,1]{1,0,2:T(8,128)}, u32[]{:S(2)}) copy-start(f32[128,256,1]{1,0,2:T(8,128)} %get-tuple-element.26) | copy-start | bytes 393220
  89.6 2.9 %copy-start.5 = (f32[64,128]{1,0:T(8,128)S(1)}, f32[64,128]{1,0:T(8,128)}, u32[]{:S(2)}) copy-start(f32[64,128]{1,0:T(8,128)} %get-tuple-element.28) | copy-start | bytes 98308
  92.5 5.4 %copy-start.4 = (f32[64,128]{1,0:T(8,128)S(1)}, f32[64,128]{1,0:T(8,128)}, u32[]{:S(2)}) copy-start(f32[64,128]{1,0:T(8,128)} %get-tuple-element.27) | copy-start | bytes 98308
Sparse Core Ops, SparseCore 0:
  21.5 9.3 all-gather.4
  32.5 46.8 all-gather.2
where the time goes:
time: 116 us; the launch traced here: 115 us
  waiting for transfers between devices  46.9 us (40%)
  between operations  18.9 us (16%)
  matrix products  16.8 us (14%)
  local copies, waits for them, and re-layouts  15.4 us (13%)
  other arithmetic  6.87 us (6%)
  starting transfers between devices  6.21 us (5%)
  blocking collectives  4.15 us (4%)
    all_gather x1, waiting for transfers between devices, local(): candidates = lax.all_gather(own_half, 'sta', axis=0, tiled=False)  41.4 us
    dot_general x2, matrix products, local(): lax.dot_general(lag_weights, cross_spectra, (((1, 2), (0, 1)), ((), ())),...  10.8 us
    dot_general x2, matrix products, cross_terms(): jnp.einsum('ctfs,tfn->fcsn', left_stack, right_stack, preferred_element_t...  5.46 us
    ppermute x1, starting transfers between devices, padded(): lax.ppermute(tail, axis, [(i, (i + 1) % count) for i in range(ends)])  4.88 us
    another operation x1, local copies, waits for them, and re-layouts, local(): return jnp.stack(results, 0)  4.71 us
    unnamed x22, local copies, waits for them, and re-layouts  4.32 us
    all_to_all x1, blocking collectives, local(): lax.all_to_all(white, 'seg', split_axis=3, concat_axis=0, tiled=True)  4.15 us
    ppermute x1, waiting for transfers between devices, padded(): lax.ppermute(head, axis, [((i + 1) % count, i) for i in range(ends)])  4.13 us
  transfers between devices with their start and end apart: 4, of which 3 were waited for; matrix products, arithmetic and copies ran while one was open for 6% of the time, Pallas kernels for 0%

commit v1 on v0

--- a/solution.py
+++ b/solution.py
@@ -91,9 +91,23 @@
     ).astype(jnp.float32)
     smooth = window_sums / in_range[None, :, None]
     white = (spectra / (smooth[:, None] + EPSILON)).astype(jnp.bfloat16)
-    receivers = lax.all_gather(white, "seg", axis=0, tiled=True)
-    own_half = lax.all_to_all(white, "seg", split_axis=3, concat_axis=0, tiled=True)
-    candidates = lax.all_gather(own_half, "sta", axis=0, tiled=False)
+    seg_count = lax.axis_size("seg")
+    sta_count = lax.axis_size("sta")
+    receivers = lax.all_gather(white, "seg", axis=0, tiled=True) if seg_count > 2 else None
+    if receivers is None:
+        partner = lax.ppermute(white, "seg", [(0, 1), (1, 0)])
+        receivers = jnp.where(
+            seg_position == 0,
+            jnp.concatenate([white, partner], 0),
+            jnp.concatenate([partner, white], 0),
+        )
+    own_half = lax.dynamic_slice_in_dim(receivers, seg_position * half_sources, half_sources, 3)
+    shifted = [own_half]
+    for shift in range(1, sta_count):
+        shifted.append(
+            lax.ppermute(own_half, "sta", [(i, (i + shift) % sta_count) for i in range(sta_count)])
+        )
+    candidates = jnp.stack(shifted, 0)
     blk_dev = sta_local // SRC
     lag_weights = lag_table(band_position * band_bins).reshape(LAGS, band_bins, 2)
     receiver_ids = sta_position * sta_local + jnp.arange(sta_local, dtype=jnp.int32)
@@ -103,7 +117,8 @@
     for step_number in range(STEPS):
         block_number = plan[step_number]
         owner_position = block_number // blk_dev
-        held = lax.dynamic_index_in_dim(candidates, owner_position, 0, keepdims=False)
+        distance = (sta_position - owner_position) % sta_count
+        held = lax.dynamic_index_in_dim(candidates, distance, 0, keepdims=False)
         sources = lax.dynamic_slice_in_dim(
             held, (block_number % blk_dev) * half_sources, half_sources, 3
         )

time: 116 us -> 97.1 us (0.84)
  between operations: 18.9 us -> 6.79 us
  starting transfers between devices: 6.21 us -> 10.9 us
  waiting for transfers between devices: 46.9 us -> 42.6 us
  blocking collectives: 4.15 us -> 0 us
  local copies, waits for them, and re-layouts: 15.4 us -> 11.5 us
  other arithmetic: 6.87 us -> 8.16 us
    ppermute x0 -> x4, waiting for transfers between devices: none -> 42.6 us  [the longest x3 41.5 us: local(): lax.ppermute(own_half, 'sta', [(i, (i + shift) % sta_count) for i in rang...]
    all_gather x2 -> x0, waiting for transfers between devices: 41.4 us -> none  [the longest x1 41.4 us: local(): candidates = lax.all_gather(own_half, 'sta', axis=0, tiled=False)]
    ppermute x0 -> x4, starting transfers between devices: none -> 4.74 us  [the longest x3 4.67 us: local(): lax.ppermute(own_half, 'sta', [(i, (i + shift) % sta_count) for i in rang...]
    all_to_all x1 -> x0, blocking collectives: 4.15 us -> none  [local(): lax.all_to_all(white, 'seg', split_axis=3, concat_axis=0, tiled=True)]
    ppermute x1, waiting for transfers between devices: 4.13 us -> 0.01 us  [padded(): lax.ppermute(head, axis, [((i + 1) % count, i) for i in range(ends)])]
    another operation x0 -> x1, other arithmetic: none -> 1.46 us  [local(): candidates = jnp.stack(shifted, 0)]
    convert_element_type x1 -> x0, local copies, waits for them, and re-layouts: 1.4 us -> none  [local(): white = (spectra / (smooth[:, None] + EPSILON)).astype(jnp.bfloat16)]
    ppermute x1, waiting for transfers between devices: 1.39 us -> 0.01 us  [padded(): lax.ppermute(tail, axis, [(i, (i + 1) % count) for i in range(ends)])]
  transfers between devices with their start and end apart: 4 -> 6, of which waited for: 3 -> 3; matrix products, arithmetic and copies ran while one was open for 6% -> 3% of each run, Pallas kernels for 0% -> 0%
where the time goes in v1:
time: 97.1 us; the launch traced here: 96.8 us
  waiting for transfers between devices  42.6 us (44%)
  matrix products  16.8 us (17%)
  local copies, waits for them, and re-layouts  11.5 us (12%)
  starting transfers between devices  10.9 us (11%)
  other arithmetic  8.16 us (8%)
  between operations  6.79 us (7%)
    ppermute x3, waiting for transfers between devices, local(): lax.ppermute(own_half, 'sta', [(i, (i + shift) % sta_count) for i in rang...  41.5 us
    dot_general x2, matrix products, local(): lax.dot_general(lag_weights, cross_spectra, (((1, 2), (0, 1)), ((), ())),...  10.8 us
    dot_general x2, matrix products, cross_terms(): jnp.einsum('ctfs,tfn->fcsn', left_stack, right_stack, preferred_element_t...  5.48 us
    ppermute x1, starting transfers between devices, padded(): lax.ppermute(tail, axis, [(i, (i + 1) % count) for i in range(ends)])  4.88 us
    another operation x1, local copies, waits for them, and re-layouts, local(): return jnp.stack(results, 0)  4.71 us
    ppermute x3, starting transfers between devices, local(): lax.ppermute(own_half, 'sta', [(i, (i + shift) % sta_count) for i in rang...  4.67 us
    unnamed x18, local copies, waits for them, and re-layouts  3.82 us
  transfers between devices with their start and end apart: 6, of which 3 were waited for; matrix products, arithmetic and copies ran while one was open for 3% of the time, Pallas kernels for 0%

profile of v1, /device:TPU:0, one launch (start us, length us, event | category | flops | bytes accessed | tf_op | source)
XLA Modules:
  0.0 96.8 jit_solution(11337849166178350457)
XLA Ops:
  0.0 1.4 %sqrt_bitcast_fusion = f32[4,256,128]{2,1,0:T(8,128)S(1)} fusion(f32[4,2,256,128]{3,2,1,0:T(8,128)} %param.3), kind=kLoop, calls=%fused_computation.40 | loop fusion | flops 393216 | bytes 1572864 | tf_op jit(solution)/shard_map/sqrt | solution.py:74
  1.4 4.9 %collective-permute-start = (f32[4,64,128]{2,1,0:T(8,128)S(1)}, f32[4,64,128]{2,1,0:T(8,128)S(1)}, u32[]{:S(2)}, u32[]{:S(2)}) collective-permute-start(f32[4,64,128]{2,1,0:T(8,128)S(1)} %get-tuple-element.21), channel_id=1, source_target_pairs={{0,2},{1,3},{4,6},{5,7},{8,10},{9,11},{12,14},{13,15},{16,18},{17,... | collective-permute-start | bytes 393224 | tf_op jit(solution)/shard_map/ppermute | solution.py:28
  6.3 1.3 %collective-permute-start.1 = (f32[4,64,128]{2,1,0:T(8,128)S(1)}, f32[4,64,128]{2,1,0:T(8,128)S(1)}, u32[]{:S(2)}, u32[]{:S(2)}) collective-permute-start(f32[4,64,128]{2,1,0:T(8,128)S(1)} %get-tuple-element.22), channel_id=1, source_target_pairs={{2,0},{3,1},{6,4},{7,5},{10,8},{11,9},{14,12},{15,13},{18,16},{19,... | collective-permute-start | bytes 393224 | tf_op jit(solution)/shard_map/ppermute | solution.py:30
  7.6 0.6 fusion.54
  13.5 0.5 fusion.22
  14.7 0.7 fusion.26
  15.7 0.7 compare_select_fusion.1
  16.4 1.1 %collective-permute-done.2 = bf16[4,2,256,128]{3,0,2,1:T(4,128)(2,1)S(1)} collective-permute-done((bf16[4,2,256,128]{3,0,2,1:T(4,128)(2,1)S(1)}, bf16[4,2,256,128]{3,0,2,1:T(4,128)(2,1)S(1)}, u32[]{:S(2)}, u32[]{:S(2)}) %collective-permute-start.2) | collective-permute-done | bytes 524320 | tf_op jit(solution)/shard_map/ppermute | solution.py:98
  17.4 0.9 maximum_select_fusion
  18.7 0.7 copy.43
  19.5 3.7 %collective-permute-start.5 = (bf16[8,2,256,64]{2,3,1,0:T(8,128)(2,1)S(1)}, bf16[8,2,256,64]{2,3,1,0:T(8,128)(2,1)S(1)}, u32[]{:S(2)}, u32[]{:S(2)}) collective-permute-start(bf16[8,2,256,64]{2,3,1,0:T(8,128)(2,1)S(1)} %copy.43), channel_id=1, source_target_pairs={{0,12},{4,0},{8,4},{12,8},{1,13},{5,1},{9,5},{13,9},{2,14},{6,2},{... | collective-permute-start | bytes 1572872 | tf_op jit(solution)/shard_map/ppermute | solution.py:108
  23.1 1.0 %collective-permute-start.3 = (bf16[8,2,256,64]{2,3,1,0:T(8,128)(2,1)S(1)}, bf16[8,2,256,64]{2,3,1,0:T(8,128)(2,1)}, u32[]{:S(2)}, u32[]{:S(2)}) collective-permute-start(bf16[8,2,256,64]{2,3,1,0:T(8,128)(2,1)S(1)} %copy.43), channel_id=1, source_target_pairs={{0,4},{4,8},{8,12},{12,0},{1,5},{5,9},{9,13},{13,1},{2,6},{6,10},{... | collective-permute-start | bytes 1572872 | tf_op jit(solution)/shard_map/ppermute | solution.py:108
  25.5 1.3 %fusion.37 = (f32[128,256,1]{1,0,2:T(8,128)S(1)}, f32[128,256,1]{1,0,2:T(8,128)}) fusion(s32[256]{0:T(256)S(1)} %get-tuple-element.36, s32[128]{0:T(128)S(1)} %iota_add_fusion.5), kind=kLoop, calls=%fused_computation.58 | loop fusion | flops 491520 | bytes 263680 | tf_op jit(solution)/shard_map/cos | solution.py:48
  26.8 8.7 %collective-permute-done.5 = bf16[8,2,256,64]{2,3,1,0:T(8,128)(2,1)S(1)} collective-permute-done((bf16[8,2,256,64]{2,3,1,0:T(8,128)(2,1)S(1)}, bf16[8,2,256,64]{2,3,1,0:T(8,128)(2,1)S(1)}, u32[]{:S(2)}, u32[]{:S(2)}) %collective-permute-start.5) | collective-permute-done | bytes 524320 | tf_op jit(solution)/shard_map/ppermute | solution.py:108
  35.5 32.8 %collective-permute-done.4 = bf16[8,2,256,64]{2,3,1,0:T(8,128)(2,1)} collective-permute-done((bf16[8,2,256,64]{2,3,1,0:T(8,128)(2,1)S(1)}, bf16[8,2,256,64]{2,3,1,0:T(8,128)(2,1)}, u32[]{:S(2)}, u32[]{:S(2)}) %collective-permute-start.4) | collective-permute-done | bytes 524320 | tf_op jit(solution)/shard_map/ppermute | solution.py:108
  68.3 1.5 %pad_maximum_fusion.1 = bf16[4,8,2,256,64]{3,4,2,1,0:T(8,128)(2,1)S(1)} fusion(bf16[1,8,2,256,64]{3,4,2,1,0:T(8,128)(2,1)S(1)} %bitcast.86, bf16[1,8,2,256,64]{3,4,2,1,0:T(8,128)(2,1)} %bitcast.10, bf16[1,8,2,256,64]{3,4,2,1,0:T(8,128)(2,1)} %bitcast.9, bf16[1,8,2,256,64]{3,4,2,1,0:T(8,128)(2,1)S(1)} %bitcast.85), kind=kLoop, calls=%fused_computation.11 | loop fusion | flops 3145728 | bytes 4194304 | tf_op jit(solution)/shard_map/stack | solution.py:110
  70.6 0.7 fusion.51
  71.4 2.0 %copy.61 = bf16[8,1,256,64]{3,0,2,1:T(8,128)(2,1)} copy(bf16[8,1,256,64]{2,3,1,0:T(8,128)(2,1)} %get-tuple-element.13) | data formatting | bytes 524288
  74.2 0.6 copy-done.1
  75.3 2.6 %convolution_convert_fusion = bf16[256,2,64,128]{3,2,1,0:T(8,128)(2,1)S(1)} fusion(bf16[1,16,256,64]{3,1,0,2:T(8,128)(2,1)S(1)} %get-tuple-element.16, bf16[1,16,256,64]{3,1,0,2:T(8,128)(2,1)S(1)} %get-tuple-element.15, bf16[8,256,128]{2,0,1:T(8,128)(2,1)S(1)} %get-tuple-element.10, bf16[8,256,128]{2,0,1:T(8,128)(2,1)S(1)} %get-tuple-element.9), kind=kOutput, calls=%fused_computation.4 | convolution fusion | flops 141033472 | bytes 10485760 | tf_op jit(solution)/shard_map/ctfs,tfn->fcsn/dot_general | solution.py:59
  77.9 2.8 %convolution_convert_fusion.1 = bf16[256,2,64,128]{3,2,1,0:T(8,128)(2,1)S(1)} fusion(bf16[1,16,256,64]{3,1,0,2:T(8,128)(2,1)S(1)} %get-tuple-element.12, bf16[1,16,256,64]{3,1,0,2:T(8,128)(2,1)S(1)} %get-tuple-element.11, bf16[8,256,128]{2,0,1:T(8,128)(2,1)S(1)} %get-tuple-element.10, bf16[8,256,128]{2,0,1:T(8,128)(2,1)S(1)} %get-tuple-element.9), kind=kOutput, calls=%fused_computation.5 | convolution fusion | flops 141033472 | bytes 10485760 | tf_op jit(solution)/shard_map/ctfs,tfn->fcsn/dot_general | solution.py:59
  80.8 5.4 %fusion.19 = bf16[1,128,64,128]{3,1,2,0:T(8,128)(2,1)S(1)} fusion(f32[64,128]{1,0:T(8,128)S(1)} %copy-done.4, bf16[256,2,64,128]{3,2,1,0:T(8,128)(2,1)S(1)} %convolution_convert_fusion, f32[128,256,1]{1,0,2:T(8,128)S(1)} %copy-done.2, f32[128,256,1]{1,0,2:T(8,128)S(1)} %get-tuple-element.25), kind=kOutput, calls=%fused_computation.19 | convolution fusion | flops 1076035584 | bytes 10780672 | tf_op jit(solution)/shard_map/dot_general | solution.py:126
  86.2 5.4 %fusion.16 = bf16[1,128,64,128]{3,1,2,0:T(8,128)(2,1)S(1)} fusion(f32[64,128]{1,0:T(8,128)S(1)} %copy-done.3, bf16[256,2,64,128]{3,2,1,0:T(8,128)(2,1)S(1)} %convolution_convert_fusion.1, f32[128,256,1]{1,0,2:T(8,128)S(1)} %copy-done.2, f32[128,256,1]{1,0,2:T(8,128)S(1)} %get-tuple-element.25), kind=kOutput, calls=%fused_computation.18 | convolution fusion | flops 1076035584 | bytes 10780672 | tf_op jit(solution)/shard_map/dot_general | solution.py:126
  92.0 4.7 %copy.55 = bf16[2,128,64,128]{3,2,1,0:T(8,128)(2,1)} copy(bf16[2,128,64,128]{3,1,2,0:T(8,128)(2,1)S(1)} %pad_maximum_fusion) | data formatting | bytes 8388608 | tf_op jit(solution)/shard_map/stack | solution.py:143
  (41 shorter events, 3.8 us)
Async XLA Ops:
  0.0 7.6 %copy-start.5 = (s32[2]{0:T(128)S(1)}, s32[2]{0:T(128)}, u32[]{:S(2)}) copy-start(s32[2]{0:T(128)} %param.4) | copy-start | bytes 28
  1.4 12.0 %collective-permute-start = (f32[4,64,128]{2,1,0:T(8,128)S(1)}, f32[4,64,128]{2,1,0:T(8,128)S(1)}, u32[]{:S(2)}, u32[]{:S(2)}) collective-permute-start(f32[4,64,128]{2,1,0:T(8,128)S(1)} %get-tuple-element.21), channel_id=1, source_target_pairs={{0,2},{1,3},{4,6},{5,7},{8,10},{9,11},{12,14},{13,15},{16,18},{17,... | collective-permute-start | bytes 393224 | tf_op jit(solution)/shard_map/ppermute | solution.py:28
  6.3 7.1 %collective-permute-start.1 = (f32[4,64,128]{2,1,0:T(8,128)S(1)}, f32[4,64,128]{2,1,0:T(8,128)S(1)}, u32[]{:S(2)}, u32[]{:S(2)}) collective-permute-start(f32[4,64,128]{2,1,0:T(8,128)S(1)} %get-tuple-element.22), channel_id=1, source_target_pairs={{2,0},{3,1},{6,4},{7,5},{10,8},{11,9},{14,12},{15,13},{18,16},{19,... | collective-permute-start | bytes 393224 | tf_op jit(solution)/shard_map/ppermute | solution.py:30
  13.5 1.2 %copy-start = (f32[4,2,256,128]{3,2,1,0:T(8,128)S(1)}, f32[4,2,256,128]{3,2,1,0:T(8,128)}, u32[]{:S(2)}) copy-start(f32[4,2,256,128]{3,2,1,0:T(8,128)} %param.3) | copy-start | bytes 3145732
  14.0 1.5 %copy-start.6 = (s32[4,4]{1,0:T(4,128)S(1)}, s32[4,4]{1,0:T(4,128)}, u32[]{:S(2)}) copy-start(s32[4,4]{1,0:T(4,128)} %param.5) | copy-start | bytes 196
  15.5 2.0 %collective-permute-start.2 = (bf16[4,2,256,128]{3,0,2,1:T(4,128)(2,1)S(1)}, bf16[4,2,256,128]{3,0,2,1:T(4,128)(2,1)S(1)}, u32[]{:S(2)}, u32[]{:S(2)}) collective-permute-start(bf16[4,2,256,128]{3,0,2,1:T(4,128)(2,1)S(1)} %fusion.26), channel_id=1, source_target_pairs={{0,1},{1,0},{2,3},{3,2},{4,5},{5,4},{6,7},{7,6},{8,9},{9,8},{10,11... | collective-permute-start | bytes 1572872 | tf_op jit(solution)/shard_map/ppermute | solution.py:98
  19.5 16.1 %collective-permute-start.5 = (bf16[8,2,256,64]{2,3,1,0:T(8,128)(2,1)S(1)}, bf16[8,2,256,64]{2,3,1,0:T(8,128)(2,1)S(1)}, u32[]{:S(2)}, u32[]{:S(2)}) collective-permute-start(bf16[8,2,256,64]{2,3,1,0:T(8,128)(2,1)S(1)} %copy.43), channel_id=1, source_target_pairs={{0,12},{4,0},{8,4},{12,8},{1,13},{5,1},{9,5},{13,9},{2,14},{6,2},{... | collective-permute-start | bytes 1572872 | tf_op jit(solution)/shard_map/ppermute | solution.py:108
  23.1 45.2 %collective-permute-start.4 = (bf16[8,2,256,64]{2,3,1,0:T(8,128)(2,1)S(1)}, bf16[8,2,256,64]{2,3,1,0:T(8,128)(2,1)}, u32[]{:S(2)}, u32[]{:S(2)}) collective-permute-start(bf16[8,2,256,64]{2,3,1,0:T(8,128)(2,1)S(1)} %copy.43), channel_id=1, source_target_pairs={{0,8},{4,12},{8,0},{12,4},{1,9},{5,13},{9,1},{13,5},{2,10},{6,14},... | collective-permute-start | bytes 1572872 | tf_op jit(solution)/shard_map/ppermute | solution.py:108
  23.1 45.2 %collective-permute-start.3 = (bf16[8,2,256,64]{2,3,1,0:T(8,128)(2,1)S(1)}, bf16[8,2,256,64]{2,3,1,0:T(8,128)(2,1)}, u32[]{:S(2)}, u32[]{:S(2)}) collective-permute-start(bf16[8,2,256,64]{2,3,1,0:T(8,128)(2,1)S(1)} %copy.43), channel_id=1, source_target_pairs={{0,4},{4,8},{8,12},{12,0},{1,5},{5,9},{9,13},{13,1},{2,6},{6,10},{... | collective-permute-start | bytes 1572872 | tf_op jit(solution)/shard_map/ppermute | solution.py:108
  73.8 1.0 %copy-start.1 = (bf16[8,1,256,64]{3,0,2,1:T(8,128)(2,1)S(1)}, bf16[8,1,256,64]{3,0,2,1:T(8,128)(2,1)}, u32[]{:S(2)}) copy-start(bf16[8,1,256,64]{3,0,2,1:T(8,128)(2,1)} %copy.61) | copy-start | bytes 786436
  77.9 2.9 %copy-start.2 = (f32[128,256,1]{1,0,2:T(8,128)S(1)}, f32[128,256,1]{1,0,2:T(8,128)}, u32[]{:S(2)}) copy-start(f32[128,256,1]{1,0,2:T(8,128)} %get-tuple-element.26) | copy-start | bytes 393220
  77.9 2.9 %copy-start.4 = (f32[64,128]{1,0:T(8,128)S(1)}, f32[64,128]{1,0:T(8,128)}, u32[]{:S(2)}) copy-start(f32[64,128]{1,0:T(8,128)} %get-tuple-element.28) | copy-start | bytes 98308
  80.8 5.4 %copy-start.3 = (f32[64,128]{1,0:T(8,128)S(1)}, f32[64,128]{1,0:T(8,128)}, u32[]{:S(2)}) copy-start(f32[64,128]{1,0:T(8,128)} %get-tuple-element.27) | copy-start | bytes 98308

commit v2 on v1

--- a/solution.py
+++ b/solution.py
@@ -12,6 +12,7 @@
 BAND_BINS = 256
 HALF = 64
 LAGS = 128
+CHUNKS = 2
 
 
 EPSILON = 1e-06
@@ -102,33 +103,47 @@
             jnp.concatenate([partner, white], 0),
         )
     own_half = lax.dynamic_slice_in_dim(receivers, seg_position * half_sources, half_sources, 3)
-    shifted = [own_half]
-    for shift in range(1, sta_count):
-        shifted.append(
-            lax.ppermute(own_half, "sta", [(i, (i + shift) % sta_count) for i in range(sta_count)])
-        )
-    candidates = jnp.stack(shifted, 0)
     blk_dev = sta_local // SRC
     lag_weights = lag_table(band_position * band_bins).reshape(LAGS, band_bins, 2)
     receiver_ids = sta_position * sta_local + jnp.arange(sta_local, dtype=jnp.int32)
     block_columns = jnp.arange(pair_mask.shape[1], dtype=jnp.int32)
     block_onehot = ((receiver_ids // SRC)[:, None] == block_columns[None, :]).astype(jnp.float32)
+    chunks = CHUNKS if half_sources % CHUNKS == 0 else 1
+    width = half_sources // chunks
+    pieces = [[] for _ in range(STEPS)]
+    arrived = None
+    for chunk in range(chunks):
+        piece = lax.slice_in_dim(own_half, chunk * width, (chunk + 1) * width, axis=3)
+        if arrived is not None:
+            piece, _ = lax.optimization_barrier((piece, arrived))
+        shifted = [piece]
+        for shift in range(1, sta_count):
+            shifted.append(
+                lax.ppermute(piece, "sta", [(i, (i + shift) % sta_count) for i in range(sta_count)])
+            )
+        arrived = shifted[1:]
+        candidates = jnp.stack(shifted, 0)
+        for step_number in range(STEPS):
+            block_number = plan[step_number]
+            owner_position = block_number // blk_dev
+            distance = (sta_position - owner_position) % sta_count
+            held = lax.dynamic_index_in_dim(candidates, distance, 0, keepdims=False)
+            sources = lax.dynamic_slice_in_dim(
+                held, (block_number % blk_dev) * width, width, 3
+            )
+            cross_spectra = cross_terms(sources, receivers)
+            pieces[step_number].append(
+                lax.dot_general(
+                    lag_weights,
+                    cross_spectra,
+                    (((1, 2), (0, 1)), ((), ())),
+                    preferred_element_type=jnp.float32,
+                )
+            )
     results = []
     for step_number in range(STEPS):
         block_number = plan[step_number]
-        owner_position = block_number // blk_dev
-        distance = (sta_position - owner_position) % sta_count
-        held = lax.dynamic_index_in_dim(candidates, distance, 0, keepdims=False)
-        sources = lax.dynamic_slice_in_dim(
-            held, (block_number % blk_dev) * half_sources, half_sources, 3
-        )
-        cross_spectra = cross_terms(sources, receivers)
-        correlated = lax.dot_general(
-            lag_weights,
-            cross_spectra,
-            (((1, 2), (0, 1)), ((), ())),
-            preferred_element_type=jnp.float32,
-        )
+        correlated = jnp.concatenate(pieces[step_number], 1)
         mask_row = pair_mask[block_number].astype(jnp.float32)
         allowed = jnp.sum(block_onehot * mask_row[None, :], axis=1)
         source_ids = (

time: 97.1 us -> 111 us (1.14)
  waiting for transfers between devices: 42.6 us -> 17.1 us
  local copies, waits for them, and re-layouts: 11.5 us -> 29.3 us
  starting transfers between devices: 10.9 us -> 20.9 us
  other arithmetic: 8.16 us -> 13.7 us
  matrix products: 16.8 us -> 22.2 us
    ppermute x3 -> x6, waiting for transfers between devices: 41.5 us -> 16.6 us  [local(): lax.ppermute(piece, 'sta', [(i, (i + shift) % sta_count) for i in range(s...]
    another operation x0 -> x6, local copies, waits for them, and re-layouts: none -> 17.4 us  [the longest x4 15.9 us: cross_terms(): jnp.stack([jnp.concatenate([src_real, src_imag], 0), jnp.concatenate([src...]
    ppermute x3 -> x6, starting transfers between devices: 4.67 us -> 14.6 us  [local(): lax.ppermute(piece, 'sta', [(i, (i + shift) % sta_count) for i in range(s...]
    dot_general x2 -> x4, matrix products: 10.8 us -> 14.8 us  [local(): lax.dot_general(lag_weights, cross_spectra, (((1, 2), (0, 1)), ((), ())),...]
    another operation x2 -> x8, other arithmetic: 0.8 us -> 4.03 us  [cross_terms(): jnp.stack([jnp.concatenate([src_real, src_imag], 0), jnp.concatenate([src...]
    unnamed x18 -> x22, local copies, waits for them, and re-layouts: 3.82 us -> 1.18 us
    optimization_barrier x0 -> x1, local copies, waits for them, and re-layouts: none -> 1.42 us  [local(): piece, _ = lax.optimization_barrier((piece, arrived))]
    squeeze x0 -> x4, local copies, waits for them, and re-layouts: none -> 1.41 us  [cross_terms(): src_real = sources[:, 0]]
  transfers between devices with their start and end apart: 6 -> 9, of which waited for: 3 -> 3; matrix products, arithmetic and copies ran while one was open for 3% -> 24% of each run, Pallas kernels for 0% -> 0%
where the time goes in v2:
time: 111 us; the launch traced here: 110 us
  local copies, waits for them, and re-layouts  29.3 us (26%)
  matrix products  22.2 us (20%)
  starting transfers between devices  20.9 us (19%)
  waiting for transfers between devices  17.1 us (15%)
  other arithmetic  13.7 us (12%)
  between operations  7.11 us (6%)
    ppermute x6, waiting for transfers between devices, local(): lax.ppermute(piece, 'sta', [(i, (i + shift) % sta_count) for i in range(s...  16.6 us
    another operation x4, local copies, waits for them, and re-layouts, cross_terms(): jnp.stack([jnp.concatenate([src_real, src_imag], 0), jnp.concatenate([src...  15.9 us
    dot_general x4, matrix products, local(): lax.dot_general(lag_weights, cross_spectra, (((1, 2), (0, 1)), ((), ())),...  14.8 us
    ppermute x6, starting transfers between devices, local(): lax.ppermute(piece, 'sta', [(i, (i + shift) % sta_count) for i in range(s...  14.6 us
    dot_general x4, matrix products, cross_terms(): jnp.einsum('ctfs,tfn->fcsn', left_stack, right_stack, preferred_element_t...  6.84 us
    ppermute x1, starting transfers between devices, padded(): lax.ppermute(tail, axis, [(i, (i + 1) % count) for i in range(ends)])  4.88 us
    another operation x1, local copies, waits for them, and re-layouts, local(): return jnp.stack(results, 0)  4.71 us
    another operation x8, other arithmetic, cross_terms(): jnp.stack([jnp.concatenate([src_real, src_imag], 0), jnp.concatenate([src...  4.03 us
  transfers between devices with their start and end apart: 9, of which 3 were waited for; matrix products, arithmetic and copies ran while one was open for 24% of the time, Pallas kernels for 0%

profile of v2, /device:TPU:0, one launch (start us, length us, event | category | flops | bytes accessed | tf_op | source)
XLA Modules:
  0.0 110.3 jit_solution(1237627377075295672)
XLA Ops:
  0.0 1.4 %sqrt_bitcast_fusion = f32[4,256,128]{2,1,0:T(8,128)S(1)} fusion(f32[4,2,256,128]{3,2,1,0:T(8,128)} %param.3), kind=kLoop, calls=%fused_computation.41 | loop fusion | flops 393216 | bytes 1572864 | tf_op jit(solution)/shard_map/sqrt | solution.py:75
  1.4 4.9 %collective-permute-start = (f32[4,64,128]{2,1,0:T(8,128)S(1)}, f32[4,64,128]{2,1,0:T(8,128)S(1)}, u32[]{:S(2)}, u32[]{:S(2)}) collective-permute-start(f32[4,64,128]{2,1,0:T(8,128)S(1)} %get-tuple-element.19), channel_id=1, source_target_pairs={{0,2},{1,3},{4,6},{5,7},{8,10},{9,11},{12,14},{13,15},{16,18},{17,... | collective-permute-start | bytes 393224 | tf_op jit(solution)/shard_map/ppermute | solution.py:29
  20.8 1.4 %copy.43 = bf16[8,2,256,32]{2,3,1,0:T(8,128)(2,1)} copy(bf16[8,2,256,32]{3,0,2,1:T(8,128)(2,1)S(1)} %get-tuple-element.15) | data formatting | bytes 524288 | tf_op jit(solution)/shard_map/slice | solution.py:116
  22.2 2.6 %collective-permute-start.4 = (bf16[8,2,256,32]{2,3,1,0:T(8,128)(2,1)}, bf16[8,2,256,32]{2,3,1,0:T(8,128)(2,1)}, u32[]{:S(2)}, u32[]{:S(2)}) collective-permute-start(bf16[8,2,256,32]{2,3,1,0:T(8,128)(2,1)} %copy.43), channel_id=1, source_target_pairs={{0,8},{4,12},{8,0},{12,4},{1,9},{5,13},{9,1},{13,5},{2,10},{6,14},... | collective-permute-start | bytes 786440 | tf_op jit(solution)/shard_map/ppermute | solution.py:122
  24.8 1.3 %collective-permute-start.5 = (bf16[8,2,256,32]{2,3,1,0:T(8,128)(2,1)}, bf16[8,2,256,32]{2,3,1,0:T(8,128)(2,1)}, u32[]{:S(2)}, u32[]{:S(2)}) collective-permute-start(bf16[8,2,256,32]{2,3,1,0:T(8,128)(2,1)} %copy.43), channel_id=1, source_target_pairs={{0,12},{4,0},{8,4},{12,8},{1,13},{5,1},{9,5},{13,9},{2,14},{6,2},{... | collective-permute-start | bytes 786440 | tf_op jit(solution)/shard_map/ppermute | solution.py:122
  27.6 11.3 %collective-permute-done.4 = bf16[8,2,256,32]{2,3,1,0:T(8,128)(2,1)} collective-permute-done((bf16[8,2,256,32]{2,3,1,0:T(8,128)(2,1)}, bf16[8,2,256,32]{2,3,1,0:T(8,128)(2,1)}, u32[]{:S(2)}, u32[]{:S(2)}) %collective-permute-start.4) | collective-permute-done | bytes 262176 | tf_op jit(solution)/shard_map/ppermute | solution.py:122
  38.9 5.3 %collective-permute-done.3 = bf16[8,2,256,32]{2,3,1,0:T(8,128)(2,1)} collective-permute-done((bf16[8,2,256,32]{2,3,1,0:T(8,128)(2,1)}, bf16[8,2,256,32]{2,3,1,0:T(8,128)(2,1)}, u32[]{:S(2)}, u32[]{:S(2)}) %collective-permute-start.3) | collective-permute-done | bytes 262176 | tf_op jit(solution)/shard_map/ppermute | solution.py:122
  45.5 1.4 %copy.49 = bf16[8,2,256,32]{2,3,1,0:T(8,128)(2,1)} copy(bf16[8,2,256,32]{3,0,2,1:T(8,128)(2,1)S(1)} %get-tuple-element.6) | data formatting | bytes 524288 | tf_op jit(solution)/shard_map/optimization_barrier | solution.py:118
  46.9 5.2 %collective-permute-start.6 = (bf16[8,2,256,32]{2,3,1,0:T(8,128)(2,1)}, bf16[8,2,256,32]{2,3,1,0:T(8,128)(2,1)}, u32[]{:S(2)}, u32[]{:S(2)}) collective-permute-start(bf16[8,2,256,32]{2,3,1,0:T(8,128)(2,1)} %copy.49), channel_id=1, source_target_pairs={{0,4},{4,8},{8,12},{12,0},{1,5},{5,9},{9,13},{13,1},{2,6},{6,10},{... | collective-permute-start | bytes 786440 | tf_op jit(solution)/shard_map/ppermute | solution.py:122
  52.1 1.9 %collective-permute-start.7 = (bf16[8,2,256,32]{2,3,1,0:T(8,128)(2,1)}, bf16[8,2,256,32]{2,3,1,0:T(8,128)(2,1)}, u32[]{:S(2)}, u32[]{:S(2)}) collective-permute-start(bf16[8,2,256,32]{2,3,1,0:T(8,128)(2,1)} %copy.49), channel_id=1, source_target_pairs={{0,8},{4,12},{8,0},{12,4},{1,9},{5,13},{9,1},{13,5},{2,10},{6,14},... | collective-permute-start | bytes 786440 | tf_op jit(solution)/shard_map/ppermute | solution.py:122
  54.0 2.9 %collective-permute-start.8 = (bf16[8,2,256,32]{2,3,1,0:T(8,128)(2,1)}, bf16[8,2,256,32]{2,3,1,0:T(8,128)(2,1)}, u32[]{:S(2)}, u32[]{:S(2)}) collective-permute-start(bf16[8,2,256,32]{2,3,1,0:T(8,128)(2,1)} %copy.49), channel_id=1, source_target_pairs={{0,12},{4,0},{8,4},{12,8},{1,13},{5,1},{9,5},{13,9},{2,14},{6,2},{... | collective-permute-start | bytes 786440 | tf_op jit(solution)/shard_map/ppermute | solution.py:122
  58.4 3.7 %copy.47 = bf16[2,16,256,32]{3,1,0,2:T(8,128)(2,1)} copy(bf16[2,16,256,32]{2,3,1,0:T(8,128)(2,1)S(1)} %pad_maximum_fusion.5) | data formatting | bytes 1048576 | tf_op jit(solution)/shard_map/stack | solution.py:56
  65.0 4.5 %copy.55 = bf16[2,16,256,32]{3,1,0,2:T(8,128)(2,1)} copy(bf16[2,16,256,32]{2,3,1,0:T(8,128)(2,1)} %pad_maximum_fusion.7) | data formatting | bytes 1048576 | tf_op jit(solution)/shard_map/stack | solution.py:56
  69.6 1.6 %convolution_convert_fusion.3 = bf16[256,2,32,128]{3,2,1,0:T(8,128)(2,1)S(1)} fusion(bf16[2,16,256,32]{3,1,0,2:T(8,128)(2,1)S(1)} %copy-done.3, bf16[8,256,128]{2,0,1:T(8,128)(2,1)S(1)} %get-tuple-element.14, bf16[8,256,128]{2,0,1:T(8,128)(2,1)S(1)} %get-tuple-element.13), kind=kOutput, calls=%fused_computation.16 | convolution fusion | flops 71303168 | bytes 5767168 | tf_op jit(solution)/shard_map/ctfs,tfn->fcsn/dot_general | solution.py:60
  71.2 1.7 %convolution_convert_fusion.1 = bf16[256,2,32,128]{3,2,1,0:T(8,128)(2,1)S(1)} fusion(bf16[2,16,256,32]{3,1,0,2:T(8,128)(2,1)S(1)} %copy-done.4, bf16[8,256,128]{2,0,1:T(8,128)(2,1)S(1)} %get-tuple-element.14, bf16[8,256,128]{2,0,1:T(8,128)(2,1)S(1)} %get-tuple-element.13), kind=kOutput, calls=%fused_computation.14 | convolution fusion | flops 71303168 | bytes 5767168 | tf_op jit(solution)/shard_map/ctfs,tfn->fcsn/dot_general | solution.py:60
  72.9 4.0 %fusion.10 = f32[1,128,32,128]{3,1,2,0:T(8,128)} fusion(bf16[128,256,2,1]{1,0,2,3:T(8,128)(2,1)S(1)} %fusion.32, bf16[256,2,32,128]{3,2,1,0:T(8,128)(2,1)S(1)} %convolution_convert_fusion.3), kind=kOutput, calls=%fused_computation.17 | convolution fusion | flops 536870912 | bytes 6422528 | tf_op jit(solution)/shard_map/dot_general | solution.py:136
  76.9 4.0 %fusion.16 = f32[1,128,32,128]{3,1,2,0:T(8,128)} fusion(bf16[128,256,2,1]{1,0,2,3:T(8,128)(2,1)S(1)} %fusion.32, bf16[256,2,32,128]{3,2,1,0:T(8,128)(2,1)S(1)} %convolution_convert_fusion.1), kind=kOutput, calls=%fused_computation.19 | convolution fusion | flops 536870912 | bytes 6422528 | tf_op jit(solution)/shard_map/dot_general | solution.py:136
  83.9 3.8 %copy.53 = bf16[2,16,256,32]{3,1,0,2:T(8,128)(2,1)S(1)} copy(bf16[2,16,256,32]{2,3,1,0:T(8,128)(2,1)} %pad_maximum_fusion.6) | data formatting | bytes 1048576 | tf_op jit(solution)/shard_map/stack | solution.py:56
  87.7 1.9 %convolution_convert_fusion.2 = bf16[256,2,32,128]{3,2,1,0:T(8,128)(2,1)S(1)} fusion(bf16[2,16,256,32]{3,1,0,2:T(8,128)(2,1)S(1)} %copy.53, bf16[8,256,128]{2,0,1:T(8,128)(2,1)S(1)} %get-tuple-element.14, bf16[8,256,128]{2,0,1:T(8,128)(2,1)S(1)} %get-tuple-element.13), kind=kOutput, calls=%fused_computation.15 | convolution fusion | flops 71303168 | bytes 5767168 | tf_op jit(solution)/shard_map/ctfs,tfn->fcsn/dot_general | solution.py:60
  89.6 4.0 %fusion.13 = f32[1,128,32,128]{3,1,2,0:T(8,128)} fusion(bf16[128,256,2,1]{1,0,2,3:T(8,128)(2,1)S(1)} %fusion.32, bf16[256,2,32,128]{3,2,1,0:T(8,128)(2,1)S(1)} %convolution_convert_fusion.2), kind=kOutput, calls=%fused_computation.18 | convolution fusion | flops 536870912 | bytes 6422528 | tf_op jit(solution)/shard_map/dot_general | solution.py:136
  94.6 3.8 %copy.57 = bf16[2,16,256,32]{3,1,0,2:T(8,128)(2,1)S(1)} copy(bf16[2,16,256,32]{2,3,1,0:T(8,128)(2,1)} %pad_maximum_fusion.8) | data formatting | bytes 1048576 | tf_op jit(solution)/shard_map/stack | solution.py:56
  98.4 1.7 %convolution_convert_fusion = bf16[256,2,32,128]{3,2,1,0:T(8,128)(2,1)S(1)} fusion(bf16[2,16,256,32]{3,1,0,2:T(8,128)(2,1)S(1)} %copy.57, bf16[8,256,128]{2,0,1:T(8,128)(2,1)S(1)} %get-tuple-element.14, bf16[8,256,128]{2,0,1:T(8,128)(2,1)S(1)} %get-tuple-element.13), kind=kOutput, calls=%fused_computation.13 | convolution fusion | flops 71303168 | bytes 5767168 | tf_op jit(solution)/shard_map/ctfs,tfn->fcsn/dot_general | solution.py:60
  100.1 2.7 %fusion.19 = f32[1,128,32,128]{3,1,2,0:T(8,128)S(1)} fusion(bf16[128,256,2,1]{1,0,2,3:T(8,128)(2,1)S(1)} %fusion.32, bf16[256,2,32,128]{3,2,1,0:T(8,128)(2,1)S(1)} %convolution_convert_fusion), kind=kOutput, calls=%fused_computation.20 | convolution fusion | flops 536870912 | bytes 6422528 | tf_op jit(solution)/shard_map/dot_general | solution.py:136
  105.6 4.7 %copy.59 = bf16[2,128,64,128]{3,2,1,0:T(8,128)(2,1)} copy(bf16[2,128,64,128]{3,1,2,0:T(8,128)(2,1)S(1)} %pad_maximum_fusion) | data formatting | bytes 8388608 | tf_op jit(solution)/shard_map/stack | solution.py:158
  (77 shorter events, 21.2 us)
Async XLA Ops:
  0.0 7.6 %copy-start.9 = (s32[2]{0:T(128)S(1)}, s32[2]{0:T(128)}, u32[]{:S(2)}) copy-start(s32[2]{0:T(128)} %param.4) | copy-start | bytes 28
  0.0 13.6 %copy-start.10 = (s32[4,4]{1,0:T(4,128)S(1)}, s32[4,4]{1,0:T(4,128)}, u32[]{:S(2)}) copy-start(s32[4,4]{1,0:T(4,128)} %param.5) | copy-start | bytes 196
  1.4 13.7 %collective-permute-start = (f32[4,64,128]{2,1,0:T(8,128)S(1)}, f32[4,64,128]{2,1,0:T(8,128)S(1)}, u32[]{:S(2)}, u32[]{:S(2)}) collective-permute-start(f32[4,64,128]{2,1,0:T(8,128)S(1)} %get-tuple-element.19), channel_id=1, source_target_pairs={{0,2},{1,3},{4,6},{5,7},{8,10},{9,11},{12,14},{13,15},{16,18},{17,... | collective-permute-start | bytes 393224 | tf_op jit(solution)/shard_map/ppermute | solution.py:29
  6.3 8.8 %collective-permute-start.1 = (f32[4,64,128]{2,1,0:T(8,128)S(1)}, f32[4,64,128]{2,1,0:T(8,128)S(1)}, u32[]{:S(2)}, u32[]{:S(2)}) collective-permute-start(f32[4,64,128]{2,1,0:T(8,128)S(1)} %get-tuple-element.20), channel_id=1, source_target_pairs={{2,0},{3,1},{6,4},{7,5},{10,8},{11,9},{14,12},{15,13},{18,16},{19,... | collective-permute-start | bytes 393224 | tf_op jit(solution)/shard_map/ppermute | solution.py:31
  15.2 1.2 %copy-start.5 = (f32[4,2,256,128]{3,2,1,0:T(8,128)S(1)}, f32[4,2,256,128]{3,2,1,0:T(8,128)}, u32[]{:S(2)}) copy-start(f32[4,2,256,128]{3,2,1,0:T(8,128)} %param.3) | copy-start | bytes 3145732
  17.2 2.0 %collective-permute-start.2 = (bf16[4,2,256,128]{3,0,2,1:T(4,128)(2,1)S(1)}, bf16[4,2,256,128]{3,0,2,1:T(4,128)(2,1)S(1)}, u32[]{:S(2)}, u32[]{:S(2)}) collective-permute-start(bf16[4,2,256,128]{3,0,2,1:T(4,128)(2,1)S(1)} %fusion.26), channel_id=1, source_target_pairs={{0,1},{1,0},{2,3},{3,2},{4,5},{5,4},{6,7},{7,6},{8,9},{9,8},{10,11... | collective-permute-start | bytes 1572872 | tf_op jit(solution)/shard_map/ppermute | solution.py:99
  22.2 16.7 %collective-permute-start.4 = (bf16[8,2,256,32]{2,3,1,0:T(8,128)(2,1)}, bf16[8,2,256,32]{2,3,1,0:T(8,128)(2,1)}, u32[]{:S(2)}, u32[]{:S(2)}) collective-permute-start(bf16[8,2,256,32]{2,3,1,0:T(8,128)(2,1)} %copy.43), channel_id=1, source_target_pairs={{0,8},{4,12},{8,0},{12,4},{1,9},{5,13},{9,1},{13,5},{2,10},{6,14},... | collective-permute-start | bytes 786440 | tf_op jit(solution)/shard_map/ppermute | solution.py:122
  24.8 14.1 %collective-permute-start.5 = (bf16[8,2,256,32]{2,3,1,0:T(8,128)(2,1)}, bf16[8,2,256,32]{2,3,1,0:T(8,128)(2,1)}, u32[]{:S(2)}, u32[]{:S(2)}) collective-permute-start(bf16[8,2,256,32]{2,3,1,0:T(8,128)(2,1)} %copy.43), channel_id=1, source_target_pairs={{0,12},{4,0},{8,4},{12,8},{1,13},{5,1},{9,5},{13,9},{2,14},{6,2},{... | collective-permute-start | bytes 786440 | tf_op jit(solution)/shard_map/ppermute | solution.py:122
  26.1 18.0 %collective-permute-start.3 = (bf16[8,2,256,32]{2,3,1,0:T(8,128)(2,1)}, bf16[8,2,256,32]{2,3,1,0:T(8,128)(2,1)}, u32[]{:S(2)}, u32[]{:S(2)}) collective-permute-start(bf16[8,2,256,32]{2,3,1,0:T(8,128)(2,1)} %copy.43), channel_id=1, source_target_pairs={{0,4},{4,8},{8,12},{12,0},{1,5},{5,9},{9,13},{13,1},{2,6},{6,10},{... | collective-permute-start | bytes 786440 | tf_op jit(solution)/shard_map/ppermute | solution.py:122
  46.9 34.0 %collective-permute-start.6 = (bf16[8,2,256,32]{2,3,1,0:T(8,128)(2,1)}, bf16[8,2,256,32]{2,3,1,0:T(8,128)(2,1)}, u32[]{:S(2)}, u32[]{:S(2)}) collective-permute-start(bf16[8,2,256,32]{2,3,1,0:T(8,128)(2,1)} %copy.49), channel_id=1, source_target_pairs={{0,4},{4,8},{8,12},{12,0},{1,5},{5,9},{9,13},{13,1},{2,6},{6,10},{... | collective-permute-start | bytes 786440 | tf_op jit(solution)/shard_map/ppermute | solution.py:122
  52.1 28.9 %collective-permute-start.7 = (bf16[8,2,256,32]{2,3,1,0:T(8,128)(2,1)}, bf16[8,2,256,32]{2,3,1,0:T(8,128)(2,1)}, u32[]{:S(2)}, u32[]{:S(2)}) collective-permute-start(bf16[8,2,256,32]{2,3,1,0:T(8,128)(2,1)} %copy.49), channel_id=1, source_target_pairs={{0,8},{4,12},{8,0},{12,4},{1,9},{5,13},{9,1},{13,5},{2,10},{6,14},... | collective-permute-start | bytes 786440 | tf_op jit(solution)/shard_map/ppermute | solution.py:122
  54.0 26.9 %collective-permute-start.8 = (bf16[8,2,256,32]{2,3,1,0:T(8,128)(2,1)}, bf16[8,2,256,32]{2,3,1,0:T(8,128)(2,1)}, u32[]{:S(2)}, u32[]{:S(2)}) collective-permute-start(bf16[8,2,256,32]{2,3,1,0:T(8,128)(2,1)} %copy.49), channel_id=1, source_target_pairs={{0,12},{4,0},{8,4},{12,8},{1,13},{5,1},{9,5},{13,9},{2,14},{6,2},{... | collective-permute-start | bytes 786440 | tf_op jit(solution)/shard_map/ppermute | solution.py:122
  62.8 6.7 %copy-start.3 = (bf16[2,16,256,32]{3,1,0,2:T(8,128)(2,1)S(1)}, bf16[2,16,256,32]{3,1,0,2:T(8,128)(2,1)}, u32[]{:S(2)}) copy-start(bf16[2,16,256,32]{3,1,0,2:T(8,128)(2,1)} %copy.47) | copy-start | bytes 1572868
  69.5 1.7 %copy-start.4 = (bf16[2,16,256,32]{3,1,0,2:T(8,128)(2,1)S(1)}, bf16[2,16,256,32]{3,1,0,2:T(8,128)(2,1)}, u32[]{:S(2)}) copy-start(bf16[2,16,256,32]{3,1,0,2:T(8,128)(2,1)} %copy.55) | copy-start | bytes 1572868
  89.6 4.0 %copy-start.6 = (bf16[8,256,32]{1,2,0:T(8,128)(2,1)S(1)}, bf16[8,256,32]{1,2,0:T(8,128)(2,1)}, u32[]{:S(2)}) copy-start(bf16[8,256,32]{1,2,0:T(8,128)(2,1)} %get-tuple-element.28) | copy-start | bytes 393220
  100.1 2.8 %copy-start.1 = (f32[1,128,32,128]{3,1,2,0:T(8,128)S(1)}, f32[1,128,32,128]{3,1,2,0:T(8,128)}, u32[]{:S(2)}) copy-start(f32[1,128,32,128]{3,1,2,0:T(8,128)} %fusion.10) | copy-start | bytes 6291460
  100.1 2.8 %copy-start.2 = (f32[1,128,32,128]{3,1,2,0:T(8,128)S(1)}, f32[1,128,32,128]{3,1,2,0:T(8,128)}, u32[]{:S(2)}) copy-start(f32[1,128,32,128]{3,1,2,0:T(8,128)} %fusion.13) | copy-start | bytes 6291460
  100.1 2.8 %copy-start.8 = (f32[64,128]{1,0:T(8,128)S(1)}, f32[64,128]{1,0:T(8,128)}, u32[]{:S(2)}) copy-start(f32[64,128]{1,0:T(8,128)} %get-tuple-element.41) | copy-start | bytes 98308
  102.9 1.6 %copy-start = (f32[1,128,32,128]{3,1,2,0:T(8,128)S(1)}, f32[1,128,32,128]{3,1,2,0:T(8,128)}, u32[]{:S(2)}) copy-start(f32[1,128,32,128]{3,1,2,0:T(8,128)} %fusion.16) | copy-start | bytes 6291460
  102.9 1.6 %copy-start.7 = (f32[64,128]{1,0:T(8,128)S(1)}, f32[64,128]{1,0:T(8,128)}, u32[]{:S(2)}) copy-start(f32[64,128]{1,0:T(8,128)} %get-tuple-element.42) | copy-start | bytes 98308

commit v3 on v1

--- a/solution.py
+++ b/solution.py
@@ -102,12 +102,14 @@
             jnp.concatenate([partner, white], 0),
         )
     own_half = lax.dynamic_slice_in_dim(receivers, seg_position * half_sources, half_sources, 3)
-    shifted = [own_half]
-    for shift in range(1, sta_count):
-        shifted.append(
-            lax.ppermute(own_half, "sta", [(i, (i + shift) % sta_count) for i in range(sta_count)])
-        )
-    candidates = jnp.stack(shifted, 0)
+    rightward = [(i, i + 1) for i in range(sta_count - 1)]
+    leftward = [(i + 1, i) for i in range(sta_count - 1)]
+    from_left = [own_half]
+    from_right = [own_half]
+    for _ in range(1, sta_count):
+        from_left.append(lax.ppermute(from_left[-1], "sta", rightward))
+        from_right.append(lax.ppermute(from_right[-1], "sta", leftward))
+    candidates = jnp.stack(from_left + from_right[1:], 0)
     blk_dev = sta_local // SRC
     lag_weights = lag_table(band_position * band_bins).reshape(LAGS, band_bins, 2)
     receiver_ids = sta_position * sta_local + jnp.arange(sta_local, dtype=jnp.int32)
@@ -117,7 +119,11 @@
     for step_number in range(STEPS):
         block_number = plan[step_number]
         owner_position = block_number // blk_dev
-        distance = (sta_position - owner_position) % sta_count
+        distance = jnp.where(
+            owner_position <= sta_position,
+            sta_position - owner_position,
+            sta_count - 1 + owner_position - sta_position,
+        )
         held = lax.dynamic_index_in_dim(candidates, distance, 0, keepdims=False)
         sources = lax.dynamic_slice_in_dim(
             held, (block_number % blk_dev) * half_sources, half_sources, 3

time: 97.1 us -> 106 us (1.092)
  starting transfers between devices: 10.9 us -> 23.3 us
  waiting for transfers between devices: 42.6 us -> 35.3 us
  between operations: 6.79 us -> 9.33 us
  local copies, waits for them, and re-layouts: 11.5 us -> 13.6 us
  other arithmetic: 8.16 us -> 6.79 us
    ppermute x3 -> x6, starting transfers between devices: 4.67 us -> 17.1 us  [the longest x3 13.2 us: local(): from_left.append(lax.ppermute(from_left[-1], 'sta', rightward))]
    ppermute x3 -> x6, waiting for transfers between devices: 41.5 us -> 29.8 us  [the longest x3 15.9 us: local(): from_left.append(lax.ppermute(from_left[-1], 'sta', rightward))]
    ppermute x1, waiting for transfers between devices: 0.01 us -> 4.13 us  [padded(): lax.ppermute(head, axis, [((i + 1) % count, i) for i in range(ends)])]
    unnamed x18 -> x24, local copies, waits for them, and re-layouts: 3.82 us -> 5.86 us
    another operation x1 -> x0, other arithmetic: 1.46 us -> none  [local(): candidates = jnp.stack(shifted, 0)]
    ppermute x1, waiting for transfers between devices: 0.01 us -> 1.39 us  [padded(): lax.ppermute(tail, axis, [(i, (i + 1) % count) for i in range(ends)])]
    ppermute x1, waiting for transfers between devices: 1.06 us -> 0.01 us  [local(): partner = lax.ppermute(white, 'seg', [(0, 1), (1, 0)])]
  transfers between devices with their start and end apart: 6 -> 9, of which waited for: 3 -> 7; matrix products, arithmetic and copies ran while one was open for 3% -> 5% of each run, Pallas kernels for 0% -> 0%
where the time goes in v3:
time: 106 us; the launch traced here: 105 us
  waiting for transfers between devices  35.3 us (33%)
  starting transfers between devices  23.3 us (22%)
  matrix products  16.8 us (16%)
  local copies, waits for them, and re-layouts  13.6 us (13%)
  between operations  9.33 us (9%)
  other arithmetic  6.79 us (6%)
    ppermute x3, waiting for transfers between devices, local(): from_left.append(lax.ppermute(from_left[-1], 'sta', rightward))  15.9 us
    ppermute x3, waiting for transfers between devices, local(): from_right.append(lax.ppermute(from_right[-1], 'sta', leftward))  13.9 us
    ppermute x3, starting transfers between devices, local(): from_left.append(lax.ppermute(from_left[-1], 'sta', rightward))  13.2 us
    dot_general x2, matrix products, local(): lax.dot_general(lag_weights, cross_spectra, (((1, 2), (0, 1)), ((), ())),...  10.8 us
    unnamed x24, local copies, waits for them, and re-layouts  5.86 us
    dot_general x2, matrix products, cross_terms(): jnp.einsum('ctfs,tfn->fcsn', left_stack, right_stack, preferred_element_t...  5.48 us
    ppermute x1, starting transfers between devices, padded(): lax.ppermute(tail, axis, [(i, (i + 1) % count) for i in range(ends)])  4.88 us
    another operation x1, local copies, waits for them, and re-layouts, local(): return jnp.stack(results, 0)  4.71 us
  transfers between devices with their start and end apart: 9, of which 7 were waited for; matrix products, arithmetic and copies ran while one was open for 5% of the time, Pallas kernels for 0%

profile of v3, /device:TPU:0, one launch (start us, length us, event | category | flops | bytes accessed | tf_op | source)
XLA Modules:
  0.0 105.2 jit_solution(12928100849433500870)
XLA Ops:
  0.0 1.5 %sqrt_bitcast_fusion = f32[4,256,128]{2,1,0:T(8,128)S(1)} fusion(f32[4,2,256,128]{3,2,1,0:T(8,128)} %param.3), kind=kLoop, calls=%fused_computation.46 | loop fusion | flops 393216 | bytes 1572864 | tf_op jit(solution)/shard_map/sqrt | solution.py:74
  1.5 4.9 %collective-permute-start = (f32[4,64,128]{2,1,0:T(8,128)S(1)}, f32[4,64,128]{2,1,0:T(8,128)S(1)}, u32[]{:S(2)}, u32[]{:S(2)}) collective-permute-start(f32[4,64,128]{2,1,0:T(8,128)S(1)} %get-tuple-element.21), channel_id=1, source_target_pairs={{0,2},{1,3},{4,6},{5,7},{8,10},{9,11},{12,14},{13,15},{16,18},{17,... | collective-permute-start | bytes 393224 | tf_op jit(solution)/shard_map/ppermute | solution.py:28
  6.4 1.3 %collective-permute-start.1 = (f32[4,64,128]{2,1,0:T(8,128)S(1)}, f32[4,64,128]{2,1,0:T(8,128)S(1)}, u32[]{:S(2)}, u32[]{:S(2)}) collective-permute-start(f32[4,64,128]{2,1,0:T(8,128)S(1)} %get-tuple-element.22), channel_id=1, source_target_pairs={{2,0},{3,1},{6,4},{7,5},{10,8},{11,9},{14,12},{15,13},{18,16},{19,... | collective-permute-start | bytes 393224 | tf_op jit(solution)/shard_map/ppermute | solution.py:30
  7.7 1.4 %collective-permute-done = f32[4,64,128]{2,1,0:T(8,128)S(1)} collective-permute-done((f32[4,64,128]{2,1,0:T(8,128)S(1)}, f32[4,64,128]{2,1,0:T(8,128)S(1)}, u32[]{:S(2)}, u32[]{:S(2)}) %collective-permute-start) | collective-permute-done | bytes 131104 | tf_op jit(solution)/shard_map/ppermute | solution.py:28
  9.1 4.1 %collective-permute-done.1 = f32[4,64,128]{2,1,0:T(8,128)S(1)} collective-permute-done((f32[4,64,128]{2,1,0:T(8,128)S(1)}, f32[4,64,128]{2,1,0:T(8,128)S(1)}, u32[]{:S(2)}, u32[]{:S(2)}) %collective-permute-start.1) | collective-permute-done | bytes 131104 | tf_op jit(solution)/shard_map/ppermute | solution.py:30
  23.0 3.5 %collective-permute-start.3 = (bf16[8,2,256,64]{2,3,1,0:T(8,128)(2,1)S(1)}, bf16[8,2,256,64]{2,3,1,0:T(8,128)(2,1)S(1)}, u32[]{:S(2)}, u32[]{:S(2)}) collective-permute-start(bf16[8,2,256,64]{2,3,1,0:T(8,128)(2,1)S(1)} %copy.42), channel_id=1, source_target_pairs={{0,4},{4,8},{8,12},{1,5},{5,9},{9,13},{2,6},{6,10},{10,14},{3,7},{... | collective-permute-start | bytes 1572872 | tf_op jit(solution)/shard_map/ppermute | solution.py:110
  26.6 1.3 %collective-permute-start.6 = (bf16[8,2,256,64]{2,3,1,0:T(8,128)(2,1)S(1)}, bf16[8,2,256,64]{2,3,1,0:T(8,128)(2,1)}, u32[]{:S(2)}, u32[]{:S(2)}) collective-permute-start(bf16[8,2,256,64]{2,3,1,0:T(8,128)(2,1)S(1)} %copy.42), channel_id=1, source_target_pairs={{4,0},{8,4},{12,8},{5,1},{9,5},{13,9},{6,2},{10,6},{14,10},{7,3},{... | collective-permute-start | bytes 1572872 | tf_op jit(solution)/shard_map/ppermute | solution.py:111
  28.6 9.6 %collective-permute-done.3 = bf16[8,2,256,64]{2,3,1,0:T(8,128)(2,1)S(1)} collective-permute-done((bf16[8,2,256,64]{2,3,1,0:T(8,128)(2,1)S(1)}, bf16[8,2,256,64]{2,3,1,0:T(8,128)(2,1)S(1)}, u32[]{:S(2)}, u32[]{:S(2)}) %collective-permute-start.3) | collective-permute-done | bytes 524320 | tf_op jit(solution)/shard_map/ppermute | solution.py:110
  38.3 5.2 %collective-permute-start.4 = (bf16[8,2,256,64]{2,3,1,0:T(8,128)(2,1)S(1)}, bf16[8,2,256,64]{2,3,1,0:T(8,128)(2,1)}, u32[]{:S(2)}, u32[]{:S(2)}) collective-permute-start(bf16[8,2,256,64]{2,3,1,0:T(8,128)(2,1)S(1)} %collective-permute-done.3), channel_id=1, source_target_pairs={{0,4},{4,8},{8,12},{1,5},{5,9},{9,13},{2,6},{6,10},{10,14},{3,7},{... | collective-permute-start | bytes 1572872 | tf_op jit(solution)/shard_map/ppermute | solution.py:110
  47.3 1.2 %fusion.37 = (f32[128,256,1]{1,0,2:T(8,128)S(1)}, f32[128,256,1]{1,0,2:T(8,128)}) fusion(s32[256]{0:T(256)S(1)} %get-tuple-element.36, s32[128]{0:T(128)S(1)} %iota_add_fusion.5), kind=kLoop, calls=%fused_computation.64 | loop fusion | flops 491520 | bytes 263680 | tf_op jit(solution)/shard_map/cos | solution.py:48
  48.5 1.3 %collective-permute-start.7 = (bf16[8,2,256,64]{2,3,1,0:T(8,128)(2,1)}, bf16[8,2,256,64]{2,3,1,0:T(8,128)(2,1)S(1)}, u32[]{:S(2)}, u32[]{:S(2)}) collective-permute-start(bf16[8,2,256,64]{2,3,1,0:T(8,128)(2,1)} %collective-permute-done.6), channel_id=1, source_target_pairs={{4,0},{8,4},{12,8},{5,1},{9,5},{13,9},{6,2},{10,6},{14,10},{7,3},{... | collective-permute-start | bytes 1572872 | tf_op jit(solution)/shard_map/ppermute | solution.py:111
  49.9 3.8 %collective-permute-done.4 = bf16[8,2,256,64]{2,3,1,0:T(8,128)(2,1)} collective-permute-done((bf16[8,2,256,64]{2,3,1,0:T(8,128)(2,1)S(1)}, bf16[8,2,256,64]{2,3,1,0:T(8,128)(2,1)}, u32[]{:S(2)}, u32[]{:S(2)}) %collective-permute-start.4) | collective-permute-done | bytes 524320 | tf_op jit(solution)/shard_map/ppermute | solution.py:110
  53.7 4.5 %collective-permute-start.5 = (bf16[8,2,256,64]{2,3,1,0:T(8,128)(2,1)}, bf16[8,2,256,64]{2,3,1,0:T(8,128)(2,1)S(1)}, u32[]{:S(2)}, u32[]{:S(2)}) collective-permute-start(bf16[8,2,256,64]{2,3,1,0:T(8,128)(2,1)} %collective-permute-done.4), channel_id=1, source_target_pairs={{0,4},{4,8},{8,12},{1,5},{5,9},{9,13},{2,6},{6,10},{10,14},{3,7},{... | collective-permute-start | bytes 1572872 | tf_op jit(solution)/shard_map/ppermute | solution.py:110
  58.3 5.6 %collective-permute-done.7 = bf16[8,2,256,64]{2,3,1,0:T(8,128)(2,1)S(1)} collective-permute-done((bf16[8,2,256,64]{2,3,1,0:T(8,128)(2,1)}, bf16[8,2,256,64]{2,3,1,0:T(8,128)(2,1)S(1)}, u32[]{:S(2)}, u32[]{:S(2)}) %collective-permute-start.7) | collective-permute-done | bytes 524320 | tf_op jit(solution)/shard_map/ppermute | solution.py:111
  63.9 1.3 %collective-permute-start.8 = (bf16[8,2,256,64]{2,3,1,0:T(8,128)(2,1)S(1)}, bf16[8,2,256,64]{2,3,1,0:T(8,128)(2,1)S(1)}, u32[]{:S(2)}, u32[]{:S(2)}) collective-permute-start(bf16[8,2,256,64]{2,3,1,0:T(8,128)(2,1)S(1)} %collective-permute-done.7), channel_id=1, source_target_pairs={{4,0},{8,4},{12,8},{5,1},{9,5},{13,9},{6,2},{10,6},{14,10},{7,3},{... | collective-permute-start | bytes 1572872 | tf_op jit(solution)/shard_map/ppermute | solution.py:111
  65.2 1.1 %bitcast_dynamic-update-slice_fusion.4 = bf16[7,8,2,256,64]{3,4,2,1,0:T(8,128)(2,1)S(1)} fusion(bf16[7,8,2,256,64]{3,4,2,1,0:T(8,128)(2,1)S(1)} %bitcast_dynamic-update-slice_fusion.5, bf16[8,2,256,64]{2,3,1,0:T(8,128)(2,1)} %collective-permute-done.4), kind=kLoop, calls=%fused_computation.41 | loop fusion | bytes 1048576
  66.3 2.5 %collective-permute-done.5 = bf16[8,2,256,64]{2,3,1,0:T(8,128)(2,1)S(1)} collective-permute-done((bf16[8,2,256,64]{2,3,1,0:T(8,128)(2,1)}, bf16[8,2,256,64]{2,3,1,0:T(8,128)(2,1)S(1)}, u32[]{:S(2)}, u32[]{:S(2)}) %collective-permute-start.5) | collective-permute-done | bytes 524320 | tf_op jit(solution)/shard_map/ppermute | solution.py:110
  69.9 8.3 %collective-permute-done.8 = bf16[8,2,256,64]{2,3,1,0:T(8,128)(2,1)S(1)} collective-permute-done((bf16[8,2,256,64]{2,3,1,0:T(8,128)(2,1)S(1)}, bf16[8,2,256,64]{2,3,1,0:T(8,128)(2,1)S(1)}, u32[]{:S(2)}, u32[]{:S(2)}) %collective-permute-start.8) | collective-permute-done | bytes 524320 | tf_op jit(solution)/shard_map/ppermute | solution.py:111
  79.9 2.0 %copy.59 = bf16[8,1,256,64]{3,0,2,1:T(8,128)(2,1)} copy(bf16[8,1,256,64]{2,3,1,0:T(8,128)(2,1)} %get-tuple-element.13) | data formatting | bytes 524288
  83.7 2.6 %convolution_convert_fusion = bf16[256,2,64,128]{3,2,1,0:T(8,128)(2,1)S(1)} fusion(bf16[1,16,256,64]{3,1,0,2:T(8,128)(2,1)S(1)} %get-tuple-element.16, bf16[1,16,256,64]{3,1,0,2:T(8,128)(2,1)S(1)} %get-tuple-element.15, bf16[8,256,128]{2,0,1:T(8,128)(2,1)S(1)} %get-tuple-element.10, bf16[8,256,128]{2,0,1:T(8,128)(2,1)S(1)} %get-tuple-element.9), kind=kOutput, calls=%fused_computation.4 | convolution fusion | flops 141033472 | bytes 10485760 | tf_op jit(solution)/shard_map/ctfs,tfn->fcsn/dot_general | solution.py:59
  86.4 2.8 %convolution_convert_fusion.1 = bf16[256,2,64,128]{3,2,1,0:T(8,128)(2,1)S(1)} fusion(bf16[1,16,256,64]{3,1,0,2:T(8,128)(2,1)S(1)} %get-tuple-element.12, bf16[1,16,256,64]{3,1,0,2:T(8,128)(2,1)S(1)} %get-tuple-element.11, bf16[8,256,128]{2,0,1:T(8,128)(2,1)S(1)} %get-tuple-element.10, bf16[8,256,128]{2,0,1:T(8,128)(2,1)S(1)} %get-tuple-element.9), kind=kOutput, calls=%fused_computation.5 | convolution fusion | flops 141033472 | bytes 10485760 | tf_op jit(solution)/shard_map/ctfs,tfn->fcsn/dot_general | solution.py:59
  89.2 5.4 %fusion.19 = bf16[1,128,64,128]{3,1,2,0:T(8,128)(2,1)S(1)} fusion(f32[64,128]{1,0:T(8,128)S(1)} %copy-done.4, bf16[256,2,64,128]{3,2,1,0:T(8,128)(2,1)S(1)} %convolution_convert_fusion, f32[128,256,1]{1,0,2:T(8,128)S(1)} %copy-done.2, f32[128,256,1]{1,0,2:T(8,128)S(1)} %get-tuple-element.25), kind=kOutput, calls=%fused_computation.18 | convolution fusion | flops 1076035584 | bytes 10780672 | tf_op jit(solution)/shard_map/dot_general | solution.py:132
  94.7 5.4 %fusion.16 = bf16[1,128,64,128]{3,1,2,0:T(8,128)(2,1)S(1)} fusion(f32[64,128]{1,0:T(8,128)S(1)} %copy-done.3, bf16[256,2,64,128]{3,2,1,0:T(8,128)(2,1)S(1)} %convolution_convert_fusion.1, f32[128,256,1]{1,0,2:T(8,128)S(1)} %copy-done.2, f32[128,256,1]{1,0,2:T(8,128)S(1)} %get-tuple-element.25), kind=kOutput, calls=%fused_computation.17 | convolution fusion | flops 1076035584 | bytes 10780672 | tf_op jit(solution)/shard_map/dot_general | solution.py:132
  100.5 4.7 %copy.53 = bf16[2,128,64,128]{3,2,1,0:T(8,128)(2,1)} copy(bf16[2,128,64,128]{3,1,2,0:T(8,128)(2,1)S(1)} %pad_maximum_fusion) | data formatting | bytes 8388608 | tf_op jit(solution)/shard_map/stack | solution.py:149
  (53 shorter events, 10.5 us)
Async XLA Ops:
  0.0 14.3 %copy-start = (f32[4,2,256,128]{3,2,1,0:T(8,128)S(1)}, f32[4,2,256,128]{3,2,1,0:T(8,128)}, u32[]{:S(2)}) copy-start(f32[4,2,256,128]{3,2,1,0:T(8,128)} %param.3) | copy-start | bytes 3145732
  1.5 7.6 %collective-permute-start = (f32[4,64,128]{2,1,0:T(8,128)S(1)}, f32[4,64,128]{2,1,0:T(8,128)S(1)}, u32[]{:S(2)}, u32[]{:S(2)}) collective-permute-start(f32[4,64,128]{2,1,0:T(8,128)S(1)} %get-tuple-element.21), channel_id=1, source_target_pairs={{0,2},{1,3},{4,6},{5,7},{8,10},{9,11},{12,14},{13,15},{16,18},{17,... | collective-permute-start | bytes 393224 | tf_op jit(solution)/shard_map/ppermute | solution.py:28
  6.4 6.9 %collective-permute-start.1 = (f32[4,64,128]{2,1,0:T(8,128)S(1)}, f32[4,64,128]{2,1,0:T(8,128)S(1)}, u32[]{:S(2)}, u32[]{:S(2)}) collective-permute-start(f32[4,64,128]{2,1,0:T(8,128)S(1)} %get-tuple-element.22), channel_id=1, source_target_pairs={{2,0},{3,1},{6,4},{7,5},{10,8},{11,9},{14,12},{15,13},{18,16},{19,... | collective-permute-start | bytes 393224 | tf_op jit(solution)/shard_map/ppermute | solution.py:30
  7.7 7.5 %copy-start.5 = (s32[2]{0:T(128)S(1)}, s32[2]{0:T(128)}, u32[]{:S(2)}) copy-start(s32[2]{0:T(128)} %param.4) | copy-start | bytes 28
  14.4 12.1 %copy-start.6 = (s32[4,4]{1,0:T(4,128)S(1)}, s32[4,4]{1,0:T(4,128)}, u32[]{:S(2)}) copy-start(s32[4,4]{1,0:T(4,128)} %param.5) | copy-start | bytes 196
  15.1 5.8 %collective-permute-start.2 = (bf16[4,2,256,128]{3,0,2,1:T(4,128)(2,1)S(1)}, bf16[4,2,256,128]{3,0,2,1:T(4,128)(2,1)S(1)}, u32[]{:S(2)}, u32[]{:S(2)}) collective-permute-start(bf16[4,2,256,128]{3,0,2,1:T(4,128)(2,1)S(1)} %fusion.26), channel_id=1, source_target_pairs={{0,1},{1,0},{2,3},{3,2},{4,5},{5,4},{6,7},{7,6},{8,9},{9,8},{10,11... | collective-permute-start | bytes 1572872 | tf_op jit(solution)/shard_map/ppermute | solution.py:98
  23.0 15.3 %collective-permute-start.3 = (bf16[8,2,256,64]{2,3,1,0:T(8,128)(2,1)S(1)}, bf16[8,2,256,64]{2,3,1,0:T(8,128)(2,1)S(1)}, u32[]{:S(2)}, u32[]{:S(2)}) collective-permute-start(bf16[8,2,256,64]{2,3,1,0:T(8,128)(2,1)S(1)} %copy.42), channel_id=1, source_target_pairs={{0,4},{4,8},{8,12},{1,5},{5,9},{9,13},{2,6},{6,10},{10,14},{3,7},{... | collective-permute-start | bytes 1572872 | tf_op jit(solution)/shard_map/ppermute | solution.py:110
  26.6 21.9 %collective-permute-start.6 = (bf16[8,2,256,64]{2,3,1,0:T(8,128)(2,1)S(1)}, bf16[8,2,256,64]{2,3,1,0:T(8,128)(2,1)}, u32[]{:S(2)}, u32[]{:S(2)}) collective-permute-start(bf16[8,2,256,64]{2,3,1,0:T(8,128)(2,1)S(1)} %copy.42), channel_id=1, source_target_pairs={{4,0},{8,4},{12,8},{5,1},{9,5},{13,9},{6,2},{10,6},{14,10},{7,3},{... | collective-permute-start | bytes 1572872 | tf_op jit(solution)/shard_map/ppermute | solution.py:111
  38.3 15.4 %collective-permute-start.4 = (bf16[8,2,256,64]{2,3,1,0:T(8,128)(2,1)S(1)}, bf16[8,2,256,64]{2,3,1,0:T(8,128)(2,1)}, u32[]{:S(2)}, u32[]{:S(2)}) collective-permute-start(bf16[8,2,256,64]{2,3,1,0:T(8,128)(2,1)S(1)} %collective-permute-done.3), channel_id=1, source_target_pairs={{0,4},{4,8},{8,12},{1,5},{5,9},{9,13},{2,6},{6,10},{10,14},{3,7},{... | collective-permute-start | bytes 1572872 | tf_op jit(solution)/shard_map/ppermute | solution.py:110
  48.5 15.4 %collective-permute-start.7 = (bf16[8,2,256,64]{2,3,1,0:T(8,128)(2,1)}, bf16[8,2,256,64]{2,3,1,0:T(8,128)(2,1)S(1)}, u32[]{:S(2)}, u32[]{:S(2)}) collective-permute-start(bf16[8,2,256,64]{2,3,1,0:T(8,128)(2,1)} %collective-permute-done.6), channel_id=1, source_target_pairs={{4,0},{8,4},{12,8},{5,1},{9,5},{13,9},{6,2},{10,6},{14,10},{7,3},{... | collective-permute-start | bytes 1572872 | tf_op jit(solution)/shard_map/ppermute | solution.py:111
  53.7 15.0 %collective-permute-start.5 = (bf16[8,2,256,64]{2,3,1,0:T(8,128)(2,1)}, bf16[8,2,256,64]{2,3,1,0:T(8,128)(2,1)S(1)}, u32[]{:S(2)}, u32[]{:S(2)}) collective-permute-start(bf16[8,2,256,64]{2,3,1,0:T(8,128)(2,1)} %collective-permute-done.4), channel_id=1, source_target_pairs={{0,4},{4,8},{8,12},{1,5},{5,9},{9,13},{2,6},{6,10},{10,14},{3,7},{... | collective-permute-start | bytes 1572872 | tf_op jit(solution)/shard_map/ppermute | solution.py:110
  63.9 14.3 %collective-permute-start.8 = (bf16[8,2,256,64]{2,3,1,0:T(8,128)(2,1)S(1)}, bf16[8,2,256,64]{2,3,1,0:T(8,128)(2,1)S(1)}, u32[]{:S(2)}, u32[]{:S(2)}) collective-permute-start(bf16[8,2,256,64]{2,3,1,0:T(8,128)(2,1)S(1)} %collective-permute-done.7), channel_id=1, source_target_pairs={{4,0},{8,4},{12,8},{5,1},{9,5},{13,9},{6,2},{10,6},{14,10},{7,3},{... | collective-permute-start | bytes 1572872 | tf_op jit(solution)/shard_map/ppermute | solution.py:111
  82.2 1.0 copy-start.1
  86.3 2.9 %copy-start.2 = (f32[128,256,1]{1,0,2:T(8,128)S(1)}, f32[128,256,1]{1,0,2:T(8,128)}, u32[]{:S(2)}) copy-start(f32[128,256,1]{1,0,2:T(8,128)} %get-tuple-element.26) | copy-start | bytes 393220
  86.4 2.9 %copy-start.4 = (f32[64,128]{1,0:T(8,128)S(1)}, f32[64,128]{1,0:T(8,128)}, u32[]{:S(2)}) copy-start(f32[64,128]{1,0:T(8,128)} %get-tuple-element.28) | copy-start | bytes 98308
  89.2 5.4 %copy-start.3 = (f32[64,128]{1,0:T(8,128)S(1)}, f32[64,128]{1,0:T(8,128)}, u32[]{:S(2)}) copy-start(f32[64,128]{1,0:T(8,128)} %get-tuple-element.27) | copy-start | bytes 98308

commit v4 on v1

--- a/solution.py
+++ b/solution.py
@@ -23,14 +23,16 @@
         ends = count - 1
         head = lax.slice_in_dim(cells, 0, width, axis=dim)
         tail = lax.slice_in_dim(cells, cells.shape[dim] - width, cells.shape[dim], axis=dim)
-        cells = jnp.concatenate(
-            [
-                lax.ppermute(tail, axis, [(i, (i + 1) % count) for i in range(ends)]),
-                cells,
-                lax.ppermute(head, axis, [((i + 1) % count, i) for i in range(ends)]),
-            ],
-            axis=dim,
-        )
+        if count == 2:
+            first = lax.axis_index(axis) == 0
+            swapped = lax.ppermute(jnp.where(first, tail, head), axis, [(0, 1), (1, 0)])
+            zeros = jnp.zeros_like(swapped)
+            lower = jnp.where(first, zeros, swapped)
+            upper = jnp.where(first, swapped, zeros)
+        else:
+            lower = lax.ppermute(tail, axis, [(i, (i + 1) % count) for i in range(ends)])
+            upper = lax.ppermute(head, axis, [((i + 1) % count, i) for i in range(ends)])
+        cells = jnp.concatenate([lower, cells, upper], axis=dim)
     return cells
 
 
@@ -93,20 +95,26 @@
     white = (spectra / (smooth[:, None] + EPSILON)).astype(jnp.bfloat16)
     seg_count = lax.axis_size("seg")
     sta_count = lax.axis_size("sta")
-    receivers = lax.all_gather(white, "seg", axis=0, tiled=True) if seg_count > 2 else None
-    if receivers is None:
-        partner = lax.ppermute(white, "seg", [(0, 1), (1, 0)])
-        receivers = jnp.where(
-            seg_position == 0,
-            jnp.concatenate([white, partner], 0),
-            jnp.concatenate([partner, white], 0),
+    partner = lax.ppermute(white, "seg", [(h, (h + 1) % seg_count) for h in range(seg_count)])
+    receivers = jnp.concatenate([white, partner], 0)
+    halves = [
+        lax.dynamic_slice_in_dim(
+            white, ((seg_position + offset) % seg_count) * half_sources, half_sources, 3
         )
+        for offset in range(seg_count)
+    ]
     own_half = lax.dynamic_slice_in_dim(receivers, seg_position * half_sources, half_sources, 3)
     shifted = [own_half]
     for shift in range(1, sta_count):
-        shifted.append(
-            lax.ppermute(own_half, "sta", [(i, (i + shift) % sta_count) for i in range(sta_count)])
-        )
+        pieces = []
+        for offset in range(seg_count):
+            pairs = [
+                (i * seg_count + h, ((i + shift) % sta_count) * seg_count + (h + offset) % seg_count)
+                for i in range(sta_count)
+                for h in range(seg_count)
+            ]
+            pieces.append(lax.ppermute(halves[offset], ("sta", "seg"), pairs))
+        shifted.append(jnp.concatenate(pieces, 0))
     candidates = jnp.stack(shifted, 0)
     blk_dev = sta_local // SRC
     lag_weights = lag_table(band_position * band_bins).reshape(LAGS, band_bins, 2)

time: 97.1 us -> 137 us (1.41)
  waiting for transfers between devices: 42.6 us -> 83.9 us
  local copies, waits for them, and re-layouts: 11.5 us -> 8.13 us
  other arithmetic: 8.16 us -> 10.4 us
    ppermute x6 -> x8, waiting for transfers between devices: 42.6 us -> 83.9 us  [the longest x6 83.9 us: local(): pieces.append(lax.ppermute(halves[offset], ('sta', 'seg'), pairs))]
    another operation x1 -> x5, other arithmetic: 1.46 us -> 5.32 us  [local(): candidates = jnp.stack(shifted, 0)]
    unnamed x18 -> x8, local copies, waits for them, and re-layouts: 3.82 us -> 0.84 us
    ppermute x6 -> x8, starting transfers between devices: 10.9 us -> 11.1 us  [the longest x6 8.04 us: local(): pieces.append(lax.ppermute(halves[offset], ('sta', 'seg'), pairs))]
  transfers between devices with their start and end apart: 6 -> 8, of which waited for: 3 -> 4; matrix products, arithmetic and copies ran while one was open for 3% -> 4% of each run, Pallas kernels for 0% -> 0%
where the time goes in v4:
time: 137 us
  waiting for transfers between devices  83.9 us (61%)
  matrix products  16.9 us (12%)
  starting transfers between devices  11.1 us (8%)
  other arithmetic  10.4 us (8%)
  local copies, waits for them, and re-layouts  8.13 us (6%)
  between operations  6.79 us (5%)
    ppermute x6, waiting for transfers between devices, local(): pieces.append(lax.ppermute(halves[offset], ('sta', 'seg'), pairs))  83.9 us
    dot_general x2, matrix products, local(): lax.dot_general(lag_weights, cross_spectra, (((1, 2), (0, 1)), ((), ())),...  10.8 us
    ppermute x6, starting transfers between devices, local(): pieces.append(lax.ppermute(halves[offset], ('sta', 'seg'), pairs))  8.04 us
    dot_general x2, matrix products, cross_terms(): jnp.einsum('ctfs,tfn->fcsn', left_stack, right_stack, preferred_element_t...  5.52 us
    another operation x5, other arithmetic, local(): candidates = jnp.stack(shifted, 0)  5.32 us
    another operation x1, local copies, waits for them, and re-layouts, local(): return jnp.stack(results, 0)  4.71 us
    ppermute x1, starting transfers between devices, padded(): swapped = lax.ppermute(jnp.where(first, tail, head), axis, [(0, 1), (1, 0)])  3.03 us
  transfers between devices with their start and end apart: 8, of which 4 were waited for; matrix products, arithmetic and copies ran while one was open for 4% of the time, Pallas kernels for 0%

profile of v4, /device:TPU:0, one launch (start us, length us, event | category | flops | bytes accessed | tf_op | source)
XLA Modules:
  0.0 137.1 jit_solution(9307010528910072820)
XLA Ops:
  0.0 1.4 %sqrt_bitcast_fusion = f32[4,256,128]{2,1,0:T(8,128)S(1)} fusion(f32[4,2,256,128]{3,2,1,0:T(8,128)} %param.3), kind=kLoop, calls=%fused_computation.54 | loop fusion | flops 393216 | bytes 1572864 | tf_op jit(solution)/shard_map/sqrt | solution.py:76
  1.4 3.0 %collective-permute-start = (f32[4,64,128]{2,1,0:T(8,128)S(1)}, f32[4,64,128]{2,1,0:T(8,128)S(1)}, u32[]{:S(2)}, u32[]{:S(2)}) collective-permute-start(f32[4,64,128]{2,1,0:T(8,128)S(1)} %slice_select_fusion), channel_id=1, source_target_pairs={{0,2},{2,0},{1,3},{3,1},{4,6},{6,4},{5,7},{7,5},{8,10},{10,8},{9,1... | collective-permute-start | bytes 393224 | tf_op jit(solution)/shard_map/ppermute | solution.py:28
  4.5 1.3 fusion.58
  13.1 0.7 fusion.28
  13.8 0.6 constant_dynamic-slice_fusion.3
  14.4 2.8 %collective-permute-start.7 = (bf16[4,2,256,64]{3,0,2,1:T(4,128)(2,1)S(1)}, bf16[4,2,256,64]{3,0,2,1:T(4,128)(2,1)S(1)}, u32[]{:S(2)}, u32[]{:S(2)}) collective-permute-start(bf16[4,2,256,64]{3,0,2,1:T(4,128)(2,1)S(1)} %get-tuple-element.20), channel_id=1, source_target_pairs={{0,13},{1,12},{4,1},{5,0},{8,5},{9,4},{12,9},{13,8},{2,15},{3,14},... | collective-permute-start | bytes 786440 | tf_op jit(solution)/shard_map/ppermute | solution.py:116
  17.3 0.9 collective-permute-start.6
  18.2 2.7 %collective-permute-start.4 = (bf16[4,2,256,64]{3,0,2,1:T(4,128)(2,1)S(1)}, bf16[4,2,256,64]{3,0,2,1:T(4,128)(2,1)}, u32[]{:S(2)}, u32[]{:S(2)}) collective-permute-start(bf16[4,2,256,64]{3,0,2,1:T(4,128)(2,1)S(1)} %get-tuple-element.19), channel_id=1, source_target_pairs={{0,8},{1,9},{4,12},{5,13},{8,0},{9,1},{12,4},{13,5},{2,10},{3,11},... | collective-permute-start | bytes 786440 | tf_op jit(solution)/shard_map/ppermute | solution.py:116
  22.3 7.0 %collective-permute-done.7 = bf16[4,2,256,64]{3,0,2,1:T(4,128)(2,1)S(1)} collective-permute-done((bf16[4,2,256,64]{3,0,2,1:T(4,128)(2,1)S(1)}, bf16[4,2,256,64]{3,0,2,1:T(4,128)(2,1)S(1)}, u32[]{:S(2)}, u32[]{:S(2)}) %collective-permute-start.7) | collective-permute-done | bytes 262176 | tf_op jit(solution)/shard_map/ppermute | solution.py:116
  29.9 10.7 %collective-permute-done.6 = bf16[4,2,256,64]{3,0,2,1:T(4,128)(2,1)S(1)} collective-permute-done((bf16[4,2,256,64]{3,0,2,1:T(4,128)(2,1)S(1)}, bf16[4,2,256,64]{3,0,2,1:T(4,128)(2,1)S(1)}, u32[]{:S(2)}, u32[]{:S(2)}) %collective-permute-start.6) | collective-permute-done | bytes 262176 | tf_op jit(solution)/shard_map/ppermute | solution.py:116
  40.6 1.0 collective-permute-start.2
  41.7 0.7 maximum_bitcast_fusion.2
  42.3 54.8 %collective-permute-done.5 = bf16[4,2,256,64]{3,0,2,1:T(4,128)(2,1)} collective-permute-done((bf16[4,2,256,64]{3,0,2,1:T(4,128)(2,1)S(1)}, bf16[4,2,256,64]{3,0,2,1:T(4,128)(2,1)}, u32[]{:S(2)}, u32[]{:S(2)}) %collective-permute-start.5) | collective-permute-done | bytes 262176 | tf_op jit(solution)/shard_map/ppermute | solution.py:116
  97.1 11.4 %collective-permute-done.4 = bf16[4,2,256,64]{3,0,2,1:T(4,128)(2,1)} collective-permute-done((bf16[4,2,256,64]{3,0,2,1:T(4,128)(2,1)S(1)}, bf16[4,2,256,64]{3,0,2,1:T(4,128)(2,1)}, u32[]{:S(2)}, u32[]{:S(2)}) %collective-permute-start.4) | collective-permute-done | bytes 262176 | tf_op jit(solution)/shard_map/ppermute | solution.py:116
  108.5 1.9 %maximum_bitcast_fusion.1 = bf16[1,8,2,256,64]{4,1,3,2,0:T(8,128)(2,1)S(1)} fusion(bf16[4,2,256,64]{3,0,2,1:T(4,128)(2,1)} %collective-permute-done.5, bf16[4,2,256,64]{3,0,2,1:T(4,128)(2,1)} %collective-permute-done.4), kind=kLoop, calls=%fused_computation.31 | loop fusion | flops 1048576 | bytes 1048576 | tf_op jit(solution)/shard_map/stack | solution.py:118
  110.4 0.7 maximum_bitcast_fusion
  111.1 0.9 fusion.23
  112.0 1.2 pad_maximum_fusion
  114.5 0.6 copy-done.2
  115.7 2.6 %convolution_convert_fusion = bf16[256,2,64,128]{3,2,1,0:T(8,128)(2,1)S(1)} fusion(bf16[1,16,256,64]{3,1,0,2:T(8,128)(2,1)S(1)} %get-tuple-element.18, bf16[1,16,256,64]{3,1,0,2:T(8,128)(2,1)S(1)} %get-tuple-element.17, bf16[8,256,128]{2,0,1:T(8,128)(2,1)S(1)} %get-tuple-element.12, bf16[8,256,128]{2,0,1:T(8,128)(2,1)S(1)} %get-tuple-element.11), kind=kOutput, calls=%fused_computation.4 | convolution fusion | flops 141033472 | bytes 10485760 | tf_op jit(solution)/shard_map/ctfs,tfn->fcsn/dot_general | solution.py:61
  118.3 2.9 %convolution_convert_fusion.1 = bf16[256,2,64,128]{3,2,1,0:T(8,128)(2,1)S(1)} fusion(bf16[1,16,256,64]{3,1,0,2:T(8,128)(2,1)S(1)} %get-tuple-element.16, bf16[1,16,256,64]{3,1,0,2:T(8,128)(2,1)S(1)} %get-tuple-element.15, bf16[8,256,128]{2,0,1:T(8,128)(2,1)S(1)} %get-tuple-element.12, bf16[8,256,128]{2,0,1:T(8,128)(2,1)S(1)} %get-tuple-element.11), kind=kOutput, calls=%fused_computation.5 | convolution fusion | flops 141033472 | bytes 10485760 | tf_op jit(solution)/shard_map/ctfs,tfn->fcsn/dot_general | solution.py:61
  121.2 5.4 %fusion.19 = bf16[1,128,64,128]{3,1,2,0:T(8,128)(2,1)S(1)} fusion(f32[64,128]{1,0:T(8,128)S(1)} %get-tuple-element.30, bf16[256,2,64,128]{3,2,1,0:T(8,128)(2,1)S(1)} %convolution_convert_fusion, f32[128,256,1]{1,0,2:T(8,128)S(1)} %get-tuple-element.28, f32[128,256,1]{1,0,2:T(8,128)S(1)} %get-tuple-element.27), kind=kOutput, calls=%fused_computation.19 | convolution fusion | flops 1076035584 | bytes 10780672 | tf_op jit(solution)/shard_map/dot_general | solution.py:134
  126.6 5.4 %fusion.16 = bf16[1,128,64,128]{3,1,2,0:T(8,128)(2,1)S(1)} fusion(f32[64,128]{1,0:T(8,128)S(1)} %get-tuple-element.29, bf16[256,2,64,128]{3,2,1,0:T(8,128)(2,1)S(1)} %convolution_convert_fusion.1, f32[128,256,1]{1,0,2:T(8,128)S(1)} %get-tuple-element.28, f32[128,256,1]{1,0,2:T(8,128)S(1)} %get-tuple-element.27), kind=kOutput, calls=%fused_computation.18 | convolution fusion | flops 1076035584 | bytes 10780672 | tf_op jit(solution)/shard_map/dot_general | solution.py:134
  132.4 4.7 %copy.26 = bf16[2,128,64,128]{3,2,1,0:T(8,128)(2,1)} copy(bf16[2,128,64,128]{3,1,2,0:T(8,128)(2,1)S(1)} %pad_maximum_fusion.1) | data formatting | bytes 8388608 | tf_op jit(solution)/shard_map/stack | solution.py:151
  (38 shorter events, 4.9 us)
Async XLA Ops:
  0.0 10.3 %copy-start.3 = (s32[4,4]{1,0:T(4,128)S(1)}, s32[4,4]{1,0:T(4,128)}, u32[]{:S(2)}) copy-start(s32[4,4]{1,0:T(4,128)} %param.5) | copy-start | bytes 196
  1.4 10.3 %collective-permute-start = (f32[4,64,128]{2,1,0:T(8,128)S(1)}, f32[4,64,128]{2,1,0:T(8,128)S(1)}, u32[]{:S(2)}, u32[]{:S(2)}) collective-permute-start(f32[4,64,128]{2,1,0:T(8,128)S(1)} %slice_select_fusion), channel_id=1, source_target_pairs={{0,2},{2,0},{1,3},{3,1},{4,6},{6,4},{5,7},{7,5},{8,10},{10,8},{9,1... | collective-permute-start | bytes 393224 | tf_op jit(solution)/shard_map/ppermute | solution.py:28
  11.8 1.2 copy-start
  14.4 14.9 %collective-permute-start.7 = (bf16[4,2,256,64]{3,0,2,1:T(4,128)(2,1)S(1)}, bf16[4,2,256,64]{3,0,2,1:T(4,128)(2,1)S(1)}, u32[]{:S(2)}, u32[]{:S(2)}) collective-permute-start(bf16[4,2,256,64]{3,0,2,1:T(4,128)(2,1)S(1)} %get-tuple-element.20), channel_id=1, source_target_pairs={{0,13},{1,12},{4,1},{5,0},{8,5},{9,4},{12,9},{13,8},{2,15},{3,14},... | collective-permute-start | bytes 786440 | tf_op jit(solution)/shard_map/ppermute | solution.py:116
  17.3 23.4 %collective-permute-start.6 = (bf16[4,2,256,64]{3,0,2,1:T(4,128)(2,1)S(1)}, bf16[4,2,256,64]{3,0,2,1:T(4,128)(2,1)S(1)}, u32[]{:S(2)}, u32[]{:S(2)}) collective-permute-start(bf16[4,2,256,64]{3,0,2,1:T(4,128)(2,1)S(1)} %get-tuple-element.19), channel_id=1, source_target_pairs={{0,12},{1,13},{4,0},{5,1},{8,4},{9,5},{12,8},{13,9},{2,14},{3,15},... | collective-permute-start | bytes 786440 | tf_op jit(solution)/shard_map/ppermute | solution.py:116
  18.2 79.0 %collective-permute-start.5 = (bf16[4,2,256,64]{3,0,2,1:T(4,128)(2,1)S(1)}, bf16[4,2,256,64]{3,0,2,1:T(4,128)(2,1)}, u32[]{:S(2)}, u32[]{:S(2)}) collective-permute-start(bf16[4,2,256,64]{3,0,2,1:T(4,128)(2,1)S(1)} %get-tuple-element.20), channel_id=1, source_target_pairs={{0,9},{1,8},{4,13},{5,12},{8,1},{9,0},{12,5},{13,4},{2,11},{3,10},... | collective-permute-start | bytes 786440 | tf_op jit(solution)/shard_map/ppermute | solution.py:116
  18.2 90.3 %collective-permute-start.4 = (bf16[4,2,256,64]{3,0,2,1:T(4,128)(2,1)S(1)}, bf16[4,2,256,64]{3,0,2,1:T(4,128)(2,1)}, u32[]{:S(2)}, u32[]{:S(2)}) collective-permute-start(bf16[4,2,256,64]{3,0,2,1:T(4,128)(2,1)S(1)} %get-tuple-element.19), channel_id=1, source_target_pairs={{0,8},{1,9},{4,12},{5,13},{8,0},{9,1},{12,4},{13,5},{2,10},{3,11},... | collective-permute-start | bytes 786440 | tf_op jit(solution)/shard_map/ppermute | solution.py:116
  20.9 90.2 %collective-permute-start.1 = (bf16[4,2,256,128]{3,0,2,1:T(4,128)(2,1)S(1)}, bf16[4,2,256,128]{3,0,2,1:T(4,128)(2,1)S(1)}, u32[]{:S(2)}, u32[]{:S(2)}) collective-permute-start(bf16[4,2,256,128]{3,0,2,1:T(4,128)(2,1)S(1)} %fusion.28), channel_id=1, source_target_pairs={{0,1},{1,0},{2,3},{3,2},{4,5},{5,4},{6,7},{7,6},{8,9},{9,8},{10,11... | collective-permute-start | bytes 1572872 | tf_op jit(solution)/shard_map/ppermute | solution.py:98
  29.4 81.0 %collective-permute-start.3 = (bf16[4,2,256,64]{3,0,2,1:T(4,128)(2,1)S(1)}, bf16[4,2,256,64]{3,0,2,1:T(4,128)(2,1)S(1)}, u32[]{:S(2)}, u32[]{:S(2)}) collective-permute-start(bf16[4,2,256,64]{3,0,2,1:T(4,128)(2,1)S(1)} %get-tuple-element.20), channel_id=1, source_target_pairs={{0,5},{1,4},{4,9},{5,8},{8,13},{9,12},{12,1},{13,0},{2,7},{3,6},{6... | collective-permute-start | bytes 786440 | tf_op jit(solution)/shard_map/ppermute | solution.py:116
  40.6 69.8 %collective-permute-start.2 = (bf16[4,2,256,64]{3,0,2,1:T(4,128)(2,1)S(1)}, bf16[4,2,256,64]{3,0,2,1:T(4,128)(2,1)S(1)}, u32[]{:S(2)}, u32[]{:S(2)}) collective-permute-start(bf16[4,2,256,64]{3,0,2,1:T(4,128)(2,1)S(1)} %get-tuple-element.19), channel_id=1, source_target_pairs={{0,4},{1,5},{4,8},{5,9},{8,12},{9,13},{12,0},{13,1},{2,6},{3,7},{6... | collective-permute-start | bytes 786440 | tf_op jit(solution)/shard_map/ppermute | solution.py:116
  111.1 2.1 %copy-start.1 = (bf16[4,2,256,128]{3,0,2,1:T(4,128)(2,1)}, bf16[4,2,256,128]{3,0,2,1:T(4,128)(2,1)S(1)}, u32[]{:S(2)}) copy-start(bf16[4,2,256,128]{3,0,2,1:T(4,128)(2,1)S(1)} %collective-permute-done.1) | copy-start | bytes 1572868
  114.1 1.0 copy-start.2

commit v5 on v1

--- a/solution.py
+++ b/solution.py
@@ -23,14 +23,16 @@
         ends = count - 1
         head = lax.slice_in_dim(cells, 0, width, axis=dim)
         tail = lax.slice_in_dim(cells, cells.shape[dim] - width, cells.shape[dim], axis=dim)
-        cells = jnp.concatenate(
-            [
-                lax.ppermute(tail, axis, [(i, (i + 1) % count) for i in range(ends)]),
-                cells,
-                lax.ppermute(head, axis, [((i + 1) % count, i) for i in range(ends)]),
-            ],
-            axis=dim,
-        )
+        if count == 2:
+            first = lax.axis_index(axis) == 0
+            swapped = lax.ppermute(jnp.where(first, tail, head), axis, [(0, 1), (1, 0)])
+            zeros = jnp.zeros_like(swapped)
+            lower = jnp.where(first, zeros, swapped)
+            upper = jnp.where(first, swapped, zeros)
+        else:
+            lower = lax.ppermute(tail, axis, [(i, (i + 1) % count) for i in range(ends)])
+            upper = lax.ppermute(head, axis, [((i + 1) % count, i) for i in range(ends)])
+        cells = jnp.concatenate([lower, cells, upper], axis=dim)
     return cells
 
 

time: 97.1 us -> 94.3 us (0.971)
  starting transfers between devices: 10.9 us -> 7.77 us
    ppermute x2 -> x1, starting transfers between devices: 6.17 us -> 3.03 us  [padded(): swapped = lax.ppermute(jnp.where(first, tail, head), axis, [(0, 1), (1, 0)])]
    unnamed x18 -> x16, local copies, waits for them, and re-layouts: 3.82 us -> 3.81 us
  transfers between devices with their start and end apart: 6 -> 5, of which waited for: 3 -> 3; matrix products, arithmetic and copies ran while one was open for 3% -> 4% of each run, Pallas kernels for 0% -> 0%
where the time goes in v5:
time: 94.3 us; the launch traced here: 94 us
  waiting for transfers between devices  42.7 us (45%)
  matrix products  16.8 us (18%)
  local copies, waits for them, and re-layouts  12.2 us (13%)
  other arithmetic  8.18 us (9%)
  starting transfers between devices  7.77 us (8%)
  between operations  6.33 us (7%)
    ppermute x3, waiting for transfers between devices, local(): lax.ppermute(own_half, 'sta', [(i, (i + shift) % sta_count) for i in rang...  41.6 us
    dot_general x2, matrix products, local(): lax.dot_general(lag_weights, cross_spectra, (((1, 2), (0, 1)), ((), ())),...  10.8 us
    dot_general x2, matrix products, cross_terms(): jnp.einsum('ctfs,tfn->fcsn', left_stack, right_stack, preferred_element_t...  5.48 us
    another operation x1, local copies, waits for them, and re-layouts, local(): return jnp.stack(results, 0)  4.71 us
    ppermute x3, starting transfers between devices, local(): lax.ppermute(own_half, 'sta', [(i, (i + shift) % sta_count) for i in rang...  4.67 us
    unnamed x16, local copies, waits for them, and re-layouts  3.81 us
    ppermute x1, starting transfers between devices, padded(): swapped = lax.ppermute(jnp.where(first, tail, head), axis, [(0, 1), (1, 0)])  3.03 us
  transfers between devices with their start and end apart: 5, of which 3 were waited for; matrix products, arithmetic and copies ran while one was open for 4% of the time, Pallas kernels for 0%

profile of v5, /device:TPU:0, one launch (start us, length us, event | category | flops | bytes accessed | tf_op | source)
XLA Modules:
  0.0 94.0 jit_solution(11154546479091370324)
XLA Ops:
  0.0 1.4 %sqrt_bitcast_fusion = f32[4,256,128]{2,1,0:T(8,128)S(1)} fusion(f32[4,2,256,128]{3,2,1,0:T(8,128)} %param.3), kind=kLoop, calls=%fused_computation.40 | loop fusion | flops 393216 | bytes 1572864 | tf_op jit(solution)/shard_map/sqrt | solution.py:76
  1.4 3.0 %collective-permute-start = (f32[4,64,128]{2,1,0:T(8,128)S(1)}, f32[4,64,128]{2,1,0:T(8,128)S(1)}, u32[]{:S(2)}, u32[]{:S(2)}) collective-permute-start(f32[4,64,128]{2,1,0:T(8,128)S(1)} %slice_select_fusion), channel_id=1, source_target_pairs={{0,2},{2,0},{1,3},{3,1},{4,6},{6,4},{5,7},{7,5},{8,10},{10,8},{9,1... | collective-permute-start | bytes 393224 | tf_op jit(solution)/shard_map/ppermute | solution.py:28
  4.4 1.3 %fusion.53 = (s32[1]{0:T(128)}, s32[1]{0:T(128)}) fusion(s32[2]{0:T(128)} %param.4), kind=kLoop, calls=%fused_computation.96 | loop fusion | bytes 16 | tf_op jit(solution)/shard_map/slice | solution.py:120
  10.7 0.5 fusion.22
  11.9 0.7 fusion.26
  12.9 0.7 compare_select_fusion.1
  13.6 1.1 %collective-permute-done.1 = bf16[4,2,256,128]{3,0,2,1:T(4,128)(2,1)S(1)} collective-permute-done((bf16[4,2,256,128]{3,0,2,1:T(4,128)(2,1)S(1)}, bf16[4,2,256,128]{3,0,2,1:T(4,128)(2,1)S(1)}, u32[]{:S(2)}, u32[]{:S(2)}) %collective-permute-start.1) | collective-permute-done | bytes 524320 | tf_op jit(solution)/shard_map/ppermute | solution.py:100
  14.7 0.9 %maximum_select_fusion = bf16[8,2,256,128]{3,0,2,1:T(8,128)(2,1)S(1)} fusion(bf16[4,2,256,128]{3,0,2,1:T(4,128)(2,1)S(1)} %collective-permute-done.1, bf16[4,2,256,128]{3,0,2,1:T(4,128)(2,1)S(1)} %fusion.26, pred[]{:T(512)S(6)} %eq.26), kind=kLoop, calls=%fused_computation.24 | loop fusion | flops 4718592 | bytes 2097153 | tf_op jit(solution)/shard_map/jit(_where)/select_n | solution.py:101
  16.0 0.7 copy.43
  16.7 3.7 %collective-permute-start.4 = (bf16[8,2,256,64]{2,3,1,0:T(8,128)(2,1)S(1)}, bf16[8,2,256,64]{2,3,1,0:T(8,128)(2,1)S(1)}, u32[]{:S(2)}, u32[]{:S(2)}) collective-permute-start(bf16[8,2,256,64]{2,3,1,0:T(8,128)(2,1)S(1)} %copy.43), channel_id=1, source_target_pairs={{0,12},{4,0},{8,4},{12,8},{1,13},{5,1},{9,5},{13,9},{2,14},{6,2},{... | collective-permute-start | bytes 1572872 | tf_op jit(solution)/shard_map/ppermute | solution.py:110
  20.4 1.0 %collective-permute-start.2 = (bf16[8,2,256,64]{2,3,1,0:T(8,128)(2,1)S(1)}, bf16[8,2,256,64]{2,3,1,0:T(8,128)(2,1)}, u32[]{:S(2)}, u32[]{:S(2)}) collective-permute-start(bf16[8,2,256,64]{2,3,1,0:T(8,128)(2,1)S(1)} %copy.43), channel_id=1, source_target_pairs={{0,4},{4,8},{8,12},{12,0},{1,5},{5,9},{9,13},{13,1},{2,6},{6,10},{... | collective-permute-start | bytes 1572872 | tf_op jit(solution)/shard_map/ppermute | solution.py:110
  22.6 1.3 %fusion.37 = (f32[128,256,1]{1,0,2:T(8,128)S(1)}, f32[128,256,1]{1,0,2:T(8,128)}) fusion(s32[256]{0:T(256)S(1)} %get-tuple-element.36, s32[128]{0:T(128)S(1)} %iota_add_fusion.5), kind=kLoop, calls=%fused_computation.61 | loop fusion | flops 491520 | bytes 263680 | tf_op jit(solution)/shard_map/cos | solution.py:50
  23.9 8.8 %collective-permute-done.4 = bf16[8,2,256,64]{2,3,1,0:T(8,128)(2,1)S(1)} collective-permute-done((bf16[8,2,256,64]{2,3,1,0:T(8,128)(2,1)S(1)}, bf16[8,2,256,64]{2,3,1,0:T(8,128)(2,1)S(1)}, u32[]{:S(2)}, u32[]{:S(2)}) %collective-permute-start.4) | collective-permute-done | bytes 524320 | tf_op jit(solution)/shard_map/ppermute | solution.py:110
  32.7 32.8 %collective-permute-done.3 = bf16[8,2,256,64]{2,3,1,0:T(8,128)(2,1)} collective-permute-done((bf16[8,2,256,64]{2,3,1,0:T(8,128)(2,1)S(1)}, bf16[8,2,256,64]{2,3,1,0:T(8,128)(2,1)}, u32[]{:S(2)}, u32[]{:S(2)}) %collective-permute-start.3) | collective-permute-done | bytes 524320 | tf_op jit(solution)/shard_map/ppermute | solution.py:110
  65.5 1.5 %pad_maximum_fusion.1 = bf16[4,8,2,256,64]{3,4,2,1,0:T(8,128)(2,1)S(1)} fusion(bf16[1,8,2,256,64]{3,4,2,1,0:T(8,128)(2,1)S(1)} %bitcast.86, bf16[1,8,2,256,64]{3,4,2,1,0:T(8,128)(2,1)} %bitcast.10, bf16[1,8,2,256,64]{3,4,2,1,0:T(8,128)(2,1)} %bitcast.9, bf16[1,8,2,256,64]{3,4,2,1,0:T(8,128)(2,1)S(1)} %bitcast.85), kind=kLoop, calls=%fused_computation.11 | loop fusion | flops 3145728 | bytes 4194304 | tf_op jit(solution)/shard_map/stack | solution.py:112
  67.9 0.7 fusion.51
  68.6 2.0 %copy.61 = bf16[8,1,256,64]{3,0,2,1:T(8,128)(2,1)} copy(bf16[8,1,256,64]{2,3,1,0:T(8,128)(2,1)} %get-tuple-element.13) | data formatting | bytes 524288
  71.4 0.6 copy-done.1
  72.1 0.4 maximum_bitcast_fusion
  72.5 2.6 %convolution_convert_fusion = bf16[256,2,64,128]{3,2,1,0:T(8,128)(2,1)S(1)} fusion(bf16[1,16,256,64]{3,1,0,2:T(8,128)(2,1)S(1)} %get-tuple-element.16, bf16[1,16,256,64]{3,1,0,2:T(8,128)(2,1)S(1)} %get-tuple-element.15, bf16[8,256,128]{2,0,1:T(8,128)(2,1)S(1)} %get-tuple-element.10, bf16[8,256,128]{2,0,1:T(8,128)(2,1)S(1)} %get-tuple-element.9), kind=kOutput, calls=%fused_computation.4 | convolution fusion | flops 141033472 | bytes 10485760 | tf_op jit(solution)/shard_map/ctfs,tfn->fcsn/dot_general | solution.py:61
  75.2 2.8 %convolution_convert_fusion.1 = bf16[256,2,64,128]{3,2,1,0:T(8,128)(2,1)S(1)} fusion(bf16[1,16,256,64]{3,1,0,2:T(8,128)(2,1)S(1)} %get-tuple-element.12, bf16[1,16,256,64]{3,1,0,2:T(8,128)(2,1)S(1)} %get-tuple-element.11, bf16[8,256,128]{2,0,1:T(8,128)(2,1)S(1)} %get-tuple-element.10, bf16[8,256,128]{2,0,1:T(8,128)(2,1)S(1)} %get-tuple-element.9), kind=kOutput, calls=%fused_computation.5 | convolution fusion | flops 141033472 | bytes 10485760 | tf_op jit(solution)/shard_map/ctfs,tfn->fcsn/dot_general | solution.py:61
  78.0 5.4 %fusion.19 = bf16[1,128,64,128]{3,1,2,0:T(8,128)(2,1)S(1)} fusion(f32[64,128]{1,0:T(8,128)S(1)} %copy-done.4, bf16[256,2,64,128]{3,2,1,0:T(8,128)(2,1)S(1)} %convolution_convert_fusion, f32[128,256,1]{1,0,2:T(8,128)S(1)} %copy-done.2, f32[128,256,1]{1,0,2:T(8,128)S(1)} %get-tuple-element.25), kind=kOutput, calls=%fused_computation.19 | convolution fusion | flops 1076035584 | bytes 10780672 | tf_op jit(solution)/shard_map/dot_general | solution.py:128
  83.5 5.4 %fusion.16 = bf16[1,128,64,128]{3,1,2,0:T(8,128)(2,1)S(1)} fusion(f32[64,128]{1,0:T(8,128)S(1)} %copy-done.3, bf16[256,2,64,128]{3,2,1,0:T(8,128)(2,1)S(1)} %convolution_convert_fusion.1, f32[128,256,1]{1,0,2:T(8,128)S(1)} %copy-done.2, f32[128,256,1]{1,0,2:T(8,128)S(1)} %get-tuple-element.25), kind=kOutput, calls=%fused_computation.18 | convolution fusion | flops 1076035584 | bytes 10780672 | tf_op jit(solution)/shard_map/dot_general | solution.py:128
  89.3 4.7 %copy.55 = bf16[2,128,64,128]{3,2,1,0:T(8,128)(2,1)} copy(bf16[2,128,64,128]{3,1,2,0:T(8,128)(2,1)S(1)} %pad_maximum_fusion) | data formatting | bytes 8388608 | tf_op jit(solution)/shard_map/stack | solution.py:145
  (38 shorter events, 3.4 us)
Async XLA Ops:
  1.4 9.2 %collective-permute-start = (f32[4,64,128]{2,1,0:T(8,128)S(1)}, f32[4,64,128]{2,1,0:T(8,128)S(1)}, u32[]{:S(2)}, u32[]{:S(2)}) collective-permute-start(f32[4,64,128]{2,1,0:T(8,128)S(1)} %slice_select_fusion), channel_id=1, source_target_pairs={{0,2},{2,0},{1,3},{3,1},{4,6},{6,4},{5,7},{7,5},{8,10},{10,8},{9,1... | collective-permute-start | bytes 393224 | tf_op jit(solution)/shard_map/ppermute | solution.py:28
  10.7 1.2 %copy-start = (f32[4,2,256,128]{3,2,1,0:T(8,128)S(1)}, f32[4,2,256,128]{3,2,1,0:T(8,128)}, u32[]{:S(2)}) copy-start(f32[4,2,256,128]{3,2,1,0:T(8,128)} %param.3) | copy-start | bytes 3145732
  11.3 1.5 %copy-start.5 = (s32[4,4]{1,0:T(4,128)S(1)}, s32[4,4]{1,0:T(4,128)}, u32[]{:S(2)}) copy-start(s32[4,4]{1,0:T(4,128)} %param.5) | copy-start | bytes 196
  12.7 2.0 %collective-permute-start.1 = (bf16[4,2,256,128]{3,0,2,1:T(4,128)(2,1)S(1)}, bf16[4,2,256,128]{3,0,2,1:T(4,128)(2,1)S(1)}, u32[]{:S(2)}, u32[]{:S(2)}) collective-permute-start(bf16[4,2,256,128]{3,0,2,1:T(4,128)(2,1)S(1)} %fusion.26), channel_id=1, source_target_pairs={{0,1},{1,0},{2,3},{3,2},{4,5},{5,4},{6,7},{7,6},{8,9},{9,8},{10,11... | collective-permute-start | bytes 1572872 | tf_op jit(solution)/shard_map/ppermute | solution.py:100
  16.7 16.1 %collective-permute-start.4 = (bf16[8,2,256,64]{2,3,1,0:T(8,128)(2,1)S(1)}, bf16[8,2,256,64]{2,3,1,0:T(8,128)(2,1)S(1)}, u32[]{:S(2)}, u32[]{:S(2)}) collective-permute-start(bf16[8,2,256,64]{2,3,1,0:T(8,128)(2,1)S(1)} %copy.43), channel_id=1, source_target_pairs={{0,12},{4,0},{8,4},{12,8},{1,13},{5,1},{9,5},{13,9},{2,14},{6,2},{... | collective-permute-start | bytes 1572872 | tf_op jit(solution)/shard_map/ppermute | solution.py:110
  20.3 45.2 %collective-permute-start.3 = (bf16[8,2,256,64]{2,3,1,0:T(8,128)(2,1)S(1)}, bf16[8,2,256,64]{2,3,1,0:T(8,128)(2,1)}, u32[]{:S(2)}, u32[]{:S(2)}) collective-permute-start(bf16[8,2,256,64]{2,3,1,0:T(8,128)(2,1)S(1)} %copy.43), channel_id=1, source_target_pairs={{0,8},{4,12},{8,0},{12,4},{1,9},{5,13},{9,1},{13,5},{2,10},{6,14},... | collective-permute-start | bytes 1572872 | tf_op jit(solution)/shard_map/ppermute | solution.py:110
  20.4 45.2 %collective-permute-start.2 = (bf16[8,2,256,64]{2,3,1,0:T(8,128)(2,1)S(1)}, bf16[8,2,256,64]{2,3,1,0:T(8,128)(2,1)}, u32[]{:S(2)}, u32[]{:S(2)}) collective-permute-start(bf16[8,2,256,64]{2,3,1,0:T(8,128)(2,1)S(1)} %copy.43), channel_id=1, source_target_pairs={{0,4},{4,8},{8,12},{12,0},{1,5},{5,9},{9,13},{13,1},{2,6},{6,10},{... | collective-permute-start | bytes 1572872 | tf_op jit(solution)/shard_map/ppermute | solution.py:110
  71.0 1.0 %copy-start.1 = (bf16[8,1,256,64]{3,0,2,1:T(8,128)(2,1)S(1)}, bf16[8,1,256,64]{3,0,2,1:T(8,128)(2,1)}, u32[]{:S(2)}) copy-start(bf16[8,1,256,64]{3,0,2,1:T(8,128)(2,1)} %copy.61) | copy-start | bytes 786436
  75.1 2.9 %copy-start.2 = (f32[128,256,1]{1,0,2:T(8,128)S(1)}, f32[128,256,1]{1,0,2:T(8,128)}, u32[]{:S(2)}) copy-start(f32[128,256,1]{1,0,2:T(8,128)} %get-tuple-element.26) | copy-start | bytes 393220
  75.1 2.9 %copy-start.4 = (f32[64,128]{1,0:T(8,128)S(1)}, f32[64,128]{1,0:T(8,128)}, u32[]{:S(2)}) copy-start(f32[64,128]{1,0:T(8,128)} %get-tuple-element.28) | copy-start | bytes 98308
  78.0 5.4 %copy-start.3 = (f32[64,128]{1,0:T(8,128)S(1)}, f32[64,128]{1,0:T(8,128)}, u32[]{:S(2)}) copy-start(f32[64,128]{1,0:T(8,128)} %get-tuple-element.27) | copy-start | bytes 98308

commit v6 on v5

--- a/solution.py
+++ b/solution.py
@@ -109,28 +109,30 @@
         shifted.append(
             lax.ppermute(own_half, "sta", [(i, (i + shift) % sta_count) for i in range(sta_count)])
         )
-    candidates = jnp.stack(shifted, 0)
     blk_dev = sta_local // SRC
     lag_weights = lag_table(band_position * band_bins).reshape(LAGS, band_bins, 2)
     receiver_ids = sta_position * sta_local + jnp.arange(sta_local, dtype=jnp.int32)
     block_columns = jnp.arange(pair_mask.shape[1], dtype=jnp.int32)
     block_onehot = ((receiver_ids // SRC)[:, None] == block_columns[None, :]).astype(jnp.float32)
+    chosen = []
+    for step_number in range(STEPS):
+        owner_position = plan[step_number] // blk_dev
+        distance = (sta_position - owner_position) % sta_count
+        sources = shifted[0]
+        for shift in range(1, sta_count):
+            sources = jnp.where(distance == shift, shifted[shift], sources)
+        chosen.append(sources)
+    sources = jnp.concatenate(chosen, 3)
+    cross_spectra = cross_terms(sources, receivers)
+    correlated = lax.dot_general(
+        lag_weights,
+        cross_spectra,
+        (((1, 2), (0, 1)), ((), ())),
+        preferred_element_type=jnp.float32,
+    )
     results = []
     for step_number in range(STEPS):
         block_number = plan[step_number]
-        owner_position = block_number // blk_dev
-        distance = (sta_position - owner_position) % sta_count
-        held = lax.dynamic_index_in_dim(candidates, distance, 0, keepdims=False)
-        sources = lax.dynamic_slice_in_dim(
-            held, (block_number % blk_dev) * half_sources, half_sources, 3
-        )
-        cross_spectra = cross_terms(sources, receivers)
-        correlated = lax.dot_general(
-            lag_weights,
-            cross_spectra,
-            (((1, 2), (0, 1)), ((), ())),
-            preferred_element_type=jnp.float32,
-        )
         mask_row = pair_mask[block_number].astype(jnp.float32)
         allowed = jnp.sum(block_onehot * mask_row[None, :], axis=1)
         source_ids = (
@@ -141,7 +143,8 @@
         keep_pairs = (source_ids[:, None] != receiver_ids[None, :]).astype(jnp.float32) * allowed[
             None, :
         ]
-        results.append((correlated * keep_pairs[None]).astype(jnp.bfloat16))
+        part = lax.slice_in_dim(correlated, step_number * half_sources, (step_number + 1) * half_sources, axis=1)
+        results.append((part * keep_pairs[None]).astype(jnp.bfloat16))
     return jnp.stack(results, 0)
 
 

time: 94.3 us -> 105 us (1.11)
  the two profiles are of different devices: /device:TPU:0 before, /device:TPU:24 now
where the time goes in v6:
time: 105 us
  waiting for transfers between devices  43.7 us (42%)
  matrix products  26.8 us (26%)
  local copies, waits for them, and re-layouts  15.1 us (14%)
  other arithmetic  9.01 us (9%)
  between operations  6.34 us (6%)
  starting transfers between devices  3.99 us (4%)
    ppermute x3, waiting for transfers between devices, local(): lax.ppermute(own_half, 'sta', [(i, (i + shift) % sta_count) for i in rang...  42 us
    dot_general x1, matrix products, local(): lax.dot_general(lag_weights, cross_spectra, (((1, 2), (0, 1)), ((), ())),...  18.1 us
    dot_general x1, matrix products, cross_terms(): jnp.einsum('ctfs,tfn->fcsn', left_stack, right_stack, preferred_element_t...  8.17 us
    another operation x1, local copies, waits for them, and re-layouts, local(): return jnp.stack(results, 0)  4.71 us
    ppermute x3, local copies, waits for them, and re-layouts, local(): lax.ppermute(own_half, 'sta', [(i, (i + shift) % sta_count) for i in rang...  4.68 us
    ppermute x3, starting transfers between devices, local(): lax.ppermute(own_half, 'sta', [(i, (i + shift) % sta_count) for i in rang...  2.36 us
    select_n x1, other arithmetic, local(): sources = jnp.where(distance == shift, shifted[shift], sources)  2.24 us
  transfers between devices with their start and end apart: 5, of which 3 were waited for; matrix products, arithmetic and copies ran while one was open for 5% of the time, Pallas kernels for 0%

profile of v6, /device:TPU:24, one launch (start us, length us, event | category | flops | bytes accessed | tf_op | source)
XLA Modules:
  0.0 104.9 jit_solution(1442189185198393005)
XLA Ops:
  0.0 1.4 %sqrt_bitcast_fusion = f32[4,256,128]{2,1,0:T(8,128)S(1)} fusion(f32[4,2,256,128]{3,2,1,0:T(8,128)} %param.3), kind=kLoop, calls=%fused_computation.39 | loop fusion | flops 393216 | bytes 1572864 | tf_op jit(solution)/shard_map/sqrt | solution.py:76
  1.4 1.6 %collective-permute-start = (f32[4,64,128]{2,1,0:T(8,128)S(1)}, f32[4,64,128]{2,1,0:T(8,128)S(1)}, u32[]{:S(2)}, u32[]{:S(2)}) collective-permute-start(f32[4,64,128]{2,1,0:T(8,128)S(1)} %slice_select_fusion), channel_id=1, source_target_pairs={{0,2},{2,0},{1,3},{3,1},{4,6},{6,4},{5,7},{7,5},{8,10},{10,8},{9,1... | collective-permute-start | bytes 393224 | tf_op jit(solution)/shard_map/ppermute | solution.py:28
  3.0 1.3 %fusion.43 = (s32[1]{0:T(128)}, s32[1]{0:T(128)}) fusion(s32[2]{0:T(128)} %param.4), kind=kLoop, calls=%fused_computation.90 | loop fusion | bytes 16 | tf_op jit(solution)/shard_map/slice | solution.py:119
  9.3 0.5 fusion.10
  10.5 0.7 fusion.16
  11.6 1.7 %collective-permute-done.1 = bf16[4,2,256,128]{3,0,2,1:T(4,128)(2,1)S(1)} collective-permute-done((bf16[4,2,256,128]{3,0,2,1:T(4,128)(2,1)S(1)}, bf16[4,2,256,128]{3,0,2,1:T(4,128)(2,1)S(1)}, u32[]{:S(2)}, u32[]{:S(2)}) %collective-permute-start.1) | collective-permute-done | bytes 524320 | tf_op jit(solution)/shard_map/ppermute | solution.py:100
  13.3 0.9 maximum_select_fusion
  14.6 1.5 %copy.14 = bf16[8,2,256,64]{2,3,1,0:T(8,128)(2,1)} copy(bf16[8,2,256,64]{3,0,2,1:T(8,128)(2,1)S(1)} %constant_dynamic-slice_fusion.2) | data formatting | bytes 1048576 | tf_op jit(solution)/shard_map/dynamic_slice | solution.py:106
  16.3 1.7 %collective-permute-start.3 = (bf16[8,2,256,64]{2,3,1,0:T(8,128)(2,1)}, bf16[8,2,256,64]{2,3,1,0:T(8,128)(2,1)}, u32[]{:S(2)}, u32[]{:S(2)}) collective-permute-start(bf16[8,2,256,64]{2,3,1,0:T(8,128)(2,1)} %copy.14), channel_id=1, source_target_pairs={{0,8},{4,12},{8,0},{12,4},{1,9},{5,13},{9,1},{13,5},{2,10},{6,14},... | collective-permute-start | bytes 1572872 | tf_op jit(solution)/shard_map/ppermute | solution.py:110
  18.0 0.4 collective-permute-start.2
  19.7 0.6 fusion.32
  20.3 1.1 %slice_bitcast_fusion.1 = (bf16[8,256,128]{2,0,1:T(8,128)(2,1)}, bf16[8,256,128]{2,0,1:T(8,128)(2,1)}) fusion(bf16[8,2,256,128]{3,0,2,1:T(8,128)(2,1)S(1)} %maximum_select_fusion), kind=kLoop, calls=%fused_computation.32 | loop fusion | bytes 2097152 | tf_op jit(solution)/shard_map/squeeze | solution.py:60
  21.4 9.2 %collective-permute-done.4 = bf16[8,2,256,64]{2,3,1,0:T(8,128)(2,1)S(1)} collective-permute-done((bf16[8,2,256,64]{2,3,1,0:T(8,128)(2,1)}, bf16[8,2,256,64]{2,3,1,0:T(8,128)(2,1)S(1)}, u32[]{:S(2)}, u32[]{:S(2)}) %collective-permute-start.4) | collective-permute-done | bytes 524320 | tf_op jit(solution)/shard_map/ppermute | solution.py:110
  30.5 0.6 copy.17
  31.1 32.9 %collective-permute-done.3 = bf16[8,2,256,64]{2,3,1,0:T(8,128)(2,1)} collective-permute-done((bf16[8,2,256,64]{2,3,1,0:T(8,128)(2,1)}, bf16[8,2,256,64]{2,3,1,0:T(8,128)(2,1)}, u32[]{:S(2)}, u32[]{:S(2)}) %collective-permute-start.3) | collective-permute-done | bytes 524320 | tf_op jit(solution)/shard_map/ppermute | solution.py:110
  64.0 1.6 %copy.18 = bf16[8,2,256,64]{3,0,2,1:T(8,128)(2,1)S(1)} copy(bf16[8,2,256,64]{2,3,1,0:T(8,128)(2,1)} %collective-permute-done.3) | data formatting | bytes 1048576 | tf_op jit(solution)/shard_map/ppermute | solution.py:110
  65.6 2.5 %copy.19 = bf16[8,2,256,64]{3,0,2,1:T(8,128)(2,1)} copy(bf16[8,2,256,64]{2,3,1,0:T(8,128)(2,1)} %collective-permute-done.2) | data formatting | bytes 1048576 | tf_op jit(solution)/shard_map/ppermute | solution.py:110
  68.1 2.2 %select_select_fusion.1 = (bf16[8,2,256,64]{3,0,2,1:T(8,128)(2,1)S(1)}, bf16[8,2,256,64]{3,0,2,1:T(8,128)(2,1)S(1)}) fusion(bf16[8,2,256,64]{3,0,2,1:T(8,128)(2,1)} %copy.19, bf16[8,2,256,64]{3,0,2,1:T(8,128)(2,1)S(1)} %copy.18, bf16[8,2,256,64]{3,0,2,1:T(8,128)(2,1)S(1)} %copy.17, pred[]{:T(512)S(6)} %eq.46, pred[]{:T(512)S(6)} %eq.45, pred[]{:T(512)S(6)} %eq.42, ...), kind=kLoop, calls=%fused_computation.27 | loop fusion | flops 1572864 | bytes 3145738 | tf_op jit(solution)/shard_map/jit(_where)/select_n | solution.py:123
  71.4 0.7 copy-done.1
  72.2 8.2 %convolution_convert_fusion = bf16[256,2,128,128]{3,2,1,0:T(8,128)(2,1)} fusion(bf16[8,256,128]{2,0,1:T(8,128)(2,1)S(1)} %copy-done.2, bf16[8,256,128]{2,0,1:T(8,128)(2,1)S(1)} %copy-done.1, bf16[1,16,256,128]{3,1,2,0:T(8,128)(2,1)S(1)} %get-tuple-element.16, bf16[1,16,256,128]{3,1,2,0:T(8,128)(2,1)S(1)} %get-tuple-element.15), kind=kOutput, calls=%fused_computation.2 | convolution fusion | flops 279969792 | bytes 19922944 | tf_op jit(solution)/shard_map/ctfs,tfn->fcsn/dot_general | solution.py:61
  80.4 18.1 %fusion.4 = f32[128,128,128]{2,0,1:T(8,128)S(1)} fusion(bf16[256,2,128,128]{3,2,1,0:T(8,128)(2,1)} %convolution_convert_fusion, f32[128,256,1]{1,0,2:T(8,128)S(1)} %get-tuple-element.24, f32[128,256,1]{1,0,2:T(8,128)S(1)} %get-tuple-element.23), kind=kOutput, calls=%fused_computation.8 | convolution fusion | flops 2147680256 | bytes 25427968 | tf_op jit(solution)/shard_map/dot_general | solution.py:127
  98.5 1.3 %fusion.7 = (bf16[1,128,64,128]{3,1,2,0:T(8,128)(2,1)S(1)}, bf16[1,128,64,128]{3,1,2,0:T(8,128)(2,1)S(1)}) fusion(f32[128,128,128]{2,0,1:T(8,128)S(1)} %fusion.4, f32[64,128]{1,0:T(8,128)S(1)} %get-tuple-element.25, f32[64,128]{1,0:T(8,128)S(1)} %get-tuple-element.26), kind=kLoop, calls=%fused_computation.9 | loop fusion | flops 4194304 | bytes 12648448 | tf_op jit(solution)/shard_map/stack | solution.py:148
  99.8 0.4 pad_maximum_fusion
  100.2 4.7 %copy.25 = bf16[2,128,64,128]{3,2,1,0:T(8,128)(2,1)} copy(bf16[2,128,64,128]{3,1,2,0:T(8,128)(2,1)S(1)} %pad_maximum_fusion) | data formatting | bytes 8388608 | tf_op jit(solution)/shard_map/stack | solution.py:148
  (28 shorter events, 2.8 us)
Async XLA Ops:
  1.4 7.8 %collective-permute-start = (f32[4,64,128]{2,1,0:T(8,128)S(1)}, f32[4,64,128]{2,1,0:T(8,128)S(1)}, u32[]{:S(2)}, u32[]{:S(2)}) collective-permute-start(f32[4,64,128]{2,1,0:T(8,128)S(1)} %slice_select_fusion), channel_id=1, source_target_pairs={{0,2},{2,0},{1,3},{3,1},{4,6},{6,4},{5,7},{7,5},{8,10},{10,8},{9,1... | collective-permute-start | bytes 393224 | tf_op jit(solution)/shard_map/ppermute | solution.py:28
  9.3 1.2 %copy-start = (f32[4,2,256,128]{3,2,1,0:T(8,128)S(1)}, f32[4,2,256,128]{3,2,1,0:T(8,128)}, u32[]{:S(2)}) copy-start(f32[4,2,256,128]{3,2,1,0:T(8,128)} %param.3) | copy-start | bytes 3145732
  9.9 1.5 %copy-start.3 = (s32[4,4]{1,0:T(4,128)S(1)}, s32[4,4]{1,0:T(4,128)}, u32[]{:S(2)}) copy-start(s32[4,4]{1,0:T(4,128)} %param.5) | copy-start | bytes 196
  11.3 2.0 %collective-permute-start.1 = (bf16[4,2,256,128]{3,0,2,1:T(4,128)(2,1)S(1)}, bf16[4,2,256,128]{3,0,2,1:T(4,128)(2,1)S(1)}, u32[]{:S(2)}, u32[]{:S(2)}) collective-permute-start(bf16[4,2,256,128]{3,0,2,1:T(4,128)(2,1)S(1)} %fusion.16), channel_id=1, source_target_pairs={{0,1},{1,0},{2,3},{3,2},{4,5},{5,4},{6,7},{7,6},{8,9},{9,8},{10,11... | collective-permute-start | bytes 1572872 | tf_op jit(solution)/shard_map/ppermute | solution.py:100
  16.1 14.4 %collective-permute-start.4 = (bf16[8,2,256,64]{2,3,1,0:T(8,128)(2,1)}, bf16[8,2,256,64]{2,3,1,0:T(8,128)(2,1)S(1)}, u32[]{:S(2)}, u32[]{:S(2)}) collective-permute-start(bf16[8,2,256,64]{2,3,1,0:T(8,128)(2,1)} %copy.14), channel_id=1, source_target_pairs={{0,4},{4,8},{8,12},{12,0},{1,5},{5,9},{9,13},{13,1},{2,6},{6,10},{... | collective-permute-start | bytes 1572872 | tf_op jit(solution)/shard_map/ppermute | solution.py:110
  16.3 47.7 %collective-permute-start.3 = (bf16[8,2,256,64]{2,3,1,0:T(8,128)(2,1)}, bf16[8,2,256,64]{2,3,1,0:T(8,128)(2,1)}, u32[]{:S(2)}, u32[]{:S(2)}) collective-permute-start(bf16[8,2,256,64]{2,3,1,0:T(8,128)(2,1)} %copy.14), channel_id=1, source_target_pairs={{0,8},{4,12},{8,0},{12,4},{1,9},{5,13},{9,1},{13,5},{2,10},{6,14},... | collective-permute-start | bytes 1572872 | tf_op jit(solution)/shard_map/ppermute | solution.py:110
  18.0 47.6 %collective-permute-start.2 = (bf16[8,2,256,64]{2,3,1,0:T(8,128)(2,1)}, bf16[8,2,256,64]{2,3,1,0:T(8,128)(2,1)}, u32[]{:S(2)}, u32[]{:S(2)}) collective-permute-start(bf16[8,2,256,64]{2,3,1,0:T(8,128)(2,1)} %copy.14), channel_id=1, source_target_pairs={{0,12},{4,0},{8,4},{12,8},{1,13},{5,1},{9,5},{13,9},{2,14},{6,2},{... | collective-permute-start | bytes 1572872 | tf_op jit(solution)/shard_map/ppermute | solution.py:110
  71.0 1.0 copy-start.1
  71.0 1.2 %copy-start.2 = (bf16[8,256,128]{2,0,1:T(8,128)(2,1)S(1)}, bf16[8,256,128]{2,0,1:T(8,128)(2,1)}, u32[]{:S(2)}) copy-start(bf16[8,256,128]{2,0,1:T(8,128)(2,1)} %get-tuple-element.14) | copy-start | bytes 1572868

commit v7 on v5

--- a/solution.py
+++ b/solution.py
@@ -104,10 +104,13 @@
             jnp.concatenate([partner, white], 0),
         )
     own_half = lax.dynamic_slice_in_dim(receivers, seg_position * half_sources, half_sources, 3)
-    shifted = [own_half]
+    split = band_bins // 2
+    gathered = lax.all_gather(own_half[:, :, :split], "sta", axis=0, tiled=False)
+    upper = own_half[:, :, split:]
+    shifted = [upper]
     for shift in range(1, sta_count):
         shifted.append(
-            lax.ppermute(own_half, "sta", [(i, (i + shift) % sta_count) for i in range(sta_count)])
+            lax.ppermute(upper, "sta", [(i, (i + shift) % sta_count) for i in range(sta_count)])
         )
     candidates = jnp.stack(shifted, 0)
     blk_dev = sta_local // SRC
@@ -120,7 +123,13 @@
         block_number = plan[step_number]
         owner_position = block_number // blk_dev
         distance = (sta_position - owner_position) % sta_count
-        held = lax.dynamic_index_in_dim(candidates, distance, 0, keepdims=False)
+        held = jnp.concatenate(
+            [
+                lax.dynamic_index_in_dim(gathered, owner_position, 0, keepdims=False),
+                lax.dynamic_index_in_dim(candidates, distance, 0, keepdims=False),
+            ],
+            2,
+        )
         sources = lax.dynamic_slice_in_dim(
             held, (block_number % blk_dev) * half_sources, half_sources, 3
         )

time: 94.3 us -> 131 us (1.39)
  waiting for transfers between devices: 42.7 us -> 64.7 us
  between operations: 6.33 us -> 20.4 us
  local copies, waits for them, and re-layouts: 12.2 us -> 9.91 us
  other arithmetic: 8.18 us -> 9.6 us
    ppermute x3, waiting for transfers between devices: 41.6 us -> 61.2 us  [local(): lax.ppermute(upper, 'sta', [(i, (i + shift) % sta_count) for i in range(s...]
    ppermute x1, waiting for transfers between devices: 0.01 us -> 3.48 us  [padded(): swapped = lax.ppermute(jnp.where(first, tail, head), axis, [(0, 1), (1, 0)])]
    unnamed x16 -> x18, local copies, waits for them, and re-layouts: 3.81 us -> 1.64 us
  transfers between devices with their start and end apart: 5 -> 6, of which waited for: 3 -> 3; matrix products, arithmetic and copies ran while one was open for 4% -> 3% of each run, Pallas kernels for 0% -> 0%
where the time goes in v7:
time: 131 us
  waiting for transfers between devices  64.7 us (49%)
  between operations  20.4 us (16%)
  matrix products  18 us (14%)
  local copies, waits for them, and re-layouts  9.91 us (8%)
  other arithmetic  9.6 us (7%)
  starting transfers between devices  7.97 us (6%)
    ppermute x3, waiting for transfers between devices, local(): lax.ppermute(upper, 'sta', [(i, (i + shift) % sta_count) for i in range(s...  61.2 us
    dot_general x2, matrix products, local(): lax.dot_general(lag_weights, cross_spectra, (((1, 2), (0, 1)), ((), ())),...  11 us
    dot_general x2, matrix products, cross_terms(): jnp.einsum('ctfs,tfn->fcsn', left_stack, right_stack, preferred_element_t...  6.46 us
    ppermute x3, starting transfers between devices, local(): lax.ppermute(upper, 'sta', [(i, (i + shift) % sta_count) for i in range(s...  4.86 us
    another operation x1, local copies, waits for them, and re-layouts, local(): return jnp.stack(results, 0)  4.71 us
    ppermute x1, waiting for transfers between devices, padded(): swapped = lax.ppermute(jnp.where(first, tail, head), axis, [(0, 1), (1, 0)])  3.48 us
    ppermute x1, starting transfers between devices, padded(): swapped = lax.ppermute(jnp.where(first, tail, head), axis, [(0, 1), (1, 0)])  3.03 us
  transfers between devices with their start and end apart: 6, of which 3 were waited for; matrix products, arithmetic and copies ran while one was open for 3% of the time, Pallas kernels for 0%

profile of v7, /device:TPU:0, one launch (start us, length us, event | category | flops | bytes accessed | tf_op | source)
XLA Modules:
  0.0 130.7 jit_solution(8416425592082281744)
XLA Ops:
  6.5 1.4 %sqrt_bitcast_fusion = f32[4,256,128]{2,1,0:T(8,128)S(1)} fusion(f32[4,2,256,128]{3,2,1,0:T(8,128)} %param.3), kind=kLoop, calls=%fused_computation.52 | loop fusion | flops 393216 | bytes 1572864 | tf_op jit(solution)/shard_map/sqrt | solution.py:76
  7.9 3.0 %collective-permute-start = (f32[4,64,128]{2,1,0:T(8,128)S(1)}, f32[4,64,128]{2,1,0:T(8,128)S(1)}, u32[]{:S(2)}, u32[]{:S(2)}) collective-permute-start(f32[4,64,128]{2,1,0:T(8,128)S(1)} %slice_select_fusion), channel_id=1, source_target_pairs={{0,2},{2,0},{1,3},{3,1},{4,6},{6,4},{5,7},{7,5},{8,10},{10,8},{9,1... | collective-permute-start | bytes 393224 | tf_op jit(solution)/shard_map/ppermute | solution.py:28
  11.0 3.5 %collective-permute-done = f32[4,64,128]{2,1,0:T(8,128)S(1)} collective-permute-done((f32[4,64,128]{2,1,0:T(8,128)S(1)}, f32[4,64,128]{2,1,0:T(8,128)S(1)}, u32[]{:S(2)}, u32[]{:S(2)}) %collective-permute-start) | collective-permute-done | bytes 131104 | tf_op jit(solution)/shard_map/ppermute | solution.py:28
  14.6 0.5 fusion.22
  15.8 0.7 fusion.26
  16.7 0.6 fusion.61
  24.0 1.0 maximum_select_fusion
  25.3 1.0 copy.32
  26.6 0.7 compare_select_fusion.1
  27.3 1.2 fusion.43
  28.5 3.9 %collective-permute-start.4 = (bf16[8,2,128,64]{3,0,2,1:T(8,128)(2,1)S(1)}, bf16[8,2,128,64]{3,0,2,1:T(8,128)(2,1)S(1)}, u32[]{:S(2)}, u32[]{:S(2)}) collective-permute-start(bf16[8,2,128,64]{3,0,2,1:T(8,128)(2,1)S(1)} %get-tuple-element.18), channel_id=1, source_target_pairs={{0,12},{4,0},{8,4},{12,8},{1,13},{5,1},{9,5},{13,9},{2,14},{6,2},{... | collective-permute-start | bytes 786440 | tf_op jit(solution)/shard_map/ppermute | solution.py:113
  32.4 1.0 collective-permute-start.2
  33.4 19.9 %collective-permute-done.4 = bf16[8,2,128,64]{3,0,2,1:T(8,128)(2,1)S(1)} collective-permute-done((bf16[8,2,128,64]{3,0,2,1:T(8,128)(2,1)S(1)}, bf16[8,2,128,64]{3,0,2,1:T(8,128)(2,1)S(1)}, u32[]{:S(2)}, u32[]{:S(2)}) %collective-permute-start.4) | collective-permute-done | bytes 262176 | tf_op jit(solution)/shard_map/ppermute | solution.py:113
  53.3 41.3 %collective-permute-done.3 = bf16[8,2,128,64]{3,0,2,1:T(8,128)(2,1)S(1)} collective-permute-done((bf16[8,2,128,64]{3,0,2,1:T(8,128)(2,1)S(1)}, bf16[8,2,128,64]{3,0,2,1:T(8,128)(2,1)S(1)}, u32[]{:S(2)}, u32[]{:S(2)}) %collective-permute-start.3) | collective-permute-done | bytes 262176 | tf_op jit(solution)/shard_map/ppermute | solution.py:113
  94.6 0.6 pad_maximum_fusion.1
  95.3 1.1 constant_dynamic-slice_fusion.4
  96.8 1.1 fusion.59
  98.6 0.4 copy-done.1
  99.8 1.4 %maximum_bitcast_fusion = (bf16[1,16,256,64]{3,1,0,2:T(8,128)(2,1)S(1)}, bf16[1,16,256,64]{3,1,0,2:T(8,128)(2,1)}) fusion(bf16[8,256,64]{2,0,1:T(8,128)(2,1)S(1)} %fusion.32, bf16[8,256,64]{2,0,1:T(8,128)(2,1)S(1)} %get-tuple-element.8, bf16[8,256,64]{2,0,1:T(8,128)(2,1)S(1)} %get-tuple-element.7), kind=kLoop, calls=%fused_computation.27 | loop fusion | flops 2097152 | bytes 1835008 | tf_op jit(solution)/shard_map/stack | solution.py:57
  101.1 2.8 %convolution_convert_fusion = bf16[256,2,64,128]{3,2,1,0:T(8,128)(2,1)S(1)} fusion(bf16[1,16,256,64]{3,1,0,2:T(8,128)(2,1)S(1)} %get-tuple-element.22, bf16[1,16,256,64]{3,1,0,2:T(8,128)(2,1)S(1)} %get-tuple-element.21, bf16[8,256,128]{2,0,1:T(8,128)(2,1)S(1)} %get-tuple-element.16, bf16[8,256,128]{2,0,1:T(8,128)(2,1)S(1)} %get-tuple-element.15), kind=kOutput, calls=%fused_computation.4 | convolution fusion | flops 141033472 | bytes 10485760 | tf_op jit(solution)/shard_map/ctfs,tfn->fcsn/dot_general | solution.py:61
  104.0 3.6 %convolution_convert_fusion.1 = bf16[256,2,64,128]{3,2,1,0:T(8,128)(2,1)S(1)} fusion(bf16[1,16,256,64]{3,1,0,2:T(8,128)(2,1)} %get-tuple-element.20, bf16[1,16,256,64]{3,1,0,2:T(8,128)(2,1)S(1)} %get-tuple-element.19, bf16[8,256,128]{2,0,1:T(8,128)(2,1)S(1)} %get-tuple-element.16, bf16[8,256,128]{2,0,1:T(8,128)(2,1)S(1)} %get-tuple-element.15), kind=kOutput, calls=%fused_computation.5 | convolution fusion | flops 141033472 | bytes 10485760 | tf_op jit(solution)/shard_map/ctfs,tfn->fcsn/dot_general | solution.py:61
  107.7 5.4 %fusion.19 = bf16[1,128,64,128]{3,1,2,0:T(8,128)(2,1)S(1)} fusion(f32[64,128]{1,0:T(8,128)S(1)} %copy-done.5, bf16[256,2,64,128]{3,2,1,0:T(8,128)(2,1)S(1)} %convolution_convert_fusion, f32[128,256,1]{1,0,2:T(8,128)S(1)} %copy-done.3, f32[128,256,1]{1,0,2:T(8,128)S(1)} %get-tuple-element.29), kind=kOutput, calls=%fused_computation.19 | convolution fusion | flops 1076035584 | bytes 10780672 | tf_op jit(solution)/shard_map/dot_general | solution.py:137
  113.1 5.6 %fusion.16 = bf16[1,128,64,128]{3,1,2,0:T(8,128)(2,1)S(1)} fusion(f32[64,128]{1,0:T(8,128)S(1)} %copy-done.4, bf16[256,2,64,128]{3,2,1,0:T(8,128)(2,1)S(1)} %convolution_convert_fusion.1, f32[128,256,1]{1,0,2:T(8,128)S(1)} %copy-done.3, f32[128,256,1]{1,0,2:T(8,128)S(1)} %get-tuple-element.29), kind=kOutput, calls=%fused_computation.18 | convolution fusion | flops 1076035584 | bytes 10780672 | tf_op jit(solution)/shard_map/dot_general | solution.py:137
  119.1 4.7 %copy.43 = bf16[2,128,64,128]{3,2,1,0:T(8,128)(2,1)} copy(bf16[2,128,64,128]{3,1,2,0:T(8,128)(2,1)S(1)} %pad_maximum_fusion) | data formatting | bytes 8388608 | tf_op jit(solution)/shard_map/stack | solution.py:154
  (44 shorter events, 3.7 us)
Async XLA Ops:
  6.5 88.8 %all-gather.3.cloned.1.call-start = ((), (), s32[]{:S(2)}) async-start(), calls=%async_computation | async-start | bytes 1310720 | tf_op jit(solution)/shard_map/all_gather | solution.py:108
  7.9 6.5 %collective-permute-start = (f32[4,64,128]{2,1,0:T(8,128)S(1)}, f32[4,64,128]{2,1,0:T(8,128)S(1)}, u32[]{:S(2)}, u32[]{:S(2)}) collective-permute-start(f32[4,64,128]{2,1,0:T(8,128)S(1)} %slice_select_fusion), channel_id=1, source_target_pairs={{0,2},{2,0},{1,3},{3,1},{4,6},{6,4},{5,7},{7,5},{8,10},{10,8},{9,1... | collective-permute-start | bytes 393224 | tf_op jit(solution)/shard_map/ppermute | solution.py:28
  14.6 1.2 copy-start
  15.1 1.5 %copy-start.6 = (s32[2]{0:T(128)S(1)}, s32[2]{0:T(128)}, u32[]{:S(2)}) copy-start(s32[2]{0:T(128)} %param.4) | copy-start | bytes 28
  16.6 7.4 %collective-permute-start.1 = (bf16[4,2,256,128]{3,0,2,1:T(4,128)(2,1)S(1)}, bf16[4,2,256,128]{3,0,2,1:T(4,128)(2,1)S(1)}, u32[]{:S(2)}, u32[]{:S(2)}) collective-permute-start(bf16[4,2,256,128]{3,0,2,1:T(4,128)(2,1)S(1)} %fusion.26), channel_id=1, source_target_pairs={{0,1},{1,0},{2,3},{3,2},{4,5},{5,4},{6,7},{7,6},{8,9},{9,8},{10,11... | collective-permute-start | bytes 1572872 | tf_op jit(solution)/shard_map/ppermute | solution.py:100
  24.9 1.5 %copy-start.7 = (s32[4,4]{1,0:T(4,128)S(1)}, s32[4,4]{1,0:T(4,128)}, u32[]{:S(2)}) copy-start(s32[4,4]{1,0:T(4,128)} %param.5) | copy-start | bytes 196
  28.5 24.8 %collective-permute-start.4 = (bf16[8,2,128,64]{3,0,2,1:T(8,128)(2,1)S(1)}, bf16[8,2,128,64]{3,0,2,1:T(8,128)(2,1)S(1)}, u32[]{:S(2)}, u32[]{:S(2)}) collective-permute-start(bf16[8,2,128,64]{3,0,2,1:T(8,128)(2,1)S(1)} %get-tuple-element.18), channel_id=1, source_target_pairs={{0,12},{4,0},{8,4},{12,8},{1,13},{5,1},{9,5},{13,9},{2,14},{6,2},{... | collective-permute-start | bytes 786440 | tf_op jit(solution)/shard_map/ppermute | solution.py:113
  32.4 62.3 %collective-permute-start.3 = (bf16[8,2,128,64]{3,0,2,1:T(8,128)(2,1)S(1)}, bf16[8,2,128,64]{3,0,2,1:T(8,128)(2,1)S(1)}, u32[]{:S(2)}, u32[]{:S(2)}) collective-permute-start(bf16[8,2,128,64]{3,0,2,1:T(8,128)(2,1)S(1)} %get-tuple-element.18), channel_id=1, source_target_pairs={{0,8},{4,12},{8,0},{12,4},{1,9},{5,13},{9,1},{13,5},{2,10},{6,14},... | collective-permute-start | bytes 786440 | tf_op jit(solution)/shard_map/ppermute | solution.py:113
  32.4 62.3 %collective-permute-start.2 = (bf16[8,2,128,64]{3,0,2,1:T(8,128)(2,1)S(1)}, bf16[8,2,128,64]{3,0,2,1:T(8,128)(2,1)S(1)}, u32[]{:S(2)}, u32[]{:S(2)}) collective-permute-start(bf16[8,2,128,64]{3,0,2,1:T(8,128)(2,1)S(1)} %get-tuple-element.18), channel_id=1, source_target_pairs={{0,4},{4,8},{8,12},{12,0},{1,5},{5,9},{9,13},{13,1},{2,6},{6,10},{... | collective-permute-start | bytes 786440 | tf_op jit(solution)/shard_map/ppermute | solution.py:113
  98.0 1.0 copy-start.1
  98.3 1.1 copy-start.2
  103.9 3.7 %copy-start.3 = (f32[128,256,1]{1,0,2:T(8,128)S(1)}, f32[128,256,1]{1,0,2:T(8,128)}, u32[]{:S(2)}) copy-start(f32[128,256,1]{1,0,2:T(8,128)} %get-tuple-element.30) | copy-start | bytes 393220
  104.0 3.7 %copy-start.5 = (f32[64,128]{1,0:T(8,128)S(1)}, f32[64,128]{1,0:T(8,128)}, u32[]{:S(2)}) copy-start(f32[64,128]{1,0:T(8,128)} %get-tuple-element.32) | copy-start | bytes 98308
  107.6 5.4 %copy-start.4 = (f32[64,128]{1,0:T(8,128)S(1)}, f32[64,128]{1,0:T(8,128)}, u32[]{:S(2)}) copy-start(f32[64,128]{1,0:T(8,128)} %get-tuple-element.31) | copy-start | bytes 98308
Sparse Core Ops, SparseCore 0:
  26.5 61.0 all-gather.2

commit v8 on v5

--- a/solution.py
+++ b/solution.py
@@ -5,10 +5,10 @@
 from jax import lax
 from jax.sharding import PartitionSpec as P
 
+
 SEGS = 8
 STEPS = 2
 SRC = 128
-BLK_DEV = 1
 BAND_BINS = 256
 HALF = 64
 LAGS = 128
@@ -34,11 +34,6 @@
             upper = lax.ppermute(head, axis, [((i + 1) % count, i) for i in range(ends)])
         cells = jnp.concatenate([lower, cells, upper], axis=dim)
     return cells
-
-
-def from_root(block, axis, source):
-    block = jnp.where(lax.axis_index(axis) == source, block, jnp.zeros_like(block))
-    return lax.psum(block, axis)
 
 
 def lag_table(first_bin):
@@ -74,42 +69,89 @@
     total_bins = band_bins * lax.axis_size("band")
     half_sources = SRC // lax.axis_size("seg")
     amplitude = jnp.sqrt(spectra[:, 0] ** 2 + spectra[:, 1] ** 2)
-    extended = padded(amplitude, (("band", 1),), HALF)
-    block_width = 2 * HALF
-    block_count = band_bins // block_width
-    lower_part = extended[:, : block_count * block_width].reshape(
-        seg_local, block_count, block_width, sta_local
-    )
-    upper_part = extended[:, block_width:].reshape(seg_local, block_count, block_width, sta_local)
-    windows = jnp.concatenate([lower_part, upper_part], axis=2)
-    offsets = jnp.arange(2 * block_width, dtype=jnp.int32)[:, None]
-    targets = jnp.arange(block_width, dtype=jnp.int32)[None, :]
-    band_matrix = ((offsets >= targets) & (offsets <= targets + 2 * HALF)).astype(jnp.float32)
-    window_sums = jnp.einsum("tbgn,gf->tbfn", windows, band_matrix, precision=lax.Precision.HIGHEST)
-    window_sums = window_sums.reshape(seg_local, band_bins, sta_local)
+    seg_count = lax.axis_size("seg")
+    sta_count = lax.axis_size("sta")
     bin_number = band_position * band_bins + jnp.arange(band_bins, dtype=jnp.int32)
     in_range = (
         jnp.minimum(bin_number + HALF, total_bins - 1) - jnp.maximum(bin_number - HALF, 0) + 1
     ).astype(jnp.float32)
-    smooth = window_sums / in_range[None, :, None]
-    white = (spectra / (smooth[:, None] + EPSILON)).astype(jnp.bfloat16)
-    seg_count = lax.axis_size("seg")
-    sta_count = lax.axis_size("sta")
-    receivers = lax.all_gather(white, "seg", axis=0, tiled=True) if seg_count > 2 else None
-    if receivers is None:
+
+    def whiten_from(extended, spectra):
+        block_width = 2 * HALF
+        block_count = band_bins // block_width
+        lower_part = extended[:, : block_count * block_width].reshape(
+            seg_local, block_count, block_width, sta_local
+        )
+        upper_part = extended[:, block_width:].reshape(
+            seg_local, block_count, block_width, sta_local
+        )
+        windows = jnp.concatenate([lower_part, upper_part], axis=2)
+        offsets = jnp.arange(2 * block_width, dtype=jnp.int32)[:, None]
+        targets = jnp.arange(block_width, dtype=jnp.int32)[None, :]
+        band_matrix = ((offsets >= targets) & (offsets <= targets + 2 * HALF)).astype(jnp.float32)
+        window_sums = jnp.einsum(
+            "tbgn,gf->tbfn", windows, band_matrix, precision=lax.Precision.HIGHEST
+        )
+        window_sums = window_sums.reshape(seg_local, band_bins, sta_local)
+        smooth = window_sums / in_range[None, :, None]
+        return (spectra / (smooth[:, None] + EPSILON)).astype(jnp.bfloat16)
+
+    def spread(white):
         partner = lax.ppermute(white, "seg", [(0, 1), (1, 0)])
         receivers = jnp.where(
             seg_position == 0,
             jnp.concatenate([white, partner], 0),
             jnp.concatenate([partner, white], 0),
         )
-    own_half = lax.dynamic_slice_in_dim(receivers, seg_position * half_sources, half_sources, 3)
-    shifted = [own_half]
-    for shift in range(1, sta_count):
-        shifted.append(
-            lax.ppermute(own_half, "sta", [(i, (i + shift) % sta_count) for i in range(sta_count)])
+        own_half = lax.dynamic_slice_in_dim(
+            receivers, seg_position * half_sources, half_sources, 3
         )
-    candidates = jnp.stack(shifted, 0)
+        shifted = [own_half]
+        for shift in range(1, sta_count):
+            shifted.append(
+                lax.ppermute(
+                    own_half, "sta", [(i, (i + shift) % sta_count) for i in range(sta_count)]
+                )
+            )
+        return receivers, jnp.stack(shifted, 0)
+
+    split_bins = seg_count == 2 and band_bins == 4 * HALF
+    if split_bins:
+        rim = jnp.zeros((seg_local, HALF, sta_local), amplitude.dtype)
+        inner_amplitude, inner_spectra = lax.optimization_barrier((amplitude, spectra))
+        inner = whiten_from(jnp.concatenate([rim, inner_amplitude, rim], 1), inner_spectra)
+        inner = lax.optimization_barrier(inner[:, :, HALF:-HALF])
+        halo_amplitude, _ = lax.optimization_barrier((amplitude, inner))
+        extended = padded(halo_amplitude, (("band", 1),), HALF)
+        outer = whiten_from(extended, spectra)
+        outer = jnp.concatenate([outer[:, :, :HALF], outer[:, :, -HALF:]], 2)
+        inner_receivers, inner_candidates = spread(inner)
+        outer_receivers, outer_candidates = spread(outer)
+
+        def by_bins(inner_part, outer_part):
+            return jnp.concatenate(
+                [outer_part[..., :HALF, :], inner_part, outer_part[..., HALF:, :]], -2
+            )
+
+        receivers = by_bins(inner_receivers, outer_receivers)
+        candidates = by_bins(inner_candidates, outer_candidates)
+    else:
+        white = whiten_from(padded(amplitude, (("band", 1),), HALF), spectra)
+        if seg_count == 2:
+            receivers, candidates = spread(white)
+        else:
+            receivers = lax.all_gather(white, "seg", axis=0, tiled=True)
+            own_half = lax.dynamic_slice_in_dim(
+                receivers, seg_position * half_sources, half_sources, 3
+            )
+            shifted = [own_half]
+            for shift in range(1, sta_count):
+                shifted.append(
+                    lax.ppermute(
+                        own_half, "sta", [(i, (i + shift) % sta_count) for i in range(sta_count)]
+                    )
+                )
+            candidates = jnp.stack(shifted, 0)
     blk_dev = sta_local // SRC
     lag_weights = lag_table(band_position * band_bins).reshape(LAGS, band_bins, 2)
     receiver_ids = sta_position * sta_local + jnp.arange(sta_local, dtype=jnp.int32)

time: 94.3 us -> 138 us (1.46)
  starting transfers between devices: 7.77 us -> 57.4 us
  waiting for transfers between devices: 42.7 us -> 38.5 us
  local copies, waits for them, and re-layouts: 12.2 us -> 8.94 us
  matrix products: 16.8 us -> 18.4 us
    ppermute x4 -> x8, starting transfers between devices: 4.74 us -> 54.8 us  [the longest x6 54 us: spread(): lax.ppermute(own_half, 'sta', [(i, (i + shift) % sta_count) for i in rang...]
    ppermute x4 -> x8, waiting for transfers between devices: 42.7 us -> 38.5 us  [the longest x6 38.5 us: spread(): lax.ppermute(own_half, 'sta', [(i, (i + shift) % sta_count) for i in rang...]
    unnamed x16 -> x7, local copies, waits for them, and re-layouts: 3.81 us -> 0.26 us
    dot_general x1 -> x2, matrix products: 0.53 us -> 2.1 us  [whiten_from(): jnp.einsum('tbgn,gf->tbfn', windows, band_matrix, precision=lax.Precision...]
    concatenate x0 -> x3, other arithmetic: none -> 1.5 us  [the longest x2 1.33 us: by_bins(): jnp.concatenate([outer_part[..., :HALF, :], inner_part, outer_part[..., H...]
  transfers between devices with their start and end apart: 5 -> 9, of which waited for: 3 -> 2; matrix products, arithmetic and copies ran while one was open for 4% -> 5% of each run, Pallas kernels for 0% -> 0%
where the time goes in v8:
time: 138 us
  starting transfers between devices  57.4 us (42%)
  waiting for transfers between devices  38.5 us (28%)
  matrix products  18.4 us (13%)
  local copies, waits for them, and re-layouts  8.94 us (6%)
  other arithmetic  7.84 us (6%)
  between operations  7.13 us (5%)
    ppermute x6, starting transfers between devices, spread(): lax.ppermute(own_half, 'sta', [(i, (i + shift) % sta_count) for i in rang...  54 us
    ppermute x6, waiting for transfers between devices, spread(): lax.ppermute(own_half, 'sta', [(i, (i + shift) % sta_count) for i in rang...  38.5 us
    dot_general x2, matrix products, local(): lax.dot_general(lag_weights, cross_spectra, (((1, 2), (0, 1)), ((), ())),...  10.8 us
    dot_general x2, matrix products, cross_terms(): jnp.einsum('ctfs,tfn->fcsn', left_stack, right_stack, preferred_element_t...  5.52 us
    another operation x1, local copies, waits for them, and re-layouts, local(): return jnp.stack(results, 0)  4.71 us
  transfers between devices with their start and end apart: 9, of which 2 were waited for; matrix products, arithmetic and copies ran while one was open for 5% of the time, Pallas kernels for 0%

profile of v8, /device:TPU:0, one launch (start us, length us, event | category | flops | bytes accessed | tf_op | source)
XLA Modules:
  0.0 138.2 jit_solution(2608330854595455623)
XLA Ops:
  0.0 1.5 %sqrt_bitcast_fusion = f32[4,256,128]{2,1,0:T(8,128)S(1)} fusion(f32[4,2,256,128]{3,2,1,0:T(8,128)} %param.3), kind=kLoop, calls=%fused_computation.56 | loop fusion | flops 393216 | bytes 1572864 | tf_op jit(solution)/shard_map/sqrt | solution.py:71
  1.5 0.7 copy.17
  2.2 0.9 pad_slice_fusion.1
  3.1 1.6 %fusion.22 = f32[128,4,2,128]{3,0,2,1:T(8,128)S(1)} fusion(f32[4,2,128,128]{3,2,1,0:T(8,128)} %bitcast.105, f32[4,2,128,128]{3,2,1,0:T(8,128)S(1)} %bitcast.104, s32[128]{0:T(128)S(1)} %iota_add_fusion.4), kind=kOutput, calls=%fused_computation.21 | convolution fusion | flops 403013632 | bytes 1573376 | tf_op jit(solution)/shard_map/tbgn,gf->tbfn/dot_general | solution.py:92
  5.2 0.6 collective-permute-start.5
  5.7 2.6 %collective-permute-start = (f32[4,64,128]{2,1,0:T(8,128)S(1)}, f32[4,64,128]{2,1,0:T(8,128)S(1)}, u32[]{:S(2)}, u32[]{:S(2)}) collective-permute-start(f32[4,64,128]{2,1,0:T(8,128)S(1)} %slice_select_fusion), channel_id=1, source_target_pairs={{0,2},{2,0},{1,3},{3,1},{4,6},{6,4},{5,7},{7,5},{8,10},{10,8},{9,1... | collective-permute-start | bytes 393224 | tf_op jit(solution)/shard_map/ppermute | solution.py:28
  8.3 0.6 fusion.65
  15.7 0.6 fusion.45
  16.6 0.5 fusion.26
  17.7 0.8 fusion.30
  19.7 3.7 %collective-permute-start.8 = (bf16[8,2,128,64]{3,0,2,1:T(8,128)(2,1)S(1)}, bf16[8,2,128,64]{3,0,2,1:T(8,128)(2,1)S(1)}, u32[]{:S(2)}, u32[]{:S(2)}) collective-permute-start(bf16[8,2,128,64]{3,0,2,1:T(8,128)(2,1)S(1)} %constant_dynamic-slice_fusion.2), channel_id=1, source_target_pairs={{0,12},{4,0},{8,4},{12,8},{1,13},{5,1},{9,5},{13,9},{2,14},{6,2},{... | collective-permute-start | bytes 786440 | tf_op jit(solution)/shard_map/ppermute | solution.py:112
  24.3 0.8 collective-permute-start.4
  25.1 2.2 %collective-permute-start.3 = (bf16[8,2,128,64]{3,0,2,1:T(8,128)(2,1)S(1)}, bf16[8,2,128,64]{3,0,2,1:T(8,128)(2,1)S(1)}, u32[]{:S(2)}, u32[]{:S(2)}) collective-permute-start(bf16[8,2,128,64]{3,0,2,1:T(8,128)(2,1)S(1)} %constant_dynamic-slice_fusion.3), channel_id=1, source_target_pairs={{0,8},{4,12},{8,0},{12,4},{1,9},{5,13},{9,1},{13,5},{2,10},{6,14},... | collective-permute-start | bytes 786440 | tf_op jit(solution)/shard_map/ppermute | solution.py:112
  27.3 1.9 %collective-permute-start.2 = (bf16[8,2,128,64]{3,0,2,1:T(8,128)(2,1)S(1)}, bf16[8,2,128,64]{3,0,2,1:T(8,128)(2,1)S(1)}, u32[]{:S(2)}, u32[]{:S(2)}) collective-permute-start(bf16[8,2,128,64]{3,0,2,1:T(8,128)(2,1)S(1)} %constant_dynamic-slice_fusion.3), channel_id=1, source_target_pairs={{0,4},{4,8},{8,12},{12,0},{1,5},{5,9},{9,13},{13,1},{2,6},{6,10},{... | collective-permute-start | bytes 786440 | tf_op jit(solution)/shard_map/ppermute | solution.py:112
  29.7 28.5 %collective-permute-done.4 = bf16[8,2,128,64]{3,0,2,1:T(8,128)(2,1)S(1)} collective-permute-done((bf16[8,2,128,64]{3,0,2,1:T(8,128)(2,1)S(1)}, bf16[8,2,128,64]{3,0,2,1:T(8,128)(2,1)S(1)}, u32[]{:S(2)}, u32[]{:S(2)}) %collective-permute-start.4) | collective-permute-done | bytes 262176 | tf_op jit(solution)/shard_map/ppermute | solution.py:112
  58.2 45.3 %collective-permute-start.6 = (bf16[8,2,128,64]{3,0,2,1:T(8,128)(2,1)S(1)}, bf16[8,2,128,64]{3,0,2,1:T(8,128)(2,1)S(1)}, u32[]{:S(2)}, u32[]{:S(2)}) collective-permute-start(bf16[8,2,128,64]{3,0,2,1:T(8,128)(2,1)S(1)} %constant_dynamic-slice_fusion.2), channel_id=1, source_target_pairs={{0,4},{4,8},{8,12},{12,0},{1,5},{5,9},{9,13},{13,1},{2,6},{6,10},{... | collective-permute-start | bytes 786440 | tf_op jit(solution)/shard_map/ppermute | solution.py:112
  103.5 10.0 %collective-permute-done.3 = bf16[8,2,128,64]{3,0,2,1:T(8,128)(2,1)S(1)} collective-permute-done((bf16[8,2,128,64]{3,0,2,1:T(8,128)(2,1)S(1)}, bf16[8,2,128,64]{3,0,2,1:T(8,128)(2,1)S(1)}, u32[]{:S(2)}, u32[]{:S(2)}) %collective-permute-start.3) | collective-permute-done | bytes 262176 | tf_op jit(solution)/shard_map/ppermute | solution.py:112
  113.5 0.5 pad_maximum_fusion.2
  114.3 1.2 pad_maximum_fusion
  116.7 2.6 %convolution_convert_fusion = bf16[256,2,64,128]{3,2,1,0:T(8,128)(2,1)S(1)} fusion(bf16[1,16,256,64]{3,1,0,2:T(8,128)(2,1)S(1)} %get-tuple-element.28, bf16[1,16,256,64]{3,1,0,2:T(8,128)(2,1)S(1)} %get-tuple-element.27, bf16[8,256,128]{2,0,1:T(8,128)(2,1)S(1)} %get-tuple-element.20, bf16[8,256,128]{2,0,1:T(8,128)(2,1)S(1)} %get-tuple-element.19), kind=kOutput, calls=%fused_computation.4 | convolution fusion | flops 141033472 | bytes 10485760 | tf_op jit(solution)/shard_map/ctfs,tfn->fcsn/dot_general | solution.py:56
  119.4 2.9 %convolution_convert_fusion.1 = bf16[256,2,64,128]{3,2,1,0:T(8,128)(2,1)S(1)} fusion(bf16[1,16,256,64]{3,1,0,2:T(8,128)(2,1)S(1)} %get-tuple-element.24, bf16[1,16,256,64]{3,1,0,2:T(8,128)(2,1)S(1)} %get-tuple-element.23, bf16[8,256,128]{2,0,1:T(8,128)(2,1)S(1)} %get-tuple-element.20, bf16[8,256,128]{2,0,1:T(8,128)(2,1)S(1)} %get-tuple-element.19), kind=kOutput, calls=%fused_computation.5 | convolution fusion | flops 141033472 | bytes 10485760 | tf_op jit(solution)/shard_map/ctfs,tfn->fcsn/dot_general | solution.py:56
  122.3 5.4 %fusion.19 = bf16[1,128,64,128]{3,1,2,0:T(8,128)(2,1)S(1)} fusion(f32[64,128]{1,0:T(8,128)S(1)} %get-tuple-element.42, bf16[256,2,64,128]{3,2,1,0:T(8,128)(2,1)S(1)} %convolution_convert_fusion, f32[128,256,1]{1,0,2:T(8,128)S(1)} %get-tuple-element.40, f32[128,256,1]{1,0,2:T(8,128)S(1)} %get-tuple-element.39), kind=kOutput, calls=%fused_computation.20 | convolution fusion | flops 1076035584 | bytes 10780672 | tf_op jit(solution)/shard_map/dot_general | solution.py:170
  127.7 5.4 %fusion.16 = bf16[1,128,64,128]{3,1,2,0:T(8,128)(2,1)S(1)} fusion(f32[64,128]{1,0:T(8,128)S(1)} %get-tuple-element.41, bf16[256,2,64,128]{3,2,1,0:T(8,128)(2,1)S(1)} %convolution_convert_fusion.1, f32[128,256,1]{1,0,2:T(8,128)S(1)} %get-tuple-element.40, f32[128,256,1]{1,0,2:T(8,128)S(1)} %get-tuple-element.39), kind=kOutput, calls=%fused_computation.19 | convolution fusion | flops 1076035584 | bytes 10780672 | tf_op jit(solution)/shard_map/dot_general | solution.py:170
  133.5 4.7 %copy.30 = bf16[2,128,64,128]{3,2,1,0:T(8,128)(2,1)} copy(bf16[2,128,64,128]{3,1,2,0:T(8,128)(2,1)S(1)} %pad_maximum_fusion.1) | data formatting | bytes 8388608 | tf_op jit(solution)/shard_map/stack | solution.py:187
  (51 shorter events, 5.6 us)
Async XLA Ops:
  0.0 1.5 %copy-start = (f32[4,2,256,128]{3,2,1,0:T(8,128)S(1)}, f32[4,2,256,128]{3,2,1,0:T(8,128)}, u32[]{:S(2)}) copy-start(f32[4,2,256,128]{3,2,1,0:T(8,128)} %param.3) | copy-start | bytes 3145732
  4.7 3.6 %copy-start.1 = (s32[2]{0:T(128)S(1)}, s32[2]{0:T(128)}, u32[]{:S(2)}) copy-start(s32[2]{0:T(128)} %param.4) | copy-start | bytes 28
  4.7 11.6 %copy-start.2 = (s32[4,4]{1,0:T(4,128)S(1)}, s32[4,4]{1,0:T(4,128)}, u32[]{:S(2)}) copy-start(s32[4,4]{1,0:T(4,128)} %param.5) | copy-start | bytes 196
  5.2 13.8 %collective-permute-start.5 = (bf16[4,2,128,128]{3,0,2,1:T(4,128)(2,1)S(1)}, bf16[4,2,128,128]{3,0,2,1:T(4,128)(2,1)S(1)}, u32[]{:S(2)}, u32[]{:S(2)}) collective-permute-start(bf16[4,2,128,128]{3,0,2,1:T(4,128)(2,1)S(1)} %fusion.33), channel_id=1, source_target_pairs={{0,1},{1,0},{2,3},{3,2},{4,5},{5,4},{6,7},{7,6},{8,9},{9,8},{10,11... | collective-permute-start | bytes 786440 | tf_op jit(solution)/shard_map/ppermute | solution.py:100
  5.7 10.8 %collective-permute-start = (f32[4,64,128]{2,1,0:T(8,128)S(1)}, f32[4,64,128]{2,1,0:T(8,128)S(1)}, u32[]{:S(2)}, u32[]{:S(2)}) collective-permute-start(f32[4,64,128]{2,1,0:T(8,128)S(1)} %slice_select_fusion), channel_id=1, source_target_pairs={{0,2},{2,0},{1,3},{3,1},{4,6},{6,4},{5,7},{7,5},{8,10},{10,8},{9,1... | collective-permute-start | bytes 393224 | tf_op jit(solution)/shard_map/ppermute | solution.py:28
  18.7 4.8 %collective-permute-start.1 = (bf16[4,2,128,128]{3,0,2,1:T(4,128)(2,1)S(1)}, bf16[4,2,128,128]{3,0,2,1:T(4,128)(2,1)S(1)}, u32[]{:S(2)}, u32[]{:S(2)}) collective-permute-start(bf16[4,2,128,128]{3,0,2,1:T(4,128)(2,1)S(1)} %pad_maximum_fusion.6), channel_id=1, source_target_pairs={{0,1},{1,0},{2,3},{3,2},{4,5},{5,4},{6,7},{7,6},{8,9},{9,8},{10,11... | collective-permute-start | bytes 786440 | tf_op jit(solution)/shard_map/ppermute | solution.py:100
  19.7 94.6 %collective-permute-start.8 = (bf16[8,2,128,64]{3,0,2,1:T(8,128)(2,1)S(1)}, bf16[8,2,128,64]{3,0,2,1:T(8,128)(2,1)S(1)}, u32[]{:S(2)}, u32[]{:S(2)}) collective-permute-start(bf16[8,2,128,64]{3,0,2,1:T(8,128)(2,1)S(1)} %constant_dynamic-slice_fusion.2), channel_id=1, source_target_pairs={{0,12},{4,0},{8,4},{12,8},{1,13},{5,1},{9,5},{13,9},{2,14},{6,2},{... | collective-permute-start | bytes 786440 | tf_op jit(solution)/shard_map/ppermute | solution.py:112
  23.3 90.9 %collective-permute-start.7 = (bf16[8,2,128,64]{3,0,2,1:T(8,128)(2,1)S(1)}, bf16[8,2,128,64]{3,0,2,1:T(8,128)(2,1)S(1)}, u32[]{:S(2)}, u32[]{:S(2)}) collective-permute-start(bf16[8,2,128,64]{3,0,2,1:T(8,128)(2,1)S(1)} %constant_dynamic-slice_fusion.2), channel_id=1, source_target_pairs={{0,8},{4,12},{8,0},{12,4},{1,9},{5,13},{9,1},{13,5},{2,10},{6,14},... | collective-permute-start | bytes 786440 | tf_op jit(solution)/shard_map/ppermute | solution.py:112
  24.3 33.9 %collective-permute-start.4 = (bf16[8,2,128,64]{3,0,2,1:T(8,128)(2,1)S(1)}, bf16[8,2,128,64]{3,0,2,1:T(8,128)(2,1)S(1)}, u32[]{:S(2)}, u32[]{:S(2)}) collective-permute-start(bf16[8,2,128,64]{3,0,2,1:T(8,128)(2,1)S(1)} %constant_dynamic-slice_fusion.3), channel_id=1, source_target_pairs={{0,12},{4,0},{8,4},{12,8},{1,13},{5,1},{9,5},{13,9},{2,14},{6,2},{... | collective-permute-start | bytes 786440 | tf_op jit(solution)/shard_map/ppermute | solution.py:112
  25.1 88.4 %collective-permute-start.3 = (bf16[8,2,128,64]{3,0,2,1:T(8,128)(2,1)S(1)}, bf16[8,2,128,64]{3,0,2,1:T(8,128)(2,1)S(1)}, u32[]{:S(2)}, u32[]{:S(2)}) collective-permute-start(bf16[8,2,128,64]{3,0,2,1:T(8,128)(2,1)S(1)} %constant_dynamic-slice_fusion.3), channel_id=1, source_target_pairs={{0,8},{4,12},{8,0},{12,4},{1,9},{5,13},{9,1},{13,5},{2,10},{6,14},... | collective-permute-start | bytes 786440 | tf_op jit(solution)/shard_map/ppermute | solution.py:112
  27.3 86.2 %collective-permute-start.2 = (bf16[8,2,128,64]{3,0,2,1:T(8,128)(2,1)S(1)}, bf16[8,2,128,64]{3,0,2,1:T(8,128)(2,1)S(1)}, u32[]{:S(2)}, u32[]{:S(2)}) collective-permute-start(bf16[8,2,128,64]{3,0,2,1:T(8,128)(2,1)S(1)} %constant_dynamic-slice_fusion.3), channel_id=1, source_target_pairs={{0,4},{4,8},{8,12},{12,0},{1,5},{5,9},{9,13},{13,1},{2,6},{6,10},{... | collective-permute-start | bytes 786440 | tf_op jit(solution)/shard_map/ppermute | solution.py:112
  58.2 56.0 %collective-permute-start.6 = (bf16[8,2,128,64]{3,0,2,1:T(8,128)(2,1)S(1)}, bf16[8,2,128,64]{3,0,2,1:T(8,128)(2,1)S(1)}, u32[]{:S(2)}, u32[]{:S(2)}) collective-permute-start(bf16[8,2,128,64]{3,0,2,1:T(8,128)(2,1)S(1)} %constant_dynamic-slice_fusion.2), channel_id=1, source_target_pairs={{0,4},{4,8},{8,12},{12,0},{1,5},{5,9},{9,13},{13,1},{2,6},{6,10},{... | collective-permute-start | bytes 786440 | tf_op jit(solution)/shard_map/ppermute | solution.py:112

commit v9 on v5

--- a/solution.py
+++ b/solution.py
@@ -104,12 +104,8 @@
             jnp.concatenate([partner, white], 0),
         )
     own_half = lax.dynamic_slice_in_dim(receivers, seg_position * half_sources, half_sources, 3)
-    shifted = [own_half]
-    for shift in range(1, sta_count):
-        shifted.append(
-            lax.ppermute(own_half, "sta", [(i, (i + shift) % sta_count) for i in range(sta_count)])
-        )
-    candidates = jnp.stack(shifted, 0)
+    copies = jnp.broadcast_to(own_half[None], (sta_count,) + own_half.shape)
+    candidates = lax.all_to_all(copies, "sta", 0, 0, tiled=True)
     blk_dev = sta_local // SRC
     lag_weights = lag_table(band_position * band_bins).reshape(LAGS, band_bins, 2)
     receiver_ids = sta_position * sta_local + jnp.arange(sta_local, dtype=jnp.int32)
@@ -119,8 +115,7 @@
     for step_number in range(STEPS):
         block_number = plan[step_number]
         owner_position = block_number // blk_dev
-        distance = (sta_position - owner_position) % sta_count
-        held = lax.dynamic_index_in_dim(candidates, distance, 0, keepdims=False)
+        held = lax.dynamic_index_in_dim(candidates, owner_position, 0, keepdims=False)
         sources = lax.dynamic_slice_in_dim(
             held, (block_number % blk_dev) * half_sources, half_sources, 3
         )

time: 94.3 us -> 98.1 us (1.040)
  waiting for transfers between devices: 42.7 us -> 46.2 us
  local copies, waits for them, and re-layouts: 12.2 us -> 14.3 us
  other arithmetic: 8.18 us -> 6.72 us
  between operations: 6.33 us -> 5.28 us
    ppermute x3 -> x0, waiting for transfers between devices: 41.6 us -> none  [local(): lax.ppermute(own_half, 'sta', [(i, (i + shift) % sta_count) for i in rang...]
    all_to_all x0 -> x1, waiting for transfers between devices: none -> 40.8 us  [local(): candidates = lax.all_to_all(copies, 'sta', 0, 0, tiled=True)]
    all_to_all x0 -> x1, starting transfers between devices: none -> 5.25 us  [local(): candidates = lax.all_to_all(copies, 'sta', 0, 0, tiled=True)]
    ppermute x3 -> x0, starting transfers between devices: 4.67 us -> none  [local(): lax.ppermute(own_half, 'sta', [(i, (i + shift) % sta_count) for i in rang...]
    ppermute x1, waiting for transfers between devices: 0.01 us -> 3.48 us  [padded(): swapped = lax.ppermute(jnp.where(first, tail, head), axis, [(0, 1), (1, 0)])]
    broadcast_in_dim x0 -> x1, local copies, waits for them, and re-layouts: none -> 1.6 us  [local(): copies = jnp.broadcast_to(own_half[None], (sta_count,) + own_half.shape)]
    another operation x1 -> x0, other arithmetic: 1.46 us -> none  [local(): candidates = jnp.stack(shifted, 0)]
    squeeze x1, local copies, waits for them, and re-layouts: 0.08 us -> 1.27 us  [local(): lax.dynamic_index_in_dim(candidates, owner_position, 0, keepdims=False)]
  transfers between devices with their start and end apart: 5 -> 3, of which waited for: 3 -> 3; matrix products, arithmetic and copies ran while one was open for 4% -> 3% of each run, Pallas kernels for 0% -> 0%
where the time goes in v9:
time: 98.1 us; the launch traced here: 97.7 us
  waiting for transfers between devices  46.2 us (47%)
  matrix products  16.8 us (17%)
  local copies, waits for them, and re-layouts  14.3 us (15%)
  starting transfers between devices  8.35 us (9%)
  other arithmetic  6.72 us (7%)
  between operations  5.28 us (5%)
    all_to_all x1, waiting for transfers between devices, local(): candidates = lax.all_to_all(copies, 'sta', 0, 0, tiled=True)  40.8 us
    dot_general x2, matrix products, local(): lax.dot_general(lag_weights, cross_spectra, (((1, 2), (0, 1)), ((), ())),...  10.8 us
    dot_general x2, matrix products, cross_terms(): jnp.einsum('ctfs,tfn->fcsn', left_stack, right_stack, preferred_element_t...  5.48 us
    all_to_all x1, starting transfers between devices, local(): candidates = lax.all_to_all(copies, 'sta', 0, 0, tiled=True)  5.25 us
    another operation x1, local copies, waits for them, and re-layouts, local(): return jnp.stack(results, 0)  4.71 us
    unnamed x18, local copies, waits for them, and re-layouts  3.83 us
    ppermute x1, waiting for transfers between devices, padded(): swapped = lax.ppermute(jnp.where(first, tail, head), axis, [(0, 1), (1, 0)])  3.48 us
    ppermute x1, starting transfers between devices, padded(): swapped = lax.ppermute(jnp.where(first, tail, head), axis, [(0, 1), (1, 0)])  3.03 us
  transfers between devices with their start and end apart: 3, of which 3 were waited for; matrix products, arithmetic and copies ran while one was open for 3% of the time, Pallas kernels for 0%

profile of v9, /device:TPU:0, one launch (start us, length us, event | category | flops | bytes accessed | tf_op | source)
XLA Modules:
  0.0 97.7 jit_solution(14150846084472124047)
XLA Ops:
  0.0 1.4 %sqrt_bitcast_fusion = f32[4,256,128]{2,1,0:T(8,128)S(1)} fusion(f32[4,2,256,128]{3,2,1,0:T(8,128)} %param.3), kind=kLoop, calls=%fused_computation.39 | loop fusion | flops 393216 | bytes 1572864 | tf_op jit(solution)/shard_map/sqrt | solution.py:76
  1.4 3.0 %collective-permute-start = (f32[4,64,128]{2,1,0:T(8,128)S(1)}, f32[4,64,128]{2,1,0:T(8,128)S(1)}, u32[]{:S(2)}, u32[]{:S(2)}) collective-permute-start(f32[4,64,128]{2,1,0:T(8,128)S(1)} %slice_select_fusion), channel_id=1, source_target_pairs={{0,2},{2,0},{1,3},{3,1},{4,6},{6,4},{5,7},{7,5},{8,10},{10,8},{9,1... | collective-permute-start | bytes 393224 | tf_op jit(solution)/shard_map/ppermute | solution.py:28
  4.5 3.5 %collective-permute-done = f32[4,64,128]{2,1,0:T(8,128)S(1)} collective-permute-done((f32[4,64,128]{2,1,0:T(8,128)S(1)}, f32[4,64,128]{2,1,0:T(8,128)S(1)}, u32[]{:S(2)}, u32[]{:S(2)}) %collective-permute-start) | collective-permute-done | bytes 131104 | tf_op jit(solution)/shard_map/ppermute | solution.py:28
  8.1 0.5 fusion.22
  9.3 0.7 fusion.26
  10.1 1.9 %collective-permute-done.1 = bf16[4,2,256,128]{3,0,2,1:T(4,128)(2,1)S(1)} collective-permute-done((bf16[4,2,256,128]{3,0,2,1:T(4,128)(2,1)S(1)}, bf16[4,2,256,128]{3,0,2,1:T(4,128)(2,1)S(1)}, u32[]{:S(2)}, u32[]{:S(2)}) %collective-permute-start.1) | collective-permute-done | bytes 524320 | tf_op jit(solution)/shard_map/ppermute | solution.py:100
  12.0 0.9 maximum_select_fusion
  13.3 0.7 copy.15
  14.0 1.6 %broadcast_in_dim.5 = bf16[4,8,2,256,64]{3,4,2,1,0:T(8,128)(2,1)} broadcast(bf16[8,2,256,64]{2,3,1,0:T(8,128)(2,1)S(1)} %copy.15), dimensions={1,2,3,4} | broadcast | bytes 2621440 | tf_op jit(solution)/shard_map/broadcast_in_dim | solution.py:107
  15.6 5.3 %all-to-all-start = ((bf16[4,8,2,256,64]{3,4,2,1,0:T(8,128)(2,1)}), bf16[4,8,2,256,64]{3,4,2,1,0:T(8,128)(2,1)}, u32[]{:S(2)}, u32[]{:S(2)}) async-start(bf16[4,8,2,256,64]{3,4,2,1,0:T(8,128)(2,1)} %broadcast_in_dim.5), calls=%async_computation | async-start | bytes 4194304 | tf_op jit(solution)/shard_map/all_to_all | solution.py:108
  20.9 0.6 fusion.53
  26.7 0.7 compare_select_fusion.1
  27.4 1.2 %fusion.37 = (f32[128,256,1]{1,0,2:T(8,128)S(1)}, f32[128,256,1]{1,0,2:T(8,128)}) fusion(s32[256]{0:T(256)S(1)} %get-tuple-element.36, s32[128]{0:T(128)S(1)} %iota_add_fusion.5), kind=kLoop, calls=%fused_computation.60 | loop fusion | flops 491520 | bytes 263680 | tf_op jit(solution)/shard_map/cos | solution.py:50
  28.7 40.8 %all-to-all-done = bf16[4,8,2,256,64]{3,4,2,1,0:T(8,128)(2,1)} async-done(((bf16[4,8,2,256,64]{3,4,2,1,0:T(8,128)(2,1)}), bf16[4,8,2,256,64]{3,4,2,1,0:T(8,128)(2,1)}, u32[]{:S(2)}, u32[]{:S(2)}) %all-to-all-start) | async-done | bytes 2097184 | tf_op jit(solution)/shard_map/all_to_all | solution.py:108
  69.5 1.3 %dynamic-slice_bitcast_fusion.1 = (bf16[8,2,256,64]{2,3,1,0:T(8,128)(2,1)S(1)}, bf16[8,2,256,64]{2,3,1,0:T(8,128)(2,1)S(1)}) fusion(bf16[4,8,2,256,64]{3,4,2,1,0:T(8,128)(2,1)} %all-to-all-done, s32[]{:T(128)S(6)} %select_n.84, s32[]{:T(128)S(6)} %select_n.87), kind=kLoop, calls=%fused_computation.38 | loop fusion | bytes 2097160 | tf_op jit(solution)/shard_map/jit(dynamic_index_in_dim)/squeeze | solution.py:118
  71.5 0.7 fusion.51
  72.3 2.0 %copy.30 = bf16[8,1,256,64]{3,0,2,1:T(8,128)(2,1)} copy(bf16[8,1,256,64]{2,3,1,0:T(8,128)(2,1)} %get-tuple-element.13) | data formatting | bytes 524288
  75.1 0.6 copy-done.1
  75.8 0.4 maximum_bitcast_fusion
  76.2 2.6 %convolution_convert_fusion = bf16[256,2,64,128]{3,2,1,0:T(8,128)(2,1)S(1)} fusion(bf16[1,16,256,64]{3,1,0,2:T(8,128)(2,1)S(1)} %get-tuple-element.16, bf16[1,16,256,64]{3,1,0,2:T(8,128)(2,1)S(1)} %get-tuple-element.15, bf16[8,256,128]{2,0,1:T(8,128)(2,1)S(1)} %get-tuple-element.10, bf16[8,256,128]{2,0,1:T(8,128)(2,1)S(1)} %get-tuple-element.9), kind=kOutput, calls=%fused_computation.4 | convolution fusion | flops 141033472 | bytes 10485760 | tf_op jit(solution)/shard_map/ctfs,tfn->fcsn/dot_general | solution.py:61
  78.8 2.8 %convolution_convert_fusion.1 = bf16[256,2,64,128]{3,2,1,0:T(8,128)(2,1)S(1)} fusion(bf16[1,16,256,64]{3,1,0,2:T(8,128)(2,1)S(1)} %get-tuple-element.12, bf16[1,16,256,64]{3,1,0,2:T(8,128)(2,1)S(1)} %get-tuple-element.11, bf16[8,256,128]{2,0,1:T(8,128)(2,1)S(1)} %get-tuple-element.10, bf16[8,256,128]{2,0,1:T(8,128)(2,1)S(1)} %get-tuple-element.9), kind=kOutput, calls=%fused_computation.5 | convolution fusion | flops 141033472 | bytes 10485760 | tf_op jit(solution)/shard_map/ctfs,tfn->fcsn/dot_general | solution.py:61
  81.7 5.4 %fusion.19 = bf16[1,128,64,128]{3,1,2,0:T(8,128)(2,1)S(1)} fusion(f32[64,128]{1,0:T(8,128)S(1)} %copy-done.4, bf16[256,2,64,128]{3,2,1,0:T(8,128)(2,1)S(1)} %convolution_convert_fusion, f32[128,256,1]{1,0,2:T(8,128)S(1)} %copy-done.2, f32[128,256,1]{1,0,2:T(8,128)S(1)} %get-tuple-element.25), kind=kOutput, calls=%fused_computation.18 | convolution fusion | flops 1076035584 | bytes 10780672 | tf_op jit(solution)/shard_map/dot_general | solution.py:123
  87.1 5.4 %fusion.16 = bf16[1,128,64,128]{3,1,2,0:T(8,128)(2,1)S(1)} fusion(f32[64,128]{1,0:T(8,128)S(1)} %copy-done.3, bf16[256,2,64,128]{3,2,1,0:T(8,128)(2,1)S(1)} %convolution_convert_fusion.1, f32[128,256,1]{1,0,2:T(8,128)S(1)} %copy-done.2, f32[128,256,1]{1,0,2:T(8,128)S(1)} %get-tuple-element.25), kind=kOutput, calls=%fused_computation.17 | convolution fusion | flops 1076035584 | bytes 10780672 | tf_op jit(solution)/shard_map/dot_general | solution.py:123
  92.9 4.7 %copy.24 = bf16[2,128,64,128]{3,2,1,0:T(8,128)(2,1)} copy(bf16[2,128,64,128]{3,1,2,0:T(8,128)(2,1)S(1)} %pad_maximum_fusion) | data formatting | bytes 8388608 | tf_op jit(solution)/shard_map/stack | solution.py:140
  (36 shorter events, 3.4 us)
Async XLA Ops:
  1.4 6.5 %collective-permute-start = (f32[4,64,128]{2,1,0:T(8,128)S(1)}, f32[4,64,128]{2,1,0:T(8,128)S(1)}, u32[]{:S(2)}, u32[]{:S(2)}) collective-permute-start(f32[4,64,128]{2,1,0:T(8,128)S(1)} %slice_select_fusion), channel_id=1, source_target_pairs={{0,2},{2,0},{1,3},{3,1},{4,6},{6,4},{5,7},{7,5},{8,10},{10,8},{9,1... | collective-permute-start | bytes 393224 | tf_op jit(solution)/shard_map/ppermute | solution.py:28
  8.1 1.2 %copy-start = (f32[4,2,256,128]{3,2,1,0:T(8,128)S(1)}, f32[4,2,256,128]{3,2,1,0:T(8,128)}, u32[]{:S(2)}) copy-start(f32[4,2,256,128]{3,2,1,0:T(8,128)} %param.3) | copy-start | bytes 3145732
  10.0 2.0 %collective-permute-start.1 = (bf16[4,2,256,128]{3,0,2,1:T(4,128)(2,1)S(1)}, bf16[4,2,256,128]{3,0,2,1:T(4,128)(2,1)S(1)}, u32[]{:S(2)}, u32[]{:S(2)}) collective-permute-start(bf16[4,2,256,128]{3,0,2,1:T(4,128)(2,1)S(1)} %fusion.26), channel_id=1, source_target_pairs={{0,1},{1,0},{2,3},{3,2},{4,5},{5,4},{6,7},{7,6},{8,9},{9,8},{10,11... | collective-permute-start | bytes 1572872 | tf_op jit(solution)/shard_map/ppermute | solution.py:100
  15.6 5.3 %copy-start.5 = (s32[2]{0:T(128)S(1)}, s32[2]{0:T(128)}, u32[]{:S(2)}) copy-start(s32[2]{0:T(128)} %param.4) | copy-start | bytes 28
  15.6 10.9 %copy-start.6 = (s32[4,4]{1,0:T(4,128)S(1)}, s32[4,4]{1,0:T(4,128)}, u32[]{:S(2)}) copy-start(s32[4,4]{1,0:T(4,128)} %param.5) | copy-start | bytes 196
  15.6 53.9 %all-to-all-start = ((bf16[4,8,2,256,64]{3,4,2,1,0:T(8,128)(2,1)}), bf16[4,8,2,256,64]{3,4,2,1,0:T(8,128)(2,1)}, u32[]{:S(2)}, u32[]{:S(2)}) async-start(bf16[4,8,2,256,64]{3,4,2,1,0:T(8,128)(2,1)} %broadcast_in_dim.5), calls=%async_computation | async-start | bytes 4194304 | tf_op jit(solution)/shard_map/all_to_all | solution.py:108
  74.7 1.0 %copy-start.1 = (bf16[8,1,256,64]{3,0,2,1:T(8,128)(2,1)S(1)}, bf16[8,1,256,64]{3,0,2,1:T(8,128)(2,1)}, u32[]{:S(2)}) copy-start(bf16[8,1,256,64]{3,0,2,1:T(8,128)(2,1)} %copy.30) | copy-start | bytes 786436
  78.8 2.9 %copy-start.2 = (f32[128,256,1]{1,0,2:T(8,128)S(1)}, f32[128,256,1]{1,0,2:T(8,128)}, u32[]{:S(2)}) copy-start(f32[128,256,1]{1,0,2:T(8,128)} %get-tuple-element.26) | copy-start | bytes 393220
  78.8 2.9 %copy-start.4 = (f32[64,128]{1,0:T(8,128)S(1)}, f32[64,128]{1,0:T(8,128)}, u32[]{:S(2)}) copy-start(f32[64,128]{1,0:T(8,128)} %get-tuple-element.28) | copy-start | bytes 98308
  81.7 5.4 %copy-start.3 = (f32[64,128]{1,0:T(8,128)S(1)}, f32[64,128]{1,0:T(8,128)}, u32[]{:S(2)}) copy-start(f32[64,128]{1,0:T(8,128)} %get-tuple-element.27) | copy-start | bytes 98308

commit v10 on v5

--- a/solution.py
+++ b/solution.py
@@ -98,18 +98,13 @@
     receivers = lax.all_gather(white, "seg", axis=0, tiled=True) if seg_count > 2 else None
     if receivers is None:
         partner = lax.ppermute(white, "seg", [(0, 1), (1, 0)])
-        receivers = jnp.where(
-            seg_position == 0,
-            jnp.concatenate([white, partner], 0),
-            jnp.concatenate([partner, white], 0),
-        )
+        receivers = jnp.concatenate([white, partner], 0)
     own_half = lax.dynamic_slice_in_dim(receivers, seg_position * half_sources, half_sources, 3)
     shifted = [own_half]
     for shift in range(1, sta_count):
         shifted.append(
             lax.ppermute(own_half, "sta", [(i, (i + shift) % sta_count) for i in range(sta_count)])
         )
-    candidates = jnp.stack(shifted, 0)
     blk_dev = sta_local // SRC
     lag_weights = lag_table(band_position * band_bins).reshape(LAGS, band_bins, 2)
     receiver_ids = sta_position * sta_local + jnp.arange(sta_local, dtype=jnp.int32)
@@ -120,7 +115,7 @@
         block_number = plan[step_number]
         owner_position = block_number // blk_dev
         distance = (sta_position - owner_position) % sta_count
-        held = lax.dynamic_index_in_dim(candidates, distance, 0, keepdims=False)
+        held = lax.switch(distance, [lambda x=x: x for x in shifted])
         sources = lax.dynamic_slice_in_dim(
             held, (block_number % blk_dev) * half_sources, half_sources, 3
         )

time: 94.3 us -> 116 us (1.23)
  local copies, waits for them, and re-layouts: 12.2 us -> 28.5 us
  other arithmetic: 8.18 us -> 12.9 us
  waiting for transfers between devices: 42.7 us -> 40.4 us
  matrix products: 16.8 us -> 18.2 us
    another operation x0 -> x2, local copies, waits for them, and re-layouts: none -> 7.71 us  [cross_terms(): jnp.stack([jnp.concatenate([src_real, src_imag], 0), jnp.concatenate([src...]
    ppermute x3, waiting for transfers between devices: 41.6 us -> 36.9 us  [local(): lax.ppermute(own_half, 'sta', [(i, (i + shift) % sta_count) for i in rang...]
    cond x0 -> x4, local copies, waits for them, and re-layouts: none -> 3.91 us
    ppermute x0 -> x3, local copies, waits for them, and re-layouts: none -> 3.51 us  [local(): lax.ppermute(own_half, 'sta', [(i, (i + shift) % sta_count) for i in rang...]
    ppermute x1, waiting for transfers between devices: 0.01 us -> 3.48 us  [padded(): swapped = lax.ppermute(jnp.where(first, tail, head), axis, [(0, 1), (1, 0)])]
    another operation x2 -> x4, other arithmetic: 0.8 us -> 3.53 us  [cross_terms(): jnp.stack([jnp.concatenate([src_real, src_imag], 0), jnp.concatenate([src...]
    neg x2, other arithmetic: 0.14 us -> 1.99 us  [cross_terms(): -src_real]
    squeeze x0 -> x1, other arithmetic: none -> 1.51 us  [cross_terms(): right_stack = jnp.concatenate([receivers[:, 0], receivers[:, 1]], 0)]
  transfers between devices with their start and end apart: 5 -> 5, of which waited for: 3 -> 3; matrix products, arithmetic and copies ran while one was open for 4% -> 6% of each run, Pallas kernels for 0% -> 0%
where the time goes in v10:
time: 116 us; the launch traced here: 115 us
  waiting for transfers between devices  40.4 us (35%)
  local copies, waits for them, and re-layouts  28.5 us (25%)
  matrix products  18.2 us (16%)
  other arithmetic  12.9 us (11%)
  starting transfers between devices  8.02 us (7%)
  between operations  6.75 us (6%)
    ppermute x3, waiting for transfers between devices, local(): lax.ppermute(own_half, 'sta', [(i, (i + shift) % sta_count) for i in rang...  36.9 us
    dot_general x2, matrix products, local(): lax.dot_general(lag_weights, cross_spectra, (((1, 2), (0, 1)), ((), ())),...  10.8 us
    another operation x2, local copies, waits for them, and re-layouts, cross_terms(): jnp.stack([jnp.concatenate([src_real, src_imag], 0), jnp.concatenate([src...  7.71 us
    dot_general x2, matrix products, cross_terms(): jnp.einsum('ctfs,tfn->fcsn', left_stack, right_stack, preferred_element_t...  6.83 us
    ppermute x3, starting transfers between devices, local(): lax.ppermute(own_half, 'sta', [(i, (i + shift) % sta_count) for i in rang...  4.92 us
    unnamed x24, local copies, waits for them, and re-layouts  4.89 us
    another operation x1, local copies, waits for them, and re-layouts, local(): return jnp.stack(results, 0)  4.71 us
    cond x4, local copies, waits for them, and re-layouts  3.91 us
  transfers between devices with their start and end apart: 5, of which 3 were waited for; matrix products, arithmetic and copies ran while one was open for 6% of the time, Pallas kernels for 0%

profile of v10, /device:TPU:0, one launch (start us, length us, event | category | flops | bytes accessed | tf_op | source)
XLA Modules:
  0.0 115.0 jit_solution(16199249643769808713)
XLA Ops:
  0.0 1.5 %sqrt_bitcast_fusion = f32[4,256,128]{2,1,0:T(8,128)S(1)} fusion(f32[4,2,256,128]{3,2,1,0:T(8,128)} %param.11), kind=kLoop, calls=%fused_computation.47 | loop fusion | flops 393216 | bytes 1572864 | tf_op jit(solution)/shard_map/sqrt | solution.py:76
  1.5 3.0 %collective-permute-start = (f32[4,64,128]{2,1,0:T(8,128)S(1)}, f32[4,64,128]{2,1,0:T(8,128)S(1)}, u32[]{:S(2)}, u32[]{:S(2)}) collective-permute-start(f32[4,64,128]{2,1,0:T(8,128)S(1)} %slice_select_fusion), channel_id=1, source_target_pairs={{0,2},{2,0},{1,3},{3,1},{4,6},{6,4},{5,7},{7,5},{8,10},{10,8},{9,1... | collective-permute-start | bytes 393224 | tf_op jit(solution)/shard_map/ppermute | solution.py:28
  4.6 3.5 %collective-permute-done = f32[4,64,128]{2,1,0:T(8,128)S(1)} collective-permute-done((f32[4,64,128]{2,1,0:T(8,128)S(1)}, f32[4,64,128]{2,1,0:T(8,128)S(1)}, u32[]{:S(2)}, u32[]{:S(2)}) %collective-permute-start) | collective-permute-done | bytes 131104 | tf_op jit(solution)/shard_map/ppermute | solution.py:28
  17.5 3.9 %collective-permute-start.4 = (bf16[8,2,256,64]{2,3,1,0:T(8,128)(2,1)S(1)}, bf16[8,2,256,64]{2,3,1,0:T(8,128)(2,1)}, u32[]{:S(2)}, u32[]{:S(2)}) collective-permute-start(bf16[8,2,256,64]{2,3,1,0:T(8,128)(2,1)S(1)} %copy.76), channel_id=1, source_target_pairs={{0,12},{4,0},{8,4},{12,8},{1,13},{5,1},{9,5},{13,9},{2,14},{6,2},{... | collective-permute-start | bytes 1572872 | tf_op jit(solution)/shard_map/ppermute | solution.py:106
  24.4 1.2 %fusion.35 = (f32[128,256,1]{1,0,2:T(8,128)S(1)}, f32[128,256,1]{1,0,2:T(8,128)}) fusion(s32[256]{0:T(256)S(1)} %get-tuple-element.232, s32[128]{0:T(128)S(1)} %iota_add_fusion.5), kind=kLoop, calls=%fused_computation.70 | loop fusion | flops 491520 | bytes 263680 | tf_op jit(solution)/shard_map/cos | solution.py:50
  25.7 1.2 %copy.79 = bf16[8,2,256,64]{3,2,1,0:T(8,128)(2,1)} copy(bf16[8,2,256,64]{3,0,2,1:T(8,128)(2,1)S(1)} %fusion.16) | data formatting | bytes 1048576 | tf_op jit(solution)/shard_map/dynamic_slice | solution.py:102
  26.9 1.5 %fusion.23 = (bf16[8,256,128]{2,0,1:T(8,128)(2,1)}, bf16[8,256,128]{2,0,1:T(8,128)(2,1)}) fusion(bf16[4,2,256,128]{3,0,2,1:T(4,128)(2,1)S(1)} %fusion.21, bf16[4,2,256,128]{3,0,2,1:T(4,128)(2,1)S(1)} %collective-permute-done.1), kind=kLoop, calls=%fused_computation.36 | loop fusion | flops 2097152 | bytes 2097152 | tf_op jit(solution)/shard_map/squeeze | solution.py:60
  28.4 5.4 %collective-permute-done.4 = bf16[8,2,256,64]{2,3,1,0:T(8,128)(2,1)} collective-permute-done((bf16[8,2,256,64]{2,3,1,0:T(8,128)(2,1)S(1)}, bf16[8,2,256,64]{2,3,1,0:T(8,128)(2,1)}, u32[]{:S(2)}, u32[]{:S(2)}) %collective-permute-start.4) | collective-permute-done | bytes 524320 | tf_op jit(solution)/shard_map/ppermute | solution.py:106
  33.8 1.5 %copy.82 = bf16[8,2,256,64]{3,2,1,0:T(8,128)(2,1)S(1)} copy(bf16[8,2,256,64]{2,3,1,0:T(8,128)(2,1)} %collective-permute-done.4) | data formatting | bytes 1048576 | tf_op jit(solution)/shard_map/ppermute | solution.py:106
  35.3 31.5 %collective-permute-done.3 = bf16[8,2,256,64]{2,3,1,0:T(8,128)(2,1)S(1)} collective-permute-done((bf16[8,2,256,64]{2,3,1,0:T(8,128)(2,1)S(1)}, bf16[8,2,256,64]{2,3,1,0:T(8,128)(2,1)S(1)}, u32[]{:S(2)}, u32[]{:S(2)}) %collective-permute-start.3) | collective-permute-done | bytes 524320 | tf_op jit(solution)/shard_map/ppermute | solution.py:106
  67.3 1.5 %copy.80 = bf16[8,2,256,64]{3,2,1,0:T(8,128)(2,1)S(1)} copy(bf16[8,2,256,64]{2,3,1,0:T(8,128)(2,1)} %collective-permute-done.2) | data formatting | bytes 1048576 | tf_op jit(solution)/shard_map/ppermute | solution.py:106
  68.9 3.9 %conditional.3 = (bf16[8,2,256,64]{3,2,1,0:T(8,128)(2,1)S(1)}, bf16[8,256,64]{1,2,0:T(8,128)(2,1)}, bf16[8,256,64]{1,2,0:T(8,128)(2,1)S(1)}) conditional(s32[]{:T(128)} %clamp.7, bf16[8,2,256,64]{3,2,1,0:T(8,128)(2,1)} %copy.79, bf16[8,2,256,64]{3,2,1,0:T(8,128)(2,1)S(1)} %copy.80, ...), branch_computations={%region_5.6_spmd.clone, %region_6.7_spmd.clone, %region_7.8_spmd.c... | conditional | flops 131072 | bytes 2621464 | solution.py:118
  69.7 1.9 %copy.107 = bf16[8,256,64]{1,2,0:T(8,128)(2,1)} copy(bf16[8,256,64]{2,1,0:T(8,128)(2,1)} %slice_bitcast_fusion.5) | data formatting | bytes 524288 | tf_op jit(solution)/shard_map/cond
  73.9 3.1 %conditional.2 = (bf16[8,2,256,64]{3,2,1,0:T(8,128)(2,1)}, bf16[8,256,64]{1,2,0:T(8,128)(2,1)}, bf16[8,256,64]{1,2,0:T(8,128)(2,1)S(1)}) conditional(s32[]{:T(128)} %clamp.6, bf16[8,2,256,64]{3,2,1,0:T(8,128)(2,1)} %copy.79, bf16[8,2,256,64]{3,2,1,0:T(8,128)(2,1)S(1)} %copy.80, ...), branch_computations={%region_0.1_spmd.clone, %region_1.2_spmd.clone, %region_2.3_spmd.c... | conditional | flops 131072 | bytes 2621464 | solution.py:118
  77.7 1.5 %copy.83 = bf16[8,2,256,64]{2,3,0,1:T(8,128)(2,1)S(1)} copy(bf16[8,2,256,64]{3,2,1,0:T(8,128)(2,1)} %get-tuple-element.182) | data formatting | bytes 1048576
  79.2 1.5 %copy.92 = bf16[8,2,256,64]{2,3,0,1:T(8,128)(2,1)S(1)} copy(bf16[8,2,256,64]{3,2,1,0:T(8,128)(2,1)} %copy-done.3) | data formatting | bytes 1048576
  82.1 3.1 %copy.86 = bf16[2,16,256,64]{3,1,0,2:T(8,128)(2,1)S(1)} copy(bf16[2,16,256,64]{2,3,1,0:T(8,128)(2,1)S(1)} %pad_maximum_fusion.1) | data formatting | bytes 2097152 | tf_op jit(solution)/shard_map/stack | solution.py:57
  85.2 1.2 %maximum_bitcast_fusion.5 = (bf16[1,16,256,64]{2,3,1,0:T(8,128)(2,1)S(1)}, bf16[1,16,256,64]{2,3,1,0:T(8,128)(2,1)S(1)}) fusion(bf16[8,256,64]{1,2,0:T(8,128)(2,1)S(1)} %slice_bitcast_fusion.8, bf16[8,256,64]{1,2,0:T(8,128)(2,1)} %get-tuple-element.205, bf16[8,256,64]{1,2,0:T(8,128)(2,1)} %copy-done.4), kind=kLoop, calls=%fused_computation.43 | loop fusion | flops 524288 | bytes 1835008 | tf_op jit(solution)/shard_map/stack | solution.py:57
  87.5 4.6 %copy.95 = bf16[2,16,256,64]{3,1,0,2:T(8,128)(2,1)} copy(bf16[2,16,256,64]{2,3,1,0:T(8,128)(2,1)} %pad_maximum_fusion.2) | data formatting | bytes 2097152 | tf_op jit(solution)/shard_map/stack | solution.py:57
  92.1 4.0 %convolution_convert_fusion = bf16[256,2,64,128]{3,2,1,0:T(8,128)(2,1)S(1)} fusion(bf16[2,16,256,64]{3,1,0,2:T(8,128)(2,1)} %copy.95, bf16[8,256,128]{2,0,1:T(8,128)(2,1)S(1)} %copy-done.1, bf16[8,256,128]{2,0,1:T(8,128)(2,1)S(1)} %copy-done), kind=kOutput, calls=%fused_computation.12 | convolution fusion | flops 140509184 | bytes 10485760 | tf_op jit(solution)/shard_map/ctfs,tfn->fcsn/dot_general | solution.py:61
  96.1 2.9 %convolution_convert_fusion.1 = bf16[256,2,64,128]{3,2,1,0:T(8,128)(2,1)S(1)} fusion(bf16[2,16,256,64]{3,1,0,2:T(8,128)(2,1)S(1)} %copy.86, bf16[8,256,128]{2,0,1:T(8,128)(2,1)S(1)} %copy-done.1, bf16[8,256,128]{2,0,1:T(8,128)(2,1)S(1)} %copy-done), kind=kOutput, calls=%fused_computation.13 | convolution fusion | flops 140509184 | bytes 10485760 | tf_op jit(solution)/shard_map/ctfs,tfn->fcsn/dot_general | solution.py:61
  99.0 5.4 %fusion.13 = bf16[1,128,64,128]{3,1,2,0:T(8,128)(2,1)S(1)} fusion(f32[64,128]{1,0:T(8,128)S(1)} %copy-done.8, bf16[256,2,64,128]{3,2,1,0:T(8,128)(2,1)S(1)} %convolution_convert_fusion, f32[128,256,1]{1,0,2:T(8,128)S(1)} %copy-done.6, f32[128,256,1]{1,0,2:T(8,128)S(1)} %get-tuple-element.221), kind=kOutput, calls=%fused_computation.20 | convolution fusion | flops 1076035584 | bytes 10780672 | tf_op jit(solution)/shard_map/dot_general | solution.py:123
  104.4 5.4 %fusion.10 = bf16[1,128,64,128]{3,1,2,0:T(8,128)(2,1)S(1)} fusion(f32[64,128]{1,0:T(8,128)S(1)} %copy-done.7, bf16[256,2,64,128]{3,2,1,0:T(8,128)(2,1)S(1)} %convolution_convert_fusion.1, f32[128,256,1]{1,0,2:T(8,128)S(1)} %copy-done.6, f32[128,256,1]{1,0,2:T(8,128)S(1)} %get-tuple-element.221), kind=kOutput, calls=%fused_computation.19 | convolution fusion | flops 1076035584 | bytes 10780672 | tf_op jit(solution)/shard_map/dot_general | solution.py:123
  110.2 4.7 %copy.97 = bf16[2,128,64,128]{3,2,1,0:T(8,128)(2,1)} copy(bf16[2,128,64,128]{3,1,2,0:T(8,128)(2,1)S(1)} %pad_maximum_fusion) | data formatting | bytes 8388608 | tf_op jit(solution)/shard_map/stack | solution.py:140
  (59 shorter events, 15.9 us)
Async XLA Ops:
  0.0 9.2 %copy-start.2 = (f32[4,2,256,128]{3,2,1,0:T(8,128)S(1)}, f32[4,2,256,128]{3,2,1,0:T(8,128)}, u32[]{:S(2)}) copy-start(f32[4,2,256,128]{3,2,1,0:T(8,128)} %param.11) | copy-start | bytes 3145732
  1.5 8.6 %copy-start.9 = (s32[2]{0:T(128)S(1)}, s32[2]{0:T(128)}, u32[]{:S(2)}) copy-start(s32[2]{0:T(128)} %param.12) | copy-start | bytes 28
  1.5 14.2 %copy-start.10 = (s32[4,4]{1,0:T(4,128)S(1)}, s32[4,4]{1,0:T(4,128)}, u32[]{:S(2)}) copy-start(s32[4,4]{1,0:T(4,128)} %param.13) | copy-start | bytes 196
  1.5 6.5 %collective-permute-start = (f32[4,64,128]{2,1,0:T(8,128)S(1)}, f32[4,64,128]{2,1,0:T(8,128)S(1)}, u32[]{:S(2)}, u32[]{:S(2)}) collective-permute-start(f32[4,64,128]{2,1,0:T(8,128)S(1)} %slice_select_fusion), channel_id=1, source_target_pairs={{0,2},{2,0},{1,3},{3,1},{4,6},{6,4},{5,7},{7,5},{8,10},{10,8},{9,1... | collective-permute-start | bytes 393224 | tf_op jit(solution)/shard_map/ppermute | solution.py:28
  10.0 5.9 %collective-permute-start.1 = (bf16[4,2,256,128]{3,0,2,1:T(4,128)(2,1)S(1)}, bf16[4,2,256,128]{3,0,2,1:T(4,128)(2,1)S(1)}, u32[]{:S(2)}, u32[]{:S(2)}) collective-permute-start(bf16[4,2,256,128]{3,0,2,1:T(4,128)(2,1)S(1)} %fusion.21), channel_id=1, source_target_pairs={{0,1},{1,0},{2,3},{3,2},{4,5},{5,4},{6,7},{7,6},{8,9},{9,8},{10,11... | collective-permute-start | bytes 1572872 | tf_op jit(solution)/shard_map/ppermute | solution.py:100
  17.5 16.3 %collective-permute-start.4 = (bf16[8,2,256,64]{2,3,1,0:T(8,128)(2,1)S(1)}, bf16[8,2,256,64]{2,3,1,0:T(8,128)(2,1)}, u32[]{:S(2)}, u32[]{:S(2)}) collective-permute-start(bf16[8,2,256,64]{2,3,1,0:T(8,128)(2,1)S(1)} %copy.76), channel_id=1, source_target_pairs={{0,12},{4,0},{8,4},{12,8},{1,13},{5,1},{9,5},{13,9},{2,14},{6,2},{... | collective-permute-start | bytes 1572872 | tf_op jit(solution)/shard_map/ppermute | solution.py:106
  21.4 45.4 %collective-permute-start.3 = (bf16[8,2,256,64]{2,3,1,0:T(8,128)(2,1)S(1)}, bf16[8,2,256,64]{2,3,1,0:T(8,128)(2,1)S(1)}, u32[]{:S(2)}, u32[]{:S(2)}) collective-permute-start(bf16[8,2,256,64]{2,3,1,0:T(8,128)(2,1)S(1)} %copy.76), channel_id=1, source_target_pairs={{0,8},{4,12},{8,0},{12,4},{1,9},{5,13},{9,1},{13,5},{2,10},{6,14},... | collective-permute-start | bytes 1572872 | tf_op jit(solution)/shard_map/ppermute | solution.py:106
  21.4 45.9 %collective-permute-start.2 = (bf16[8,2,256,64]{2,3,1,0:T(8,128)(2,1)S(1)}, bf16[8,2,256,64]{2,3,1,0:T(8,128)(2,1)}, u32[]{:S(2)}, u32[]{:S(2)}) collective-permute-start(bf16[8,2,256,64]{2,3,1,0:T(8,128)(2,1)S(1)} %copy.76), channel_id=1, source_target_pairs={{0,4},{4,8},{8,12},{12,0},{1,5},{5,9},{9,13},{13,1},{2,6},{6,10},{... | collective-permute-start | bytes 1572872 | tf_op jit(solution)/shard_map/ppermute | solution.py:106
  72.8 1.0 copy-start.3
  72.8 1.1 copy-start.4
  77.0 0.7 copy-start.5
  85.1 7.0 %copy-start = (bf16[8,256,128]{2,0,1:T(8,128)(2,1)S(1)}, bf16[8,256,128]{2,0,1:T(8,128)(2,1)}, u32[]{:S(2)}) copy-start(bf16[8,256,128]{2,0,1:T(8,128)(2,1)} %get-tuple-element.209) | copy-start | bytes 1572868
  85.1 7.0 %copy-start.1 = (bf16[8,256,128]{2,0,1:T(8,128)(2,1)S(1)}, bf16[8,256,128]{2,0,1:T(8,128)(2,1)}, u32[]{:S(2)}) copy-start(bf16[8,256,128]{2,0,1:T(8,128)(2,1)} %get-tuple-element.210) | copy-start | bytes 1572868
  96.1 2.9 %copy-start.6 = (f32[128,256,1]{1,0,2:T(8,128)S(1)}, f32[128,256,1]{1,0,2:T(8,128)}, u32[]{:S(2)}) copy-start(f32[128,256,1]{1,0,2:T(8,128)} %get-tuple-element.222) | copy-start | bytes 393220
  96.1 2.9 %copy-start.8 = (f32[64,128]{1,0:T(8,128)S(1)}, f32[64,128]{1,0:T(8,128)}, u32[]{:S(2)}) copy-start(f32[64,128]{1,0:T(8,128)} %get-tuple-element.224) | copy-start | bytes 98308
  99.0 5.4 %copy-start.7 = (f32[64,128]{1,0:T(8,128)S(1)}, f32[64,128]{1,0:T(8,128)}, u32[]{:S(2)}) copy-start(f32[64,128]{1,0:T(8,128)} %get-tuple-element.223) | copy-start | bytes 98308

commit v11 on v5

--- a/solution.py
+++ b/solution.py
@@ -95,15 +95,25 @@
     white = (spectra / (smooth[:, None] + EPSILON)).astype(jnp.bfloat16)
     seg_count = lax.axis_size("seg")
     sta_count = lax.axis_size("sta")
-    receivers = lax.all_gather(white, "seg", axis=0, tiled=True) if seg_count > 2 else None
-    if receivers is None:
-        partner = lax.ppermute(white, "seg", [(0, 1), (1, 0)])
-        receivers = jnp.where(
+    if seg_count == 2:
+        mine = lax.dynamic_slice_in_dim(white, seg_position * half_sources, half_sources, 3)
+        theirs = lax.dynamic_slice_in_dim(
+            white, (1 - seg_position) * half_sources, half_sources, 3
+        )
+        wanted = lax.ppermute(theirs, "seg", [(0, 1), (1, 0)])
+        own_half = jnp.concatenate([mine, wanted], 0)
+        kept = lax.ppermute(mine, "seg", [(0, 1), (1, 0)])
+        partner = jnp.where(
             seg_position == 0,
-            jnp.concatenate([white, partner], 0),
-            jnp.concatenate([partner, white], 0),
+            jnp.concatenate([wanted, kept], 3),
+            jnp.concatenate([kept, wanted], 3),
         )
-    own_half = lax.dynamic_slice_in_dim(receivers, seg_position * half_sources, half_sources, 3)
+        receivers = jnp.concatenate([white, partner], 0)
+    else:
+        receivers = lax.all_gather(white, "seg", axis=0, tiled=True)
+        own_half = lax.dynamic_slice_in_dim(
+            receivers, seg_position * half_sources, half_sources, 3
+        )
     shifted = [own_half]
     for shift in range(1, sta_count):
         shifted.append(

time: 94.3 us -> 102 us (1.082)
  other arithmetic: 8.18 us -> 13.6 us
  local copies, waits for them, and re-layouts: 12.2 us -> 17.4 us
  waiting for transfers between devices: 42.7 us -> 38.1 us
  matrix products: 16.8 us -> 18.1 us
    ppermute x0 -> x3, local copies, waits for them, and re-layouts: none -> 7.55 us  [local(): lax.ppermute(own_half, 'sta', [(i, (i + shift) % sta_count) for i in rang...]
    ppermute x3, waiting for transfers between devices: 41.6 us -> 36.8 us  [local(): lax.ppermute(own_half, 'sta', [(i, (i + shift) % sta_count) for i in rang...]
    unnamed x16 -> x2, local copies, waits for them, and re-layouts: 3.81 us -> 0.21 us
    another operation x1 -> x2, other arithmetic: 1.46 us -> 4.22 us  [local(): candidates = jnp.stack(shifted, 0)]
    select_n x1, other arithmetic: 0.95 us -> 2.64 us  [local(): jnp.where(seg_position == 0, jnp.concatenate([wanted, kept], 3), jnp.conc...]
    concatenate x0 -> x1, local copies, waits for them, and re-layouts: none -> 1.54 us  [local(): own_half = jnp.concatenate([mine, wanted], 0)]
  transfers between devices with their start and end apart: 5 -> 6, of which waited for: 3 -> 3; matrix products, arithmetic and copies ran while one was open for 4% -> 14% of each run, Pallas kernels for 0% -> 0%
where the time goes in v11:
time: 102 us
  waiting for transfers between devices  38.1 us (37%)
  matrix products  18.1 us (18%)
  local copies, waits for them, and re-layouts  17.4 us (17%)
  other arithmetic  13.6 us (13%)
  starting transfers between devices  8.22 us (8%)
  between operations  6.3 us (6%)
    ppermute x3, waiting for transfers between devices, local(): lax.ppermute(own_half, 'sta', [(i, (i + shift) % sta_count) for i in rang...  36.8 us
    dot_general x2, matrix products, local(): lax.dot_general(lag_weights, cross_spectra, (((1, 2), (0, 1)), ((), ())),...  11.1 us
    ppermute x3, local copies, waits for them, and re-layouts, local(): lax.ppermute(own_half, 'sta', [(i, (i + shift) % sta_count) for i in rang...  7.55 us
    dot_general x2, matrix products, cross_terms(): jnp.einsum('ctfs,tfn->fcsn', left_stack, right_stack, preferred_element_t...  6.46 us
    another operation x1, local copies, waits for them, and re-layouts, local(): return jnp.stack(results, 0)  4.71 us
    ppermute x3, starting transfers between devices, local(): lax.ppermute(own_half, 'sta', [(i, (i + shift) % sta_count) for i in rang...  4.62 us
    another operation x2, other arithmetic, local(): candidates = jnp.stack(shifted, 0)  4.22 us
    ppermute x1, starting transfers between devices, padded(): swapped = lax.ppermute(jnp.where(first, tail, head), axis, [(0, 1), (1, 0)])  3.03 us
  transfers between devices with their start and end apart: 6, of which 3 were waited for; matrix products, arithmetic and copies ran while one was open for 14% of the time, Pallas kernels for 0%

profile of v11, /device:TPU:0, one launch (start us, length us, event | category | flops | bytes accessed | tf_op | source)
XLA Modules:
  0.0 101.6 jit_solution(17681674733424876043)
XLA Ops:
  0.0 1.4 %sqrt_bitcast_fusion = f32[4,256,128]{2,1,0:T(8,128)S(1)} fusion(f32[4,2,256,128]{3,2,1,0:T(8,128)} %param.3), kind=kLoop, calls=%fused_computation.49 | loop fusion | flops 393216 | bytes 1572864 | tf_op jit(solution)/shard_map/sqrt | solution.py:76
  1.4 3.0 %collective-permute-start = (f32[4,64,128]{2,1,0:T(8,128)S(1)}, f32[4,64,128]{2,1,0:T(8,128)S(1)}, u32[]{:S(2)}, u32[]{:S(2)}) collective-permute-start(f32[4,64,128]{2,1,0:T(8,128)S(1)} %slice_select_fusion), channel_id=1, source_target_pairs={{0,2},{2,0},{1,3},{3,1},{4,6},{6,4},{5,7},{7,5},{8,10},{10,8},{9,1... | collective-permute-start | bytes 393224 | tf_op jit(solution)/shard_map/ppermute | solution.py:28
  4.4 1.3 %fusion.57 = (s32[1]{0:T(128)}, s32[1]{0:T(128)}) fusion(s32[2]{0:T(128)} %param.4), kind=kLoop, calls=%fused_computation.105 | loop fusion | bytes 16 | tf_op jit(solution)/shard_map/slice | solution.py:130
  9.4 0.8 fusion.46
  12.8 0.7 fusion.26
  13.6 1.4 %constant_dynamic-slice_fusion.3 = (bf16[4,2,256,64]{3,0,2,1:T(4,128)(2,1)}, bf16[4,2,256,64]{3,0,2,1:T(4,128)(2,1)S(1)}) fusion(bf16[4,2,256,128]{3,0,2,1:T(4,128)(2,1)S(1)} %fusion.26, s32[]{:T(128)S(6)} %select_n.96, s32[]{:T(128)S(6)} %select_n.97), kind=kLoop, calls=%fused_computation.80 | loop fusion | bytes 1048584 | tf_op jit(solution)/shard_map/dynamic_slice | solution.py:99
  15.7 1.2 %collective-permute-done.1 = bf16[4,2,256,64]{3,0,2,1:T(4,128)(2,1)S(1)} collective-permute-done((bf16[4,2,256,64]{3,0,2,1:T(4,128)(2,1)S(1)}, bf16[4,2,256,64]{3,0,2,1:T(4,128)(2,1)S(1)}, u32[]{:S(2)}, u32[]{:S(2)}) %collective-permute-start.1) | collective-permute-done | bytes 262176 | tf_op jit(solution)/shard_map/ppermute | solution.py:103
  16.9 1.7 %fusion.56 = (bf16[1,8,2,256,64]{4,1,3,2,0:T(8,128)(2,1)S(1)}, bf16[8,2,256,64]{3,0,2,1:T(8,128)(2,1)S(1)}) fusion(bf16[4,2,256,64]{3,0,2,1:T(4,128)(2,1)S(1)} %collective-permute-done.1, bf16[4,2,256,64]{3,0,2,1:T(4,128)(2,1)} %get-tuple-element.21), kind=kLoop, calls=%fused_computation.104 | loop fusion | flops 1048576 | bytes 1572864 | tf_op jit(solution)/shard_map/stack | solution.py:122
  18.6 1.5 %copy.29 = bf16[8,2,256,64]{2,3,1,0:T(8,128)(2,1)} copy(bf16[8,2,256,64]{3,0,2,1:T(8,128)(2,1)S(1)} %get-tuple-element.16) | data formatting | bytes 1048576 | tf_op jit(solution)/shard_map/concatenate | solution.py:104
  20.2 3.6 %collective-permute-start.4 = (bf16[8,2,256,64]{2,3,1,0:T(8,128)(2,1)}, bf16[8,2,256,64]{2,3,1,0:T(8,128)(2,1)}, u32[]{:S(2)}, u32[]{:S(2)}) collective-permute-start(bf16[8,2,256,64]{2,3,1,0:T(8,128)(2,1)} %copy.29), channel_id=1, source_target_pairs={{0,12},{4,0},{8,4},{12,8},{1,13},{5,1},{9,5},{13,9},{2,14},{6,2},{... | collective-permute-start | bytes 1572872 | tf_op jit(solution)/shard_map/ppermute | solution.py:120
  23.8 1.0 collective-permute-start.2
  26.6 2.6 %maximum_select_fusion = bf16[4,2,256,128]{3,0,2,1:T(4,128)(2,1)S(1)} fusion(bf16[4,2,256,64]{3,0,2,1:T(4,128)(2,1)} %collective-permute-done.5, bf16[4,2,256,64]{3,0,2,1:T(4,128)(2,1)S(1)} %collective-permute-done.1, pred[]{:T(512)S(6)} %eq.27), kind=kLoop, calls=%fused_computation.46 | loop fusion | flops 2359296 | bytes 1048577 | tf_op jit(solution)/shard_map/jit(_where)/select_n | solution.py:106
  29.8 6.6 %collective-permute-done.4 = bf16[8,2,256,64]{2,3,1,0:T(8,128)(2,1)} collective-permute-done((bf16[8,2,256,64]{2,3,1,0:T(8,128)(2,1)}, bf16[8,2,256,64]{2,3,1,0:T(8,128)(2,1)}, u32[]{:S(2)}, u32[]{:S(2)}) %collective-permute-start.4) | collective-permute-done | bytes 524320 | tf_op jit(solution)/shard_map/ppermute | solution.py:120
  36.5 2.5 %copy.34 = bf16[8,2,256,64]{3,0,2,1:T(8,128)(2,1)} copy(bf16[8,2,256,64]{2,3,1,0:T(8,128)(2,1)} %collective-permute-done.4) | data formatting | bytes 1048576 | tf_op jit(solution)/shard_map/ppermute | solution.py:120
  39.0 30.2 %collective-permute-done.3 = bf16[8,2,256,64]{2,3,1,0:T(8,128)(2,1)} collective-permute-done((bf16[8,2,256,64]{2,3,1,0:T(8,128)(2,1)}, bf16[8,2,256,64]{2,3,1,0:T(8,128)(2,1)}, u32[]{:S(2)}, u32[]{:S(2)}) %collective-permute-start.3) | collective-permute-done | bytes 524320 | tf_op jit(solution)/shard_map/ppermute | solution.py:120
  69.2 2.5 %copy.32 = bf16[8,2,256,64]{3,0,2,1:T(8,128)(2,1)} copy(bf16[8,2,256,64]{2,3,1,0:T(8,128)(2,1)} %collective-permute-done.3) | data formatting | bytes 1048576 | tf_op jit(solution)/shard_map/ppermute | solution.py:120
  71.7 2.5 %copy.30 = bf16[8,2,256,64]{3,0,2,1:T(8,128)(2,1)} copy(bf16[8,2,256,64]{2,3,1,0:T(8,128)(2,1)} %collective-permute-done.2) | data formatting | bytes 1048576 | tf_op jit(solution)/shard_map/ppermute | solution.py:120
  74.2 2.5 %pad_maximum_fusion = bf16[4,8,2,256,64]{4,1,3,2,0:T(8,128)(2,1)S(1)} fusion(bf16[1,8,2,256,64]{4,1,3,2,0:T(8,128)(2,1)} %bitcast.90, bf16[1,8,2,256,64]{4,1,3,2,0:T(8,128)(2,1)} %bitcast.91, bf16[1,8,2,256,64]{4,1,3,2,0:T(8,128)(2,1)} %bitcast.92, bf16[1,8,2,256,64]{4,1,3,2,0:T(8,128)(2,1)S(1)} %get-tuple-element.15), kind=kLoop, calls=%fused_computation.6 | loop fusion | flops 3145728 | bytes 4194304 | tf_op jit(solution)/shard_map/stack | solution.py:122
  77.6 1.4 %maximum_bitcast_fusion = (bf16[1,16,256,64]{3,1,0,2:T(8,128)(2,1)S(1)}, bf16[1,16,256,64]{3,1,0,2:T(8,128)(2,1)}) fusion(bf16[8,256,64]{2,0,1:T(8,128)(2,1)S(1)} %get-tuple-element.10, bf16[8,256,64]{2,0,1:T(8,128)(2,1)S(1)} %get-tuple-element.9, bf16[8,256,64]{2,0,1:T(8,128)(2,1)S(1)} %fusion.54), kind=kLoop, calls=%fused_computation.25 | loop fusion | flops 2097152 | bytes 1835008 | tf_op jit(solution)/shard_map/stack | solution.py:57
  79.0 2.8 %convolution_convert_fusion = bf16[256,2,64,128]{3,2,1,0:T(8,128)(2,1)S(1)} fusion(bf16[1,16,256,64]{3,1,0,2:T(8,128)(2,1)S(1)} %get-tuple-element.20, bf16[1,16,256,64]{3,1,0,2:T(8,128)(2,1)S(1)} %get-tuple-element.19, bf16[8,256,128]{2,0,1:T(8,128)(2,1)S(1)} %get-tuple-element.12, bf16[8,256,128]{2,0,1:T(8,128)(2,1)S(1)} %get-tuple-element.11), kind=kOutput, calls=%fused_computation.4 | convolution fusion | flops 141033472 | bytes 10485760 | tf_op jit(solution)/shard_map/ctfs,tfn->fcsn/dot_general | solution.py:61
  81.8 3.6 %convolution_convert_fusion.1 = bf16[256,2,64,128]{3,2,1,0:T(8,128)(2,1)S(1)} fusion(bf16[1,16,256,64]{3,1,0,2:T(8,128)(2,1)} %get-tuple-element.18, bf16[1,16,256,64]{3,1,0,2:T(8,128)(2,1)S(1)} %get-tuple-element.17, bf16[8,256,128]{2,0,1:T(8,128)(2,1)S(1)} %get-tuple-element.12, bf16[8,256,128]{2,0,1:T(8,128)(2,1)S(1)} %get-tuple-element.11), kind=kOutput, calls=%fused_computation.5 | convolution fusion | flops 141033472 | bytes 10485760 | tf_op jit(solution)/shard_map/ctfs,tfn->fcsn/dot_general | solution.py:61
  85.4 5.4 %fusion.19 = bf16[1,128,64,128]{3,1,2,0:T(8,128)(2,1)S(1)} fusion(f32[64,128]{1,0:T(8,128)S(1)} %get-tuple-element.32, bf16[256,2,64,128]{3,2,1,0:T(8,128)(2,1)S(1)} %convolution_convert_fusion, f32[128,256,1]{1,0,2:T(8,128)S(1)} %get-tuple-element.30, f32[128,256,1]{1,0,2:T(8,128)S(1)} %get-tuple-element.29), kind=kOutput, calls=%fused_computation.19 | convolution fusion | flops 1076035584 | bytes 10780672 | tf_op jit(solution)/shard_map/dot_general | solution.py:138
  90.9 5.7 %fusion.16 = bf16[1,128,64,128]{3,1,2,0:T(8,128)(2,1)S(1)} fusion(f32[64,128]{1,0:T(8,128)S(1)} %get-tuple-element.31, bf16[256,2,64,128]{3,2,1,0:T(8,128)(2,1)S(1)} %convolution_convert_fusion.1, f32[128,256,1]{1,0,2:T(8,128)S(1)} %get-tuple-element.30, f32[128,256,1]{1,0,2:T(8,128)S(1)} %get-tuple-element.29), kind=kOutput, calls=%fused_computation.18 | convolution fusion | flops 1076035584 | bytes 10780672 | tf_op jit(solution)/shard_map/dot_general | solution.py:138
  96.9 4.7 %copy.45 = bf16[2,128,64,128]{3,2,1,0:T(8,128)(2,1)} copy(bf16[2,128,64,128]{3,1,2,0:T(8,128)(2,1)S(1)} %pad_maximum_fusion.1) | data formatting | bytes 8388608 | tf_op jit(solution)/shard_map/stack | solution.py:155
  (30 shorter events, 4.5 us)
Async XLA Ops:
  1.4 10.1 %collective-permute-start = (f32[4,64,128]{2,1,0:T(8,128)S(1)}, f32[4,64,128]{2,1,0:T(8,128)S(1)}, u32[]{:S(2)}, u32[]{:S(2)}) collective-permute-start(f32[4,64,128]{2,1,0:T(8,128)S(1)} %slice_select_fusion), channel_id=1, source_target_pairs={{0,2},{2,0},{1,3},{3,1},{4,6},{6,4},{5,7},{7,5},{8,10},{10,8},{9,1... | collective-permute-start | bytes 393224 | tf_op jit(solution)/shard_map/ppermute | solution.py:28
  11.6 1.2 %copy-start = (f32[4,2,256,128]{3,2,1,0:T(8,128)S(1)}, f32[4,2,256,128]{3,2,1,0:T(8,128)}, u32[]{:S(2)}) copy-start(f32[4,2,256,128]{3,2,1,0:T(8,128)} %param.3) | copy-start | bytes 3145732
  15.0 1.9 %collective-permute-start.1 = (bf16[4,2,256,64]{3,0,2,1:T(4,128)(2,1)S(1)}, bf16[4,2,256,64]{3,0,2,1:T(4,128)(2,1)S(1)}, u32[]{:S(2)}, u32[]{:S(2)}) collective-permute-start(bf16[4,2,256,64]{3,0,2,1:T(4,128)(2,1)S(1)} %get-tuple-element.22), channel_id=1, source_target_pairs={{0,1},{1,0},{2,3},{3,2},{4,5},{5,4},{6,7},{7,6},{8,9},{9,8},{10,11... | collective-permute-start | bytes 786440 | tf_op jit(solution)/shard_map/ppermute | solution.py:103
  15.1 11.5 %collective-permute-start.5 = (bf16[4,2,256,64]{3,0,2,1:T(4,128)(2,1)}, bf16[4,2,256,64]{3,0,2,1:T(4,128)(2,1)}, u32[]{:S(2)}, u32[]{:S(2)}) collective-permute-start(bf16[4,2,256,64]{3,0,2,1:T(4,128)(2,1)} %get-tuple-element.21), channel_id=1, source_target_pairs={{0,1},{1,0},{2,3},{3,2},{4,5},{5,4},{6,7},{7,6},{8,9},{9,8},{10,11... | collective-permute-start | bytes 786440 | tf_op jit(solution)/shard_map/ppermute | solution.py:105
  20.2 16.3 %collective-permute-start.4 = (bf16[8,2,256,64]{2,3,1,0:T(8,128)(2,1)}, bf16[8,2,256,64]{2,3,1,0:T(8,128)(2,1)}, u32[]{:S(2)}, u32[]{:S(2)}) collective-permute-start(bf16[8,2,256,64]{2,3,1,0:T(8,128)(2,1)} %copy.29), channel_id=1, source_target_pairs={{0,12},{4,0},{8,4},{12,8},{1,13},{5,1},{9,5},{13,9},{2,14},{6,2},{... | collective-permute-start | bytes 1572872 | tf_op jit(solution)/shard_map/ppermute | solution.py:120
  23.8 45.4 %collective-permute-start.3 = (bf16[8,2,256,64]{2,3,1,0:T(8,128)(2,1)}, bf16[8,2,256,64]{2,3,1,0:T(8,128)(2,1)}, u32[]{:S(2)}, u32[]{:S(2)}) collective-permute-start(bf16[8,2,256,64]{2,3,1,0:T(8,128)(2,1)} %copy.29), channel_id=1, source_target_pairs={{0,8},{4,12},{8,0},{12,4},{1,9},{5,13},{9,1},{13,5},{2,10},{6,14},... | collective-permute-start | bytes 1572872 | tf_op jit(solution)/shard_map/ppermute | solution.py:120
  23.8 47.9 %collective-permute-start.2 = (bf16[8,2,256,64]{2,3,1,0:T(8,128)(2,1)}, bf16[8,2,256,64]{2,3,1,0:T(8,128)(2,1)}, u32[]{:S(2)}, u32[]{:S(2)}) collective-permute-start(bf16[8,2,256,64]{2,3,1,0:T(8,128)(2,1)} %copy.29), channel_id=1, source_target_pairs={{0,4},{4,8},{8,12},{12,0},{1,5},{5,9},{9,13},{13,1},{2,6},{6,10},{... | collective-permute-start | bytes 1572872 | tf_op jit(solution)/shard_map/ppermute | solution.py:120

commit v12 on v5

--- a/solution.py
+++ b/solution.py
@@ -110,6 +110,7 @@
             lax.ppermute(own_half, "sta", [(i, (i + shift) % sta_count) for i in range(sta_count)])
         )
     candidates = jnp.stack(shifted, 0)
+    plan, pair_mask, _ = lax.optimization_barrier((plan, pair_mask, own_half))
     blk_dev = sta_local // SRC
     lag_weights = lag_table(band_position * band_bins).reshape(LAGS, band_bins, 2)
     receiver_ids = sta_position * sta_local + jnp.arange(sta_local, dtype=jnp.int32)

time: 94.3 us -> 96.2 us (1.020)
  waiting for transfers between devices: 42.7 us -> 44.9 us
    ppermute x1, waiting for transfers between devices: 0.01 us -> 3.48 us  [padded(): swapped = lax.ppermute(jnp.where(first, tail, head), axis, [(0, 1), (1, 0)])]
    unnamed x16 -> x18, local copies, waits for them, and re-layouts: 3.81 us -> 3.83 us
  transfers between devices with their start and end apart: 5 -> 5, of which waited for: 3 -> 4; matrix products, arithmetic and copies ran while one was open for 4% -> 2% of each run, Pallas kernels for 0% -> 0%
where the time goes in v12:
time: 96.2 us; the launch traced here: 95.8 us
  waiting for transfers between devices  44.9 us (47%)
  matrix products  16.8 us (17%)
  local copies, waits for them, and re-layouts  11.5 us (12%)
  other arithmetic  8.19 us (9%)
  starting transfers between devices  8.02 us (8%)
  between operations  6.4 us (7%)
    ppermute x3, waiting for transfers between devices, local(): lax.ppermute(own_half, 'sta', [(i, (i + shift) % sta_count) for i in rang...  40.8 us
    dot_general x2, matrix products, local(): lax.dot_general(lag_weights, cross_spectra, (((1, 2), (0, 1)), ((), ())),...  10.8 us
    dot_general x2, matrix products, cross_terms(): jnp.einsum('ctfs,tfn->fcsn', left_stack, right_stack, preferred_element_t...  5.48 us
    ppermute x3, starting transfers between devices, local(): lax.ppermute(own_half, 'sta', [(i, (i + shift) % sta_count) for i in rang...  4.92 us
    another operation x1, local copies, waits for them, and re-layouts, local(): return jnp.stack(results, 0)  4.71 us
    unnamed x18, local copies, waits for them, and re-layouts  3.83 us
    ppermute x1, waiting for transfers between devices, padded(): swapped = lax.ppermute(jnp.where(first, tail, head), axis, [(0, 1), (1, 0)])  3.48 us
    ppermute x1, starting transfers between devices, padded(): swapped = lax.ppermute(jnp.where(first, tail, head), axis, [(0, 1), (1, 0)])  3.03 us
  transfers between devices with their start and end apart: 5, of which 4 were waited for; matrix products, arithmetic and copies ran while one was open for 2% of the time, Pallas kernels for 0%

profile of v12, /device:TPU:0, one launch (start us, length us, event | category | flops | bytes accessed | tf_op | source)
XLA Modules:
  0.0 95.8 jit_solution(16882915930917747195)
XLA Ops:
  0.0 1.4 %sqrt_bitcast_fusion = f32[4,256,128]{2,1,0:T(8,128)S(1)} fusion(f32[4,2,256,128]{3,2,1,0:T(8,128)} %param.3), kind=kLoop, calls=%fused_computation.40 | loop fusion | flops 393216 | bytes 1572864 | tf_op jit(solution)/shard_map/sqrt | solution.py:76
  1.4 3.0 %collective-permute-start = (f32[4,64,128]{2,1,0:T(8,128)S(1)}, f32[4,64,128]{2,1,0:T(8,128)S(1)}, u32[]{:S(2)}, u32[]{:S(2)}) collective-permute-start(f32[4,64,128]{2,1,0:T(8,128)S(1)} %slice_select_fusion), channel_id=1, source_target_pairs={{0,2},{2,0},{1,3},{3,1},{4,6},{6,4},{5,7},{7,5},{8,10},{10,8},{9,1... | collective-permute-start | bytes 393224 | tf_op jit(solution)/shard_map/ppermute | solution.py:28
  4.5 3.5 %collective-permute-done = f32[4,64,128]{2,1,0:T(8,128)S(1)} collective-permute-done((f32[4,64,128]{2,1,0:T(8,128)S(1)}, f32[4,64,128]{2,1,0:T(8,128)S(1)}, u32[]{:S(2)}, u32[]{:S(2)}) %collective-permute-start) | collective-permute-done | bytes 131104 | tf_op jit(solution)/shard_map/ppermute | solution.py:28
  8.1 0.5 fusion.22
  9.3 0.7 fusion.26
  10.1 1.3 %fusion.37 = (f32[128,256,1]{1,0,2:T(8,128)S(1)}, f32[128,256,1]{1,0,2:T(8,128)}) fusion(s32[256]{0:T(256)S(1)} %get-tuple-element.36, s32[128]{0:T(128)S(1)} %iota_add_fusion.5), kind=kLoop, calls=%fused_computation.61 | loop fusion | flops 491520 | bytes 263680 | tf_op jit(solution)/shard_map/cos | solution.py:50
  11.4 0.6 collective-permute-done.1
  12.0 0.9 maximum_select_fusion
  13.3 0.6 fusion.53
  17.5 0.7 copy.43
  18.3 3.9 %collective-permute-start.4 = (bf16[8,2,256,64]{2,3,1,0:T(8,128)(2,1)S(1)}, bf16[8,2,256,64]{2,3,1,0:T(8,128)(2,1)S(1)}, u32[]{:S(2)}, u32[]{:S(2)}) collective-permute-start(bf16[8,2,256,64]{2,3,1,0:T(8,128)(2,1)S(1)} %copy.43), channel_id=1, source_target_pairs={{0,12},{4,0},{8,4},{12,8},{1,13},{5,1},{9,5},{13,9},{2,14},{6,2},{... | collective-permute-start | bytes 1572872 | tf_op jit(solution)/shard_map/ppermute | solution.py:110
  22.2 1.0 %collective-permute-start.2 = (bf16[8,2,256,64]{2,3,1,0:T(8,128)(2,1)S(1)}, bf16[8,2,256,64]{2,3,1,0:T(8,128)(2,1)}, u32[]{:S(2)}, u32[]{:S(2)}) collective-permute-start(bf16[8,2,256,64]{2,3,1,0:T(8,128)(2,1)S(1)} %copy.43), channel_id=1, source_target_pairs={{0,4},{4,8},{8,12},{12,0},{1,5},{5,9},{9,13},{13,1},{2,6},{6,10},{... | collective-permute-start | bytes 1572872 | tf_op jit(solution)/shard_map/ppermute | solution.py:110
  25.8 0.7 compare_select_fusion.1
  26.6 8.0 %collective-permute-done.4 = bf16[8,2,256,64]{2,3,1,0:T(8,128)(2,1)S(1)} collective-permute-done((bf16[8,2,256,64]{2,3,1,0:T(8,128)(2,1)S(1)}, bf16[8,2,256,64]{2,3,1,0:T(8,128)(2,1)S(1)}, u32[]{:S(2)}, u32[]{:S(2)}) %collective-permute-start.4) | collective-permute-done | bytes 524320 | tf_op jit(solution)/shard_map/ppermute | solution.py:110
  34.6 32.8 %collective-permute-done.3 = bf16[8,2,256,64]{2,3,1,0:T(8,128)(2,1)} collective-permute-done((bf16[8,2,256,64]{2,3,1,0:T(8,128)(2,1)S(1)}, bf16[8,2,256,64]{2,3,1,0:T(8,128)(2,1)}, u32[]{:S(2)}, u32[]{:S(2)}) %collective-permute-start.3) | collective-permute-done | bytes 524320 | tf_op jit(solution)/shard_map/ppermute | solution.py:110
  67.4 1.5 %pad_maximum_fusion.1 = bf16[4,8,2,256,64]{3,4,2,1,0:T(8,128)(2,1)S(1)} fusion(bf16[1,8,2,256,64]{3,4,2,1,0:T(8,128)(2,1)S(1)} %bitcast.86, bf16[1,8,2,256,64]{3,4,2,1,0:T(8,128)(2,1)} %bitcast.10, bf16[1,8,2,256,64]{3,4,2,1,0:T(8,128)(2,1)} %bitcast.9, bf16[1,8,2,256,64]{3,4,2,1,0:T(8,128)(2,1)S(1)} %bitcast.85), kind=kLoop, calls=%fused_computation.11 | loop fusion | flops 3145728 | bytes 4194304 | tf_op jit(solution)/shard_map/stack | solution.py:112
  69.7 0.7 fusion.51
  70.4 2.0 %copy.61 = bf16[8,1,256,64]{3,0,2,1:T(8,128)(2,1)} copy(bf16[8,1,256,64]{2,3,1,0:T(8,128)(2,1)} %get-tuple-element.17) | data formatting | bytes 524288
  73.3 0.6 copy-done.1
  74.3 2.6 %convolution_convert_fusion = bf16[256,2,64,128]{3,2,1,0:T(8,128)(2,1)S(1)} fusion(bf16[1,16,256,64]{3,1,0,2:T(8,128)(2,1)S(1)} %get-tuple-element.20, bf16[1,16,256,64]{3,1,0,2:T(8,128)(2,1)S(1)} %get-tuple-element.19, bf16[8,256,128]{2,0,1:T(8,128)(2,1)S(1)} %get-tuple-element.14, bf16[8,256,128]{2,0,1:T(8,128)(2,1)S(1)} %get-tuple-element.13), kind=kOutput, calls=%fused_computation.4 | convolution fusion | flops 141033472 | bytes 10485760 | tf_op jit(solution)/shard_map/ctfs,tfn->fcsn/dot_general | solution.py:61
  77.0 2.8 %convolution_convert_fusion.1 = bf16[256,2,64,128]{3,2,1,0:T(8,128)(2,1)S(1)} fusion(bf16[1,16,256,64]{3,1,0,2:T(8,128)(2,1)S(1)} %get-tuple-element.16, bf16[1,16,256,64]{3,1,0,2:T(8,128)(2,1)S(1)} %get-tuple-element.15, bf16[8,256,128]{2,0,1:T(8,128)(2,1)S(1)} %get-tuple-element.14, bf16[8,256,128]{2,0,1:T(8,128)(2,1)S(1)} %get-tuple-element.13), kind=kOutput, calls=%fused_computation.5 | convolution fusion | flops 141033472 | bytes 10485760 | tf_op jit(solution)/shard_map/ctfs,tfn->fcsn/dot_general | solution.py:61
  79.9 5.4 %fusion.19 = bf16[1,128,64,128]{3,1,2,0:T(8,128)(2,1)S(1)} fusion(f32[64,128]{1,0:T(8,128)S(1)} %copy-done.4, bf16[256,2,64,128]{3,2,1,0:T(8,128)(2,1)S(1)} %convolution_convert_fusion, f32[128,256,1]{1,0,2:T(8,128)S(1)} %copy-done.2, f32[128,256,1]{1,0,2:T(8,128)S(1)} %get-tuple-element.29), kind=kOutput, calls=%fused_computation.19 | convolution fusion | flops 1076035584 | bytes 10780672 | tf_op jit(solution)/shard_map/dot_general | solution.py:129
  85.3 5.4 %fusion.16 = bf16[1,128,64,128]{3,1,2,0:T(8,128)(2,1)S(1)} fusion(f32[64,128]{1,0:T(8,128)S(1)} %copy-done.3, bf16[256,2,64,128]{3,2,1,0:T(8,128)(2,1)S(1)} %convolution_convert_fusion.1, f32[128,256,1]{1,0,2:T(8,128)S(1)} %copy-done.2, f32[128,256,1]{1,0,2:T(8,128)S(1)} %get-tuple-element.29), kind=kOutput, calls=%fused_computation.18 | convolution fusion | flops 1076035584 | bytes 10780672 | tf_op jit(solution)/shard_map/dot_general | solution.py:129
  91.1 4.7 %copy.55 = bf16[2,128,64,128]{3,2,1,0:T(8,128)(2,1)} copy(bf16[2,128,64,128]{3,1,2,0:T(8,128)(2,1)S(1)} %pad_maximum_fusion) | data formatting | bytes 8388608 | tf_op jit(solution)/shard_map/stack | solution.py:146
  (41 shorter events, 3.8 us)
Async XLA Ops:
  1.4 6.5 %collective-permute-start = (f32[4,64,128]{2,1,0:T(8,128)S(1)}, f32[4,64,128]{2,1,0:T(8,128)S(1)}, u32[]{:S(2)}, u32[]{:S(2)}) collective-permute-start(f32[4,64,128]{2,1,0:T(8,128)S(1)} %slice_select_fusion), channel_id=1, source_target_pairs={{0,2},{2,0},{1,3},{3,1},{4,6},{6,4},{5,7},{7,5},{8,10},{10,8},{9,1... | collective-permute-start | bytes 393224 | tf_op jit(solution)/shard_map/ppermute | solution.py:28
  8.1 1.2 %copy-start = (f32[4,2,256,128]{3,2,1,0:T(8,128)S(1)}, f32[4,2,256,128]{3,2,1,0:T(8,128)}, u32[]{:S(2)}) copy-start(f32[4,2,256,128]{3,2,1,0:T(8,128)} %param.3) | copy-start | bytes 3145732
  10.0 2.0 %collective-permute-start.1 = (bf16[4,2,256,128]{3,0,2,1:T(4,128)(2,1)S(1)}, bf16[4,2,256,128]{3,0,2,1:T(4,128)(2,1)S(1)}, u32[]{:S(2)}, u32[]{:S(2)}) collective-permute-start(bf16[4,2,256,128]{3,0,2,1:T(4,128)(2,1)S(1)} %fusion.26), channel_id=1, source_target_pairs={{0,1},{1,0},{2,3},{3,2},{4,5},{5,4},{6,7},{7,6},{8,9},{9,8},{10,11... | collective-permute-start | bytes 1572872 | tf_op jit(solution)/shard_map/ppermute | solution.py:100
  11.4 1.9 %copy-start.5 = (s32[2]{0:T(128)S(1)}, s32[2]{0:T(128)}, u32[]{:S(2)}) copy-start(s32[2]{0:T(128)} %param.4) | copy-start | bytes 28
  13.0 11.4 %copy-start.6 = (s32[4,4]{1,0:T(4,128)S(1)}, s32[4,4]{1,0:T(4,128)}, u32[]{:S(2)}) copy-start(s32[4,4]{1,0:T(4,128)} %param.5) | copy-start | bytes 196
  18.3 16.3 %collective-permute-start.4 = (bf16[8,2,256,64]{2,3,1,0:T(8,128)(2,1)S(1)}, bf16[8,2,256,64]{2,3,1,0:T(8,128)(2,1)S(1)}, u32[]{:S(2)}, u32[]{:S(2)}) collective-permute-start(bf16[8,2,256,64]{2,3,1,0:T(8,128)(2,1)S(1)} %copy.43), channel_id=1, source_target_pairs={{0,12},{4,0},{8,4},{12,8},{1,13},{5,1},{9,5},{13,9},{2,14},{6,2},{... | collective-permute-start | bytes 1572872 | tf_op jit(solution)/shard_map/ppermute | solution.py:110
  22.2 45.2 %collective-permute-start.3 = (bf16[8,2,256,64]{2,3,1,0:T(8,128)(2,1)S(1)}, bf16[8,2,256,64]{2,3,1,0:T(8,128)(2,1)}, u32[]{:S(2)}, u32[]{:S(2)}) collective-permute-start(bf16[8,2,256,64]{2,3,1,0:T(8,128)(2,1)S(1)} %copy.43), channel_id=1, source_target_pairs={{0,8},{4,12},{8,0},{12,4},{1,9},{5,13},{9,1},{13,5},{2,10},{6,14},... | collective-permute-start | bytes 1572872 | tf_op jit(solution)/shard_map/ppermute | solution.py:110
  22.2 45.2 %collective-permute-start.2 = (bf16[8,2,256,64]{2,3,1,0:T(8,128)(2,1)S(1)}, bf16[8,2,256,64]{2,3,1,0:T(8,128)(2,1)}, u32[]{:S(2)}, u32[]{:S(2)}) collective-permute-start(bf16[8,2,256,64]{2,3,1,0:T(8,128)(2,1)S(1)} %copy.43), channel_id=1, source_target_pairs={{0,4},{4,8},{8,12},{12,0},{1,5},{5,9},{9,13},{13,1},{2,6},{6,10},{... | collective-permute-start | bytes 1572872 | tf_op jit(solution)/shard_map/ppermute | solution.py:110
  72.9 1.0 %copy-start.1 = (bf16[8,1,256,64]{3,0,2,1:T(8,128)(2,1)S(1)}, bf16[8,1,256,64]{3,0,2,1:T(8,128)(2,1)}, u32[]{:S(2)}) copy-start(bf16[8,1,256,64]{3,0,2,1:T(8,128)(2,1)} %copy.61) | copy-start | bytes 786436
  77.0 2.9 %copy-start.2 = (f32[128,256,1]{1,0,2:T(8,128)S(1)}, f32[128,256,1]{1,0,2:T(8,128)}, u32[]{:S(2)}) copy-start(f32[128,256,1]{1,0,2:T(8,128)} %get-tuple-element.30) | copy-start | bytes 393220
  77.0 2.9 %copy-start.4 = (f32[64,128]{1,0:T(8,128)S(1)}, f32[64,128]{1,0:T(8,128)}, u32[]{:S(2)}) copy-start(f32[64,128]{1,0:T(8,128)} %get-tuple-element.32) | copy-start | bytes 98308
  79.8 5.4 %copy-start.3 = (f32[64,128]{1,0:T(8,128)S(1)}, f32[64,128]{1,0:T(8,128)}, u32[]{:S(2)}) copy-start(f32[64,128]{1,0:T(8,128)} %get-tuple-element.31) | copy-start | bytes 98308

commit v13 on v12

--- a/solution.py
+++ b/solution.py
@@ -5,10 +5,10 @@
 from jax import lax
 from jax.sharding import PartitionSpec as P
 
+
 SEGS = 8
 STEPS = 2
 SRC = 128
-BLK_DEV = 1
 BAND_BINS = 256
 HALF = 64
 LAGS = 128
@@ -34,11 +34,6 @@
             upper = lax.ppermute(head, axis, [((i + 1) % count, i) for i in range(ends)])
         cells = jnp.concatenate([lower, cells, upper], axis=dim)
     return cells
-
-
-def from_root(block, axis, source):
-    block = jnp.where(lax.axis_index(axis) == source, block, jnp.zeros_like(block))
-    return lax.psum(block, axis)
 
 
 def lag_table(first_bin):
@@ -111,6 +106,8 @@
         )
     candidates = jnp.stack(shifted, 0)
     plan, pair_mask, _ = lax.optimization_barrier((plan, pair_mask, own_half))
+    steps_blocks = [plan[step_number] for step_number in range(STEPS)]
+    mask_rows = [pair_mask[block].astype(jnp.float32) for block in steps_blocks]
     blk_dev = sta_local // SRC
     lag_weights = lag_table(band_position * band_bins).reshape(LAGS, band_bins, 2)
     receiver_ids = sta_position * sta_local + jnp.arange(sta_local, dtype=jnp.int32)
@@ -118,7 +115,7 @@
     block_onehot = ((receiver_ids // SRC)[:, None] == block_columns[None, :]).astype(jnp.float32)
     results = []
     for step_number in range(STEPS):
-        block_number = plan[step_number]
+        block_number = steps_blocks[step_number]
         owner_position = block_number // blk_dev
         distance = (sta_position - owner_position) % sta_count
         held = lax.dynamic_index_in_dim(candidates, distance, 0, keepdims=False)
@@ -132,7 +129,7 @@
             (((1, 2), (0, 1)), ((), ())),
             preferred_element_type=jnp.float32,
         )
-        mask_row = pair_mask[block_number].astype(jnp.float32)
+        mask_row = mask_rows[step_number]
         allowed = jnp.sum(block_onehot * mask_row[None, :], axis=1)
         source_ids = (
             block_number * SRC

time: 96.2 us -> 96.2 us (level)
  no operation moved by 1% of the time
where the time goes in v13:
time: 96.2 us; the launch traced here: 95.8 us
  waiting for transfers between devices  44.9 us (47%)
  matrix products  16.8 us (17%)
  local copies, waits for them, and re-layouts  11.5 us (12%)
  other arithmetic  8.19 us (9%)
  starting transfers between devices  8.02 us (8%)
  between operations  6.4 us (7%)
    ppermute x3, waiting for transfers between devices, local(): lax.ppermute(own_half, 'sta', [(i, (i + shift) % sta_count) for i in rang...  40.8 us
    dot_general x2, matrix products, local(): lax.dot_general(lag_weights, cross_spectra, (((1, 2), (0, 1)), ((), ())),...  10.8 us
    dot_general x2, matrix products, cross_terms(): jnp.einsum('ctfs,tfn->fcsn', left_stack, right_stack, preferred_element_t...  5.48 us
    ppermute x3, starting transfers between devices, local(): lax.ppermute(own_half, 'sta', [(i, (i + shift) % sta_count) for i in rang...  4.92 us
    another operation x1, local copies, waits for them, and re-layouts, local(): return jnp.stack(results, 0)  4.71 us
    unnamed x18, local copies, waits for them, and re-layouts  3.83 us
    ppermute x1, waiting for transfers between devices, padded(): swapped = lax.ppermute(jnp.where(first, tail, head), axis, [(0, 1), (1, 0)])  3.48 us
    ppermute x1, starting transfers between devices, padded(): swapped = lax.ppermute(jnp.where(first, tail, head), axis, [(0, 1), (1, 0)])  3.03 us
  transfers between devices with their start and end apart: 5, of which 4 were waited for; matrix products, arithmetic and copies ran while one was open for 2% of the time, Pallas kernels for 0%

profile of v13, /device:TPU:0, one launch (start us, length us, event | category | flops | bytes accessed | tf_op | source)
XLA Modules:
  0.0 95.8 jit_solution(16882915930917747195)
XLA Ops:
  0.0 1.4 %sqrt_bitcast_fusion = f32[4,256,128]{2,1,0:T(8,128)S(1)} fusion(f32[4,2,256,128]{3,2,1,0:T(8,128)} %param.3), kind=kLoop, calls=%fused_computation.40 | loop fusion | flops 393216 | bytes 1572864 | tf_op jit(solution)/shard_map/sqrt | solution.py:71
  1.4 3.0 %collective-permute-start = (f32[4,64,128]{2,1,0:T(8,128)S(1)}, f32[4,64,128]{2,1,0:T(8,128)S(1)}, u32[]{:S(2)}, u32[]{:S(2)}) collective-permute-start(f32[4,64,128]{2,1,0:T(8,128)S(1)} %slice_select_fusion), channel_id=1, source_target_pairs={{0,2},{2,0},{1,3},{3,1},{4,6},{6,4},{5,7},{7,5},{8,10},{10,8},{9,1... | collective-permute-start | bytes 393224 | tf_op jit(solution)/shard_map/ppermute | solution.py:28
  4.5 3.5 %collective-permute-done = f32[4,64,128]{2,1,0:T(8,128)S(1)} collective-permute-done((f32[4,64,128]{2,1,0:T(8,128)S(1)}, f32[4,64,128]{2,1,0:T(8,128)S(1)}, u32[]{:S(2)}, u32[]{:S(2)}) %collective-permute-start) | collective-permute-done | bytes 131104 | tf_op jit(solution)/shard_map/ppermute | solution.py:28
  8.1 0.5 fusion.22
  9.3 0.7 fusion.26
  10.1 1.3 %fusion.37 = (f32[128,256,1]{1,0,2:T(8,128)S(1)}, f32[128,256,1]{1,0,2:T(8,128)}) fusion(s32[256]{0:T(256)S(1)} %get-tuple-element.36, s32[128]{0:T(128)S(1)} %iota_add_fusion.5), kind=kLoop, calls=%fused_computation.61 | loop fusion | flops 491520 | bytes 263680 | tf_op jit(solution)/shard_map/cos | solution.py:45
  11.4 0.6 collective-permute-done.1
  12.0 0.9 maximum_select_fusion
  13.3 0.6 fusion.53
  17.5 0.7 copy.43
  18.3 3.9 %collective-permute-start.4 = (bf16[8,2,256,64]{2,3,1,0:T(8,128)(2,1)S(1)}, bf16[8,2,256,64]{2,3,1,0:T(8,128)(2,1)S(1)}, u32[]{:S(2)}, u32[]{:S(2)}) collective-permute-start(bf16[8,2,256,64]{2,3,1,0:T(8,128)(2,1)S(1)} %copy.43), channel_id=1, source_target_pairs={{0,12},{4,0},{8,4},{12,8},{1,13},{5,1},{9,5},{13,9},{2,14},{6,2},{... | collective-permute-start | bytes 1572872 | tf_op jit(solution)/shard_map/ppermute | solution.py:105
  22.2 1.0 %collective-permute-start.2 = (bf16[8,2,256,64]{2,3,1,0:T(8,128)(2,1)S(1)}, bf16[8,2,256,64]{2,3,1,0:T(8,128)(2,1)}, u32[]{:S(2)}, u32[]{:S(2)}) collective-permute-start(bf16[8,2,256,64]{2,3,1,0:T(8,128)(2,1)S(1)} %copy.43), channel_id=1, source_target_pairs={{0,4},{4,8},{8,12},{12,0},{1,5},{5,9},{9,13},{13,1},{2,6},{6,10},{... | collective-permute-start | bytes 1572872 | tf_op jit(solution)/shard_map/ppermute | solution.py:105
  25.8 0.7 compare_select_fusion.1
  26.6 8.0 %collective-permute-done.4 = bf16[8,2,256,64]{2,3,1,0:T(8,128)(2,1)S(1)} collective-permute-done((bf16[8,2,256,64]{2,3,1,0:T(8,128)(2,1)S(1)}, bf16[8,2,256,64]{2,3,1,0:T(8,128)(2,1)S(1)}, u32[]{:S(2)}, u32[]{:S(2)}) %collective-permute-start.4) | collective-permute-done | bytes 524320 | tf_op jit(solution)/shard_map/ppermute | solution.py:105
  34.6 32.8 %collective-permute-done.3 = bf16[8,2,256,64]{2,3,1,0:T(8,128)(2,1)} collective-permute-done((bf16[8,2,256,64]{2,3,1,0:T(8,128)(2,1)S(1)}, bf16[8,2,256,64]{2,3,1,0:T(8,128)(2,1)}, u32[]{:S(2)}, u32[]{:S(2)}) %collective-permute-start.3) | collective-permute-done | bytes 524320 | tf_op jit(solution)/shard_map/ppermute | solution.py:105
  67.4 1.5 %pad_maximum_fusion.1 = bf16[4,8,2,256,64]{3,4,2,1,0:T(8,128)(2,1)S(1)} fusion(bf16[1,8,2,256,64]{3,4,2,1,0:T(8,128)(2,1)S(1)} %bitcast.86, bf16[1,8,2,256,64]{3,4,2,1,0:T(8,128)(2,1)} %bitcast.10, bf16[1,8,2,256,64]{3,4,2,1,0:T(8,128)(2,1)} %bitcast.9, bf16[1,8,2,256,64]{3,4,2,1,0:T(8,128)(2,1)S(1)} %bitcast.85), kind=kLoop, calls=%fused_computation.11 | loop fusion | flops 3145728 | bytes 4194304 | tf_op jit(solution)/shard_map/stack | solution.py:107
  69.7 0.7 fusion.51
  70.4 2.0 %copy.61 = bf16[8,1,256,64]{3,0,2,1:T(8,128)(2,1)} copy(bf16[8,1,256,64]{2,3,1,0:T(8,128)(2,1)} %get-tuple-element.17) | data formatting | bytes 524288
  73.3 0.6 copy-done.1
  74.3 2.6 %convolution_convert_fusion = bf16[256,2,64,128]{3,2,1,0:T(8,128)(2,1)S(1)} fusion(bf16[1,16,256,64]{3,1,0,2:T(8,128)(2,1)S(1)} %get-tuple-element.20, bf16[1,16,256,64]{3,1,0,2:T(8,128)(2,1)S(1)} %get-tuple-element.19, bf16[8,256,128]{2,0,1:T(8,128)(2,1)S(1)} %get-tuple-element.14, bf16[8,256,128]{2,0,1:T(8,128)(2,1)S(1)} %get-tuple-element.13), kind=kOutput, calls=%fused_computation.4 | convolution fusion | flops 141033472 | bytes 10485760 | tf_op jit(solution)/shard_map/ctfs,tfn->fcsn/dot_general | solution.py:56
  77.0 2.8 %convolution_convert_fusion.1 = bf16[256,2,64,128]{3,2,1,0:T(8,128)(2,1)S(1)} fusion(bf16[1,16,256,64]{3,1,0,2:T(8,128)(2,1)S(1)} %get-tuple-element.16, bf16[1,16,256,64]{3,1,0,2:T(8,128)(2,1)S(1)} %get-tuple-element.15, bf16[8,256,128]{2,0,1:T(8,128)(2,1)S(1)} %get-tuple-element.14, bf16[8,256,128]{2,0,1:T(8,128)(2,1)S(1)} %get-tuple-element.13), kind=kOutput, calls=%fused_computation.5 | convolution fusion | flops 141033472 | bytes 10485760 | tf_op jit(solution)/shard_map/ctfs,tfn->fcsn/dot_general | solution.py:56
  79.9 5.4 %fusion.19 = bf16[1,128,64,128]{3,1,2,0:T(8,128)(2,1)S(1)} fusion(f32[64,128]{1,0:T(8,128)S(1)} %copy-done.4, bf16[256,2,64,128]{3,2,1,0:T(8,128)(2,1)S(1)} %convolution_convert_fusion, f32[128,256,1]{1,0,2:T(8,128)S(1)} %copy-done.2, f32[128,256,1]{1,0,2:T(8,128)S(1)} %get-tuple-element.29), kind=kOutput, calls=%fused_computation.19 | convolution fusion | flops 1076035584 | bytes 10780672 | tf_op jit(solution)/shard_map/dot_general | solution.py:126
  85.3 5.4 %fusion.16 = bf16[1,128,64,128]{3,1,2,0:T(8,128)(2,1)S(1)} fusion(f32[64,128]{1,0:T(8,128)S(1)} %copy-done.3, bf16[256,2,64,128]{3,2,1,0:T(8,128)(2,1)S(1)} %convolution_convert_fusion.1, f32[128,256,1]{1,0,2:T(8,128)S(1)} %copy-done.2, f32[128,256,1]{1,0,2:T(8,128)S(1)} %get-tuple-element.29), kind=kOutput, calls=%fused_computation.18 | convolution fusion | flops 1076035584 | bytes 10780672 | tf_op jit(solution)/shard_map/dot_general | solution.py:126
  91.1 4.7 %copy.55 = bf16[2,128,64,128]{3,2,1,0:T(8,128)(2,1)} copy(bf16[2,128,64,128]{3,1,2,0:T(8,128)(2,1)S(1)} %pad_maximum_fusion) | data formatting | bytes 8388608 | tf_op jit(solution)/shard_map/stack | solution.py:143
  (41 shorter events, 3.8 us)
Async XLA Ops:
  1.4 6.5 %collective-permute-start = (f32[4,64,128]{2,1,0:T(8,128)S(1)}, f32[4,64,128]{2,1,0:T(8,128)S(1)}, u32[]{:S(2)}, u32[]{:S(2)}) collective-permute-start(f32[4,64,128]{2,1,0:T(8,128)S(1)} %slice_select_fusion), channel_id=1, source_target_pairs={{0,2},{2,0},{1,3},{3,1},{4,6},{6,4},{5,7},{7,5},{8,10},{10,8},{9,1... | collective-permute-start | bytes 393224 | tf_op jit(solution)/shard_map/ppermute | solution.py:28
  8.1 1.2 %copy-start = (f32[4,2,256,128]{3,2,1,0:T(8,128)S(1)}, f32[4,2,256,128]{3,2,1,0:T(8,128)}, u32[]{:S(2)}) copy-start(f32[4,2,256,128]{3,2,1,0:T(8,128)} %param.3) | copy-start | bytes 3145732
  10.0 2.0 %collective-permute-start.1 = (bf16[4,2,256,128]{3,0,2,1:T(4,128)(2,1)S(1)}, bf16[4,2,256,128]{3,0,2,1:T(4,128)(2,1)S(1)}, u32[]{:S(2)}, u32[]{:S(2)}) collective-permute-start(bf16[4,2,256,128]{3,0,2,1:T(4,128)(2,1)S(1)} %fusion.26), channel_id=1, source_target_pairs={{0,1},{1,0},{2,3},{3,2},{4,5},{5,4},{6,7},{7,6},{8,9},{9,8},{10,11... | collective-permute-start | bytes 1572872 | tf_op jit(solution)/shard_map/ppermute | solution.py:95
  11.4 1.9 %copy-start.5 = (s32[2]{0:T(128)S(1)}, s32[2]{0:T(128)}, u32[]{:S(2)}) copy-start(s32[2]{0:T(128)} %param.4) | copy-start | bytes 28
  13.0 11.4 %copy-start.6 = (s32[4,4]{1,0:T(4,128)S(1)}, s32[4,4]{1,0:T(4,128)}, u32[]{:S(2)}) copy-start(s32[4,4]{1,0:T(4,128)} %param.5) | copy-start | bytes 196
  18.3 16.3 %collective-permute-start.4 = (bf16[8,2,256,64]{2,3,1,0:T(8,128)(2,1)S(1)}, bf16[8,2,256,64]{2,3,1,0:T(8,128)(2,1)S(1)}, u32[]{:S(2)}, u32[]{:S(2)}) collective-permute-start(bf16[8,2,256,64]{2,3,1,0:T(8,128)(2,1)S(1)} %copy.43), channel_id=1, source_target_pairs={{0,12},{4,0},{8,4},{12,8},{1,13},{5,1},{9,5},{13,9},{2,14},{6,2},{... | collective-permute-start | bytes 1572872 | tf_op jit(solution)/shard_map/ppermute | solution.py:105
  22.2 45.2 %collective-permute-start.3 = (bf16[8,2,256,64]{2,3,1,0:T(8,128)(2,1)S(1)}, bf16[8,2,256,64]{2,3,1,0:T(8,128)(2,1)}, u32[]{:S(2)}, u32[]{:S(2)}) collective-permute-start(bf16[8,2,256,64]{2,3,1,0:T(8,128)(2,1)S(1)} %copy.43), channel_id=1, source_target_pairs={{0,8},{4,12},{8,0},{12,4},{1,9},{5,13},{9,1},{13,5},{2,10},{6,14},... | collective-permute-start | bytes 1572872 | tf_op jit(solution)/shard_map/ppermute | solution.py:105
  22.2 45.2 %collective-permute-start.2 = (bf16[8,2,256,64]{2,3,1,0:T(8,128)(2,1)S(1)}, bf16[8,2,256,64]{2,3,1,0:T(8,128)(2,1)}, u32[]{:S(2)}, u32[]{:S(2)}) collective-permute-start(bf16[8,2,256,64]{2,3,1,0:T(8,128)(2,1)S(1)} %copy.43), channel_id=1, source_target_pairs={{0,4},{4,8},{8,12},{12,0},{1,5},{5,9},{9,13},{13,1},{2,6},{6,10},{... | collective-permute-start | bytes 1572872 | tf_op jit(solution)/shard_map/ppermute | solution.py:105
  72.9 1.0 %copy-start.1 = (bf16[8,1,256,64]{3,0,2,1:T(8,128)(2,1)S(1)}, bf16[8,1,256,64]{3,0,2,1:T(8,128)(2,1)}, u32[]{:S(2)}) copy-start(bf16[8,1,256,64]{3,0,2,1:T(8,128)(2,1)} %copy.61) | copy-start | bytes 786436
  77.0 2.9 %copy-start.2 = (f32[128,256,1]{1,0,2:T(8,128)S(1)}, f32[128,256,1]{1,0,2:T(8,128)}, u32[]{:S(2)}) copy-start(f32[128,256,1]{1,0,2:T(8,128)} %get-tuple-element.30) | copy-start | bytes 393220
  77.0 2.9 %copy-start.4 = (f32[64,128]{1,0:T(8,128)S(1)}, f32[64,128]{1,0:T(8,128)}, u32[]{:S(2)}) copy-start(f32[64,128]{1,0:T(8,128)} %get-tuple-element.32) | copy-start | bytes 98308
  79.8 5.4 %copy-start.3 = (f32[64,128]{1,0:T(8,128)S(1)}, f32[64,128]{1,0:T(8,128)}, u32[]{:S(2)}) copy-start(f32[64,128]{1,0:T(8,128)} %get-tuple-element.31) | copy-start | bytes 98308

commit v14 on v13

--- a/solution.py
+++ b/solution.py
@@ -93,11 +93,7 @@
     receivers = lax.all_gather(white, "seg", axis=0, tiled=True) if seg_count > 2 else None
     if receivers is None:
         partner = lax.ppermute(white, "seg", [(0, 1), (1, 0)])
-        receivers = jnp.where(
-            seg_position == 0,
-            jnp.concatenate([white, partner], 0),
-            jnp.concatenate([partner, white], 0),
-        )
+        receivers = jnp.concatenate([white, partner], 0)
     own_half = lax.dynamic_slice_in_dim(receivers, seg_position * half_sources, half_sources, 3)
     shifted = [own_half]
     for shift in range(1, sta_count):

time: 96.2 us -> 96.7 us (level)
  other arithmetic: 8.19 us -> 9.68 us
    another operation x2, other arithmetic: 0.8 us -> 1.77 us  [cross_terms(): jnp.stack([jnp.concatenate([src_real, src_imag], 0), jnp.concatenate([src...]
    unnamed x18 -> x20, local copies, waits for them, and re-layouts: 3.83 us -> 3.83 us
  transfers between devices with their start and end apart: 5 -> 5, of which waited for: 4 -> 4; matrix products, arithmetic and copies ran while one was open for 2% -> 3% of each run, Pallas kernels for 0% -> 0%
where the time goes in v14:
time: 96.7 us; the launch traced here: 96.4 us
  waiting for transfers between devices  44.4 us (46%)
  matrix products  16.8 us (17%)
  local copies, waits for them, and re-layouts  11.1 us (11%)
  other arithmetic  9.68 us (10%)
  starting transfers between devices  8.02 us (8%)
  between operations  6.39 us (7%)
    ppermute x3, waiting for transfers between devices, local(): lax.ppermute(own_half, 'sta', [(i, (i + shift) % sta_count) for i in rang...  40.3 us
    dot_general x2, matrix products, local(): lax.dot_general(lag_weights, cross_spectra, (((1, 2), (0, 1)), ((), ())),...  10.8 us
    dot_general x2, matrix products, cross_terms(): jnp.einsum('ctfs,tfn->fcsn', left_stack, right_stack, preferred_element_t...  5.46 us
    ppermute x3, starting transfers between devices, local(): lax.ppermute(own_half, 'sta', [(i, (i + shift) % sta_count) for i in rang...  4.92 us
    another operation x1, local copies, waits for them, and re-layouts, local(): return jnp.stack(results, 0)  4.71 us
    unnamed x20, local copies, waits for them, and re-layouts  3.83 us
    ppermute x1, waiting for transfers between devices, padded(): swapped = lax.ppermute(jnp.where(first, tail, head), axis, [(0, 1), (1, 0)])  3.48 us
    ppermute x1, starting transfers between devices, padded(): swapped = lax.ppermute(jnp.where(first, tail, head), axis, [(0, 1), (1, 0)])  3.03 us
  transfers between devices with their start and end apart: 5, of which 4 were waited for; matrix products, arithmetic and copies ran while one was open for 3% of the time, Pallas kernels for 0%

profile of v14, /device:TPU:0, one launch (start us, length us, event | category | flops | bytes accessed | tf_op | source)
XLA Modules:
  0.0 96.4 jit_solution(8001512616358702954)
XLA Ops:
  0.0 1.4 %sqrt_bitcast_fusion = f32[4,256,128]{2,1,0:T(8,128)S(1)} fusion(f32[4,2,256,128]{3,2,1,0:T(8,128)} %param.3), kind=kLoop, calls=%fused_computation.46 | loop fusion | flops 393216 | bytes 1572864 | tf_op jit(solution)/shard_map/sqrt | solution.py:71
  1.4 3.0 %collective-permute-start = (f32[4,64,128]{2,1,0:T(8,128)S(1)}, f32[4,64,128]{2,1,0:T(8,128)S(1)}, u32[]{:S(2)}, u32[]{:S(2)}) collective-permute-start(f32[4,64,128]{2,1,0:T(8,128)S(1)} %slice_select_fusion), channel_id=1, source_target_pairs={{0,2},{2,0},{1,3},{3,1},{4,6},{6,4},{5,7},{7,5},{8,10},{10,8},{9,1... | collective-permute-start | bytes 393224 | tf_op jit(solution)/shard_map/ppermute | solution.py:28
  4.5 3.5 %collective-permute-done = f32[4,64,128]{2,1,0:T(8,128)S(1)} collective-permute-done((f32[4,64,128]{2,1,0:T(8,128)S(1)}, f32[4,64,128]{2,1,0:T(8,128)S(1)}, u32[]{:S(2)}, u32[]{:S(2)}) %collective-permute-start) | collective-permute-done | bytes 131104 | tf_op jit(solution)/shard_map/ppermute | solution.py:28
  9.3 0.7 fusion.27
  10.2 1.3 %fusion.41 = (f32[128,256,1]{1,0,2:T(8,128)S(1)}, f32[128,256,1]{1,0,2:T(8,128)}) fusion(s32[256]{0:T(256)S(1)} %get-tuple-element.36, s32[128]{0:T(128)S(1)} %iota_add_fusion.5), kind=kLoop, calls=%fused_computation.67 | loop fusion | flops 491520 | bytes 263680 | tf_op jit(solution)/shard_map/cos | solution.py:45
  11.4 0.6 collective-permute-done.1
  12.0 0.9 fusion.22
  12.9 0.6 fusion.57
  17.2 0.7 copy.43
  17.9 3.9 %collective-permute-start.4 = (bf16[8,2,256,64]{2,3,1,0:T(8,128)(2,1)S(1)}, bf16[8,2,256,64]{2,3,1,0:T(8,128)(2,1)S(1)}, u32[]{:S(2)}, u32[]{:S(2)}) collective-permute-start(bf16[8,2,256,64]{2,3,1,0:T(8,128)(2,1)S(1)} %copy.43), channel_id=1, source_target_pairs={{0,12},{4,0},{8,4},{12,8},{1,13},{5,1},{9,5},{13,9},{2,14},{6,2},{... | collective-permute-start | bytes 1572872 | tf_op jit(solution)/shard_map/ppermute | solution.py:101
  21.8 1.0 %collective-permute-start.2 = (bf16[8,2,256,64]{2,3,1,0:T(8,128)(2,1)S(1)}, bf16[8,2,256,64]{2,3,1,0:T(8,128)(2,1)}, u32[]{:S(2)}, u32[]{:S(2)}) collective-permute-start(bf16[8,2,256,64]{2,3,1,0:T(8,128)(2,1)S(1)} %copy.43), channel_id=1, source_target_pairs={{0,4},{4,8},{8,12},{12,0},{1,5},{5,9},{9,13},{13,1},{2,6},{6,10},{... | collective-permute-start | bytes 1572872 | tf_op jit(solution)/shard_map/ppermute | solution.py:101
  25.9 0.7 compare_select_fusion.1
  26.6 7.5 %collective-permute-done.4 = bf16[8,2,256,64]{2,3,1,0:T(8,128)(2,1)S(1)} collective-permute-done((bf16[8,2,256,64]{2,3,1,0:T(8,128)(2,1)S(1)}, bf16[8,2,256,64]{2,3,1,0:T(8,128)(2,1)S(1)}, u32[]{:S(2)}, u32[]{:S(2)}) %collective-permute-start.4) | collective-permute-done | bytes 524320 | tf_op jit(solution)/shard_map/ppermute | solution.py:101
  34.2 32.8 %collective-permute-done.3 = bf16[8,2,256,64]{2,3,1,0:T(8,128)(2,1)} collective-permute-done((bf16[8,2,256,64]{2,3,1,0:T(8,128)(2,1)S(1)}, bf16[8,2,256,64]{2,3,1,0:T(8,128)(2,1)}, u32[]{:S(2)}, u32[]{:S(2)}) %collective-permute-start.3) | collective-permute-done | bytes 524320 | tf_op jit(solution)/shard_map/ppermute | solution.py:101
  67.0 1.5 %pad_maximum_fusion.1 = bf16[4,8,2,256,64]{3,4,2,1,0:T(8,128)(2,1)S(1)} fusion(bf16[1,8,2,256,64]{3,4,2,1,0:T(8,128)(2,1)S(1)} %bitcast.86, bf16[1,8,2,256,64]{3,4,2,1,0:T(8,128)(2,1)} %bitcast.10, bf16[1,8,2,256,64]{3,4,2,1,0:T(8,128)(2,1)} %bitcast.9, bf16[1,8,2,256,64]{3,4,2,1,0:T(8,128)(2,1)S(1)} %bitcast.85), kind=kLoop, calls=%fused_computation.11 | loop fusion | flops 3145728 | bytes 4194304 | tf_op jit(solution)/shard_map/stack | solution.py:103
  69.3 0.7 fusion.55
  70.0 2.0 %copy.61 = bf16[8,1,256,64]{3,0,2,1:T(8,128)(2,1)} copy(bf16[8,1,256,64]{2,3,1,0:T(8,128)(2,1)} %get-tuple-element.17) | data formatting | bytes 524288
  72.9 0.6 copy-done.2
  73.5 1.4 %maximum_bitcast_fusion = (bf16[1,16,256,64]{3,1,0,2:T(8,128)(2,1)S(1)}, bf16[1,16,256,64]{3,1,0,2:T(8,128)(2,1)}) fusion(bf16[8,256,64]{2,0,1:T(8,128)(2,1)S(1)} %bitcast.82, bf16[8,256,64]{2,0,1:T(8,128)(2,1)S(1)} %bitcast.80, bf16[8,256,64]{2,0,1:T(8,128)(2,1)S(1)} %bitcast_negate_fusion.1), kind=kLoop, calls=%fused_computation.29 | loop fusion | flops 2097152 | bytes 1835008 | tf_op jit(solution)/shard_map/stack | solution.py:52
  74.9 2.6 %convolution_convert_fusion = bf16[256,2,64,128]{3,2,1,0:T(8,128)(2,1)S(1)} fusion(bf16[1,16,256,64]{3,1,0,2:T(8,128)(2,1)S(1)} %get-tuple-element.20, bf16[1,16,256,64]{3,1,0,2:T(8,128)(2,1)S(1)} %get-tuple-element.19, bf16[8,256,128]{2,0,1:T(8,128)(2,1)S(1)} %get-tuple-element.14, bf16[8,256,128]{2,0,1:T(8,128)(2,1)S(1)} %get-tuple-element.13), kind=kOutput, calls=%fused_computation.4 | convolution fusion | flops 141033472 | bytes 10485760 | tf_op jit(solution)/shard_map/ctfs,tfn->fcsn/dot_general | solution.py:56
  77.5 2.8 %convolution_convert_fusion.1 = bf16[256,2,64,128]{3,2,1,0:T(8,128)(2,1)S(1)} fusion(bf16[1,16,256,64]{3,1,0,2:T(8,128)(2,1)S(1)} %copy-done.1, bf16[1,16,256,64]{3,1,0,2:T(8,128)(2,1)S(1)} %get-tuple-element.15, bf16[8,256,128]{2,0,1:T(8,128)(2,1)S(1)} %get-tuple-element.14, bf16[8,256,128]{2,0,1:T(8,128)(2,1)S(1)} %get-tuple-element.13), kind=kOutput, calls=%fused_computation.5 | convolution fusion | flops 141033472 | bytes 10485760 | tf_op jit(solution)/shard_map/ctfs,tfn->fcsn/dot_general | solution.py:56
  80.4 5.4 %fusion.19 = bf16[1,128,64,128]{3,1,2,0:T(8,128)(2,1)S(1)} fusion(f32[64,128]{1,0:T(8,128)S(1)} %copy-done.5, bf16[256,2,64,128]{3,2,1,0:T(8,128)(2,1)S(1)} %convolution_convert_fusion, f32[128,256,1]{1,0,2:T(8,128)S(1)} %copy-done.3, f32[128,256,1]{1,0,2:T(8,128)S(1)} %get-tuple-element.29), kind=kOutput, calls=%fused_computation.19 | convolution fusion | flops 1076035584 | bytes 10780672 | tf_op jit(solution)/shard_map/dot_general | solution.py:122
  85.8 5.4 %fusion.16 = bf16[1,128,64,128]{3,1,2,0:T(8,128)(2,1)S(1)} fusion(f32[64,128]{1,0:T(8,128)S(1)} %copy-done.4, bf16[256,2,64,128]{3,2,1,0:T(8,128)(2,1)S(1)} %convolution_convert_fusion.1, f32[128,256,1]{1,0,2:T(8,128)S(1)} %copy-done.3, f32[128,256,1]{1,0,2:T(8,128)S(1)} %get-tuple-element.29), kind=kOutput, calls=%fused_computation.18 | convolution fusion | flops 1076035584 | bytes 10780672 | tf_op jit(solution)/shard_map/dot_general | solution.py:122
  91.6 4.7 %copy.55 = bf16[2,128,64,128]{3,2,1,0:T(8,128)(2,1)} copy(bf16[2,128,64,128]{3,1,2,0:T(8,128)(2,1)S(1)} %pad_maximum_fusion) | data formatting | bytes 8388608 | tf_op jit(solution)/shard_map/stack | solution.py:139
  (42 shorter events, 4.1 us)
Async XLA Ops:
  1.4 6.5 %collective-permute-start = (f32[4,64,128]{2,1,0:T(8,128)S(1)}, f32[4,64,128]{2,1,0:T(8,128)S(1)}, u32[]{:S(2)}, u32[]{:S(2)}) collective-permute-start(f32[4,64,128]{2,1,0:T(8,128)S(1)} %slice_select_fusion), channel_id=1, source_target_pairs={{0,2},{2,0},{1,3},{3,1},{4,6},{6,4},{5,7},{7,5},{8,10},{10,8},{9,1... | collective-permute-start | bytes 393224 | tf_op jit(solution)/shard_map/ppermute | solution.py:28
  8.1 1.2 %copy-start = (f32[4,2,256,128]{3,2,1,0:T(8,128)S(1)}, f32[4,2,256,128]{3,2,1,0:T(8,128)}, u32[]{:S(2)}) copy-start(f32[4,2,256,128]{3,2,1,0:T(8,128)} %param.3) | copy-start | bytes 3145732
  9.3 3.7 %copy-start.6 = (s32[2]{0:T(128)S(1)}, s32[2]{0:T(128)}, u32[]{:S(2)}) copy-start(s32[2]{0:T(128)} %param.4) | copy-start | bytes 28
  10.0 14.0 %copy-start.7 = (s32[4,4]{1,0:T(4,128)S(1)}, s32[4,4]{1,0:T(4,128)}, u32[]{:S(2)}) copy-start(s32[4,4]{1,0:T(4,128)} %param.5) | copy-start | bytes 196
  10.0 2.0 %collective-permute-start.1 = (bf16[4,2,256,128]{3,0,2,1:T(4,128)(2,1)S(1)}, bf16[4,2,256,128]{3,0,2,1:T(4,128)(2,1)S(1)}, u32[]{:S(2)}, u32[]{:S(2)}) collective-permute-start(bf16[4,2,256,128]{3,0,2,1:T(4,128)(2,1)S(1)} %fusion.27), channel_id=1, source_target_pairs={{0,1},{1,0},{2,3},{3,2},{4,5},{5,4},{6,7},{7,6},{8,9},{9,8},{10,11... | collective-permute-start | bytes 1572872 | tf_op jit(solution)/shard_map/ppermute | solution.py:95
  17.9 16.3 %collective-permute-start.4 = (bf16[8,2,256,64]{2,3,1,0:T(8,128)(2,1)S(1)}, bf16[8,2,256,64]{2,3,1,0:T(8,128)(2,1)S(1)}, u32[]{:S(2)}, u32[]{:S(2)}) collective-permute-start(bf16[8,2,256,64]{2,3,1,0:T(8,128)(2,1)S(1)} %copy.43), channel_id=1, source_target_pairs={{0,12},{4,0},{8,4},{12,8},{1,13},{5,1},{9,5},{13,9},{2,14},{6,2},{... | collective-permute-start | bytes 1572872 | tf_op jit(solution)/shard_map/ppermute | solution.py:101
  21.8 45.2 %collective-permute-start.3 = (bf16[8,2,256,64]{2,3,1,0:T(8,128)(2,1)S(1)}, bf16[8,2,256,64]{2,3,1,0:T(8,128)(2,1)}, u32[]{:S(2)}, u32[]{:S(2)}) collective-permute-start(bf16[8,2,256,64]{2,3,1,0:T(8,128)(2,1)S(1)} %copy.43), channel_id=1, source_target_pairs={{0,8},{4,12},{8,0},{12,4},{1,9},{5,13},{9,1},{13,5},{2,10},{6,14},... | collective-permute-start | bytes 1572872 | tf_op jit(solution)/shard_map/ppermute | solution.py:101
  21.8 45.2 %collective-permute-start.2 = (bf16[8,2,256,64]{2,3,1,0:T(8,128)(2,1)S(1)}, bf16[8,2,256,64]{2,3,1,0:T(8,128)(2,1)}, u32[]{:S(2)}, u32[]{:S(2)}) collective-permute-start(bf16[8,2,256,64]{2,3,1,0:T(8,128)(2,1)S(1)} %copy.43), channel_id=1, source_target_pairs={{0,4},{4,8},{8,12},{12,0},{1,5},{5,9},{9,13},{13,1},{2,6},{6,10},{... | collective-permute-start | bytes 1572872 | tf_op jit(solution)/shard_map/ppermute | solution.py:101
  72.5 1.0 %copy-start.2 = (bf16[8,1,256,64]{3,0,2,1:T(8,128)(2,1)S(1)}, bf16[8,1,256,64]{3,0,2,1:T(8,128)(2,1)}, u32[]{:S(2)}) copy-start(bf16[8,1,256,64]{3,0,2,1:T(8,128)(2,1)} %copy.61) | copy-start | bytes 786436
  74.9 2.6 %copy-start.1 = (bf16[1,16,256,64]{3,1,0,2:T(8,128)(2,1)S(1)}, bf16[1,16,256,64]{3,1,0,2:T(8,128)(2,1)}, u32[]{:S(2)}) copy-start(bf16[1,16,256,64]{3,1,0,2:T(8,128)(2,1)} %get-tuple-element.16) | copy-start | bytes 1572868
  77.5 2.9 %copy-start.3 = (f32[128,256,1]{1,0,2:T(8,128)S(1)}, f32[128,256,1]{1,0,2:T(8,128)}, u32[]{:S(2)}) copy-start(f32[128,256,1]{1,0,2:T(8,128)} %get-tuple-element.30) | copy-start | bytes 393220
  77.5 2.9 %copy-start.5 = (f32[64,128]{1,0:T(8,128)S(1)}, f32[64,128]{1,0:T(8,128)}, u32[]{:S(2)}) copy-start(f32[64,128]{1,0:T(8,128)} %get-tuple-element.32) | copy-start | bytes 98308
  80.4 5.4 %copy-start.4 = (f32[64,128]{1,0:T(8,128)S(1)}, f32[64,128]{1,0:T(8,128)}, u32[]{:S(2)}) copy-start(f32[64,128]{1,0:T(8,128)} %get-tuple-element.31) | copy-start | bytes 98308

commit v15 on v13

--- a/solution.py
+++ b/solution.py
@@ -68,8 +68,22 @@
     seg_position = lax.axis_index("seg")
     total_bins = band_bins * lax.axis_size("band")
     half_sources = SRC // lax.axis_size("seg")
-    amplitude = jnp.sqrt(spectra[:, 0] ** 2 + spectra[:, 1] ** 2)
-    extended = padded(amplitude, (("band", 1),), HALF)
+    if lax.axis_size("band") == 2:
+        first = band_position == 0
+        edge = lax.dynamic_slice_in_dim(
+            spectra, (1 - band_position) * (band_bins - HALF), HALF, 2
+        )
+        edge_amplitude = jnp.sqrt(edge[:, 0] ** 2 + edge[:, 1] ** 2)
+        swapped = lax.ppermute(edge_amplitude, "band", [(0, 1), (1, 0)])
+        held, _ = lax.optimization_barrier((spectra, edge_amplitude))
+        amplitude = jnp.sqrt(held[:, 0] ** 2 + held[:, 1] ** 2)
+        zeros = jnp.zeros_like(swapped)
+        extended = jnp.concatenate(
+            [jnp.where(first, zeros, swapped), amplitude, jnp.where(first, swapped, zeros)], 1
+        )
+    else:
+        amplitude = jnp.sqrt(spectra[:, 0] ** 2 + spectra[:, 1] ** 2)
+        extended = padded(amplitude, (("band", 1),), HALF)
     block_width = 2 * HALF
     block_count = band_bins // block_width
     lower_part = extended[:, : block_count * block_width].reshape(

time: 96.2 us -> 95.8 us (level)
  waiting for transfers between devices: 44.9 us -> 43.5 us
  other arithmetic: 8.19 us -> 9.19 us
    ppermute x1, waiting for transfers between devices: 3.48 us -> 2.09 us  [local(): swapped = lax.ppermute(edge_amplitude, 'band', [(0, 1), (1, 0)])]
    sqrt x1 -> x2, other arithmetic: 1.37 us -> 2.39 us  [the longest x1 1.37 us: local(): amplitude = jnp.sqrt(held[:, 0] ** 2 + held[:, 1] ** 2)]
  transfers between devices with their start and end apart: 5 -> 5, of which waited for: 4 -> 4; matrix products, arithmetic and copies ran while one was open for 2% -> 4% of each run, Pallas kernels for 0% -> 0%
where the time goes in v15:
time: 95.8 us; the launch traced here: 95.4 us
  waiting for transfers between devices  43.5 us (45%)
  matrix products  16.8 us (18%)
  local copies, waits for them, and re-layouts  11.5 us (12%)
  other arithmetic  9.19 us (10%)
  starting transfers between devices  8.02 us (8%)
  between operations  6.4 us (7%)
    ppermute x3, waiting for transfers between devices, local(): lax.ppermute(own_half, 'sta', [(i, (i + shift) % sta_count) for i in rang...  40.8 us
    dot_general x2, matrix products, local(): lax.dot_general(lag_weights, cross_spectra, (((1, 2), (0, 1)), ((), ())),...  10.8 us
    dot_general x2, matrix products, cross_terms(): jnp.einsum('ctfs,tfn->fcsn', left_stack, right_stack, preferred_element_t...  5.48 us
    ppermute x3, starting transfers between devices, local(): lax.ppermute(own_half, 'sta', [(i, (i + shift) % sta_count) for i in rang...  4.92 us
    another operation x1, local copies, waits for them, and re-layouts, local(): return jnp.stack(results, 0)  4.71 us
    unnamed x18, local copies, waits for them, and re-layouts  3.83 us
    ppermute x1, starting transfers between devices, local(): swapped = lax.ppermute(edge_amplitude, 'band', [(0, 1), (1, 0)])  3.03 us
    ppermute x1, waiting for transfers between devices, local(): swapped = lax.ppermute(edge_amplitude, 'band', [(0, 1), (1, 0)])  2.09 us
  transfers between devices with their start and end apart: 5, of which 4 were waited for; matrix products, arithmetic and copies ran while one was open for 4% of the time, Pallas kernels for 0%

profile of v15, /device:TPU:0, one launch (start us, length us, event | category | flops | bytes accessed | tf_op | source)
XLA Modules:
  0.0 95.4 jit_solution(14862838965058207420)
XLA Ops:
  0.0 1.0 %fusion.36 = f32[4,64,128]{2,1,0:T(8,128)S(1)} fusion(f32[4,2,256,128]{3,2,1,0:T(8,128)} %param.3, s32[]{:T(128)S(6)} %add.195, s32[]{:T(128)S(6)} %select_n.90), kind=kLoop, calls=%fused_computation.58 | loop fusion | flops 98304 | bytes 393224 | tf_op jit(solution)/shard_map/sqrt | solution.py:76
  1.0 3.0 %collective-permute-start = (f32[4,64,128]{2,1,0:T(8,128)S(1)}, f32[4,64,128]{2,1,0:T(8,128)S(1)}, u32[]{:S(2)}, u32[]{:S(2)}) collective-permute-start(f32[4,64,128]{2,1,0:T(8,128)S(1)} %fusion.36), channel_id=1, source_target_pairs={{0,2},{2,0},{1,3},{3,1},{4,6},{6,4},{5,7},{7,5},{8,10},{10,8},{9,1... | collective-permute-start | bytes 393224 | tf_op jit(solution)/shard_map/ppermute | solution.py:77
  4.1 1.4 %sqrt_bitcast_fusion = f32[4,256,128]{2,1,0:T(8,128)S(1)} fusion(f32[4,2,256,128]{3,2,1,0:T(8,128)} %param.3), kind=kLoop, calls=%fused_computation.40 | loop fusion | flops 393216 | bytes 1572864 | tf_op jit(solution)/shard_map/sqrt | solution.py:79
  5.5 2.1 %collective-permute-done = f32[4,64,128]{2,1,0:T(8,128)S(1)} collective-permute-done((f32[4,64,128]{2,1,0:T(8,128)S(1)}, f32[4,64,128]{2,1,0:T(8,128)S(1)}, u32[]{:S(2)}, u32[]{:S(2)}) %collective-permute-start) | collective-permute-done | bytes 131104 | tf_op jit(solution)/shard_map/ppermute | solution.py:77
  8.9 0.7 fusion.26
  9.8 1.3 %fusion.42 = (f32[128,256,1]{1,0,2:T(8,128)S(1)}, f32[128,256,1]{1,0,2:T(8,128)}) fusion(s32[256]{0:T(256)S(1)} %get-tuple-element.38, s32[128]{0:T(128)S(1)} %iota_add_fusion.5), kind=kLoop, calls=%fused_computation.67 | loop fusion | flops 491520 | bytes 263680 | tf_op jit(solution)/shard_map/cos | solution.py:45
  11.0 0.6 collective-permute-done.1
  11.6 0.9 maximum_select_fusion
  13.0 0.6 fusion.58
  17.2 0.7 copy.48
  17.9 3.9 %collective-permute-start.4 = (bf16[8,2,256,64]{2,3,1,0:T(8,128)(2,1)S(1)}, bf16[8,2,256,64]{2,3,1,0:T(8,128)(2,1)S(1)}, u32[]{:S(2)}, u32[]{:S(2)}) collective-permute-start(bf16[8,2,256,64]{2,3,1,0:T(8,128)(2,1)S(1)} %copy.48), channel_id=1, source_target_pairs={{0,12},{4,0},{8,4},{12,8},{1,13},{5,1},{9,5},{13,9},{2,14},{6,2},{... | collective-permute-start | bytes 1572872 | tf_op jit(solution)/shard_map/ppermute | solution.py:119
  21.8 1.0 %collective-permute-start.2 = (bf16[8,2,256,64]{2,3,1,0:T(8,128)(2,1)S(1)}, bf16[8,2,256,64]{2,3,1,0:T(8,128)(2,1)}, u32[]{:S(2)}, u32[]{:S(2)}) collective-permute-start(bf16[8,2,256,64]{2,3,1,0:T(8,128)(2,1)S(1)} %copy.48), channel_id=1, source_target_pairs={{0,4},{4,8},{8,12},{12,0},{1,5},{5,9},{9,13},{13,1},{2,6},{6,10},{... | collective-permute-start | bytes 1572872 | tf_op jit(solution)/shard_map/ppermute | solution.py:119
  25.4 0.7 compare_select_fusion.1
  26.2 8.0 %collective-permute-done.4 = bf16[8,2,256,64]{2,3,1,0:T(8,128)(2,1)S(1)} collective-permute-done((bf16[8,2,256,64]{2,3,1,0:T(8,128)(2,1)S(1)}, bf16[8,2,256,64]{2,3,1,0:T(8,128)(2,1)S(1)}, u32[]{:S(2)}, u32[]{:S(2)}) %collective-permute-start.4) | collective-permute-done | bytes 524320 | tf_op jit(solution)/shard_map/ppermute | solution.py:119
  34.2 32.8 %collective-permute-done.3 = bf16[8,2,256,64]{2,3,1,0:T(8,128)(2,1)} collective-permute-done((bf16[8,2,256,64]{2,3,1,0:T(8,128)(2,1)S(1)}, bf16[8,2,256,64]{2,3,1,0:T(8,128)(2,1)}, u32[]{:S(2)}, u32[]{:S(2)}) %collective-permute-start.3) | collective-permute-done | bytes 524320 | tf_op jit(solution)/shard_map/ppermute | solution.py:119
  67.0 1.5 %pad_maximum_fusion.1 = bf16[4,8,2,256,64]{3,4,2,1,0:T(8,128)(2,1)S(1)} fusion(bf16[1,8,2,256,64]{3,4,2,1,0:T(8,128)(2,1)S(1)} %bitcast.104, bf16[1,8,2,256,64]{3,4,2,1,0:T(8,128)(2,1)} %bitcast.11, bf16[1,8,2,256,64]{3,4,2,1,0:T(8,128)(2,1)} %bitcast.10, bf16[1,8,2,256,64]{3,4,2,1,0:T(8,128)(2,1)S(1)} %bitcast.103), kind=kLoop, calls=%fused_computation.11 | loop fusion | flops 3145728 | bytes 4194304 | tf_op jit(solution)/shard_map/stack | solution.py:121
  69.3 0.7 fusion.56
  70.0 2.0 %copy.69 = bf16[8,1,256,64]{3,0,2,1:T(8,128)(2,1)} copy(bf16[8,1,256,64]{2,3,1,0:T(8,128)(2,1)} %get-tuple-element.19) | data formatting | bytes 524288
  72.9 0.6 copy-done.1
  73.9 2.6 %convolution_convert_fusion = bf16[256,2,64,128]{3,2,1,0:T(8,128)(2,1)S(1)} fusion(bf16[1,16,256,64]{3,1,0,2:T(8,128)(2,1)S(1)} %get-tuple-element.22, bf16[1,16,256,64]{3,1,0,2:T(8,128)(2,1)S(1)} %get-tuple-element.21, bf16[8,256,128]{2,0,1:T(8,128)(2,1)S(1)} %get-tuple-element.16, bf16[8,256,128]{2,0,1:T(8,128)(2,1)S(1)} %get-tuple-element.15), kind=kOutput, calls=%fused_computation.4 | convolution fusion | flops 141033472 | bytes 10485760 | tf_op jit(solution)/shard_map/ctfs,tfn->fcsn/dot_general | solution.py:56
  76.6 2.8 %convolution_convert_fusion.1 = bf16[256,2,64,128]{3,2,1,0:T(8,128)(2,1)S(1)} fusion(bf16[1,16,256,64]{3,1,0,2:T(8,128)(2,1)S(1)} %get-tuple-element.18, bf16[1,16,256,64]{3,1,0,2:T(8,128)(2,1)S(1)} %get-tuple-element.17, bf16[8,256,128]{2,0,1:T(8,128)(2,1)S(1)} %get-tuple-element.16, bf16[8,256,128]{2,0,1:T(8,128)(2,1)S(1)} %get-tuple-element.15), kind=kOutput, calls=%fused_computation.5 | convolution fusion | flops 141033472 | bytes 10485760 | tf_op jit(solution)/shard_map/ctfs,tfn->fcsn/dot_general | solution.py:56
  79.5 5.4 %fusion.19 = bf16[1,128,64,128]{3,1,2,0:T(8,128)(2,1)S(1)} fusion(f32[64,128]{1,0:T(8,128)S(1)} %copy-done.4, bf16[256,2,64,128]{3,2,1,0:T(8,128)(2,1)S(1)} %convolution_convert_fusion, f32[128,256,1]{1,0,2:T(8,128)S(1)} %copy-done.2, f32[128,256,1]{1,0,2:T(8,128)S(1)} %get-tuple-element.31), kind=kOutput, calls=%fused_computation.19 | convolution fusion | flops 1076035584 | bytes 10780672 | tf_op jit(solution)/shard_map/dot_general | solution.py:140
  84.9 5.4 %fusion.16 = bf16[1,128,64,128]{3,1,2,0:T(8,128)(2,1)S(1)} fusion(f32[64,128]{1,0:T(8,128)S(1)} %copy-done.3, bf16[256,2,64,128]{3,2,1,0:T(8,128)(2,1)S(1)} %convolution_convert_fusion.1, f32[128,256,1]{1,0,2:T(8,128)S(1)} %copy-done.2, f32[128,256,1]{1,0,2:T(8,128)S(1)} %get-tuple-element.31), kind=kOutput, calls=%fused_computation.18 | convolution fusion | flops 1076035584 | bytes 10780672 | tf_op jit(solution)/shard_map/dot_general | solution.py:140
  90.7 4.7 %copy.60 = bf16[2,128,64,128]{3,2,1,0:T(8,128)(2,1)} copy(bf16[2,128,64,128]{3,1,2,0:T(8,128)(2,1)S(1)} %pad_maximum_fusion) | data formatting | bytes 8388608 | tf_op jit(solution)/shard_map/stack | solution.py:157
  (41 shorter events, 4.4 us)
Async XLA Ops:
  1.0 6.5 %collective-permute-start = (f32[4,64,128]{2,1,0:T(8,128)S(1)}, f32[4,64,128]{2,1,0:T(8,128)S(1)}, u32[]{:S(2)}, u32[]{:S(2)}) collective-permute-start(f32[4,64,128]{2,1,0:T(8,128)S(1)} %fusion.36), channel_id=1, source_target_pairs={{0,2},{2,0},{1,3},{3,1},{4,6},{6,4},{5,7},{7,5},{8,10},{10,8},{9,1... | collective-permute-start | bytes 393224 | tf_op jit(solution)/shard_map/ppermute | solution.py:77
  7.7 1.2 %copy-start = (f32[4,2,256,128]{3,2,1,0:T(8,128)S(1)}, f32[4,2,256,128]{3,2,1,0:T(8,128)}, u32[]{:S(2)}) copy-start(f32[4,2,256,128]{3,2,1,0:T(8,128)} %param.3) | copy-start | bytes 3145732
  9.6 2.0 %collective-permute-start.1 = (bf16[4,2,256,128]{3,0,2,1:T(4,128)(2,1)S(1)}, bf16[4,2,256,128]{3,0,2,1:T(4,128)(2,1)S(1)}, u32[]{:S(2)}, u32[]{:S(2)}) collective-permute-start(bf16[4,2,256,128]{3,0,2,1:T(4,128)(2,1)S(1)} %fusion.26), channel_id=1, source_target_pairs={{0,1},{1,0},{2,3},{3,2},{4,5},{5,4},{6,7},{7,6},{8,9},{9,8},{10,11... | collective-permute-start | bytes 1572872 | tf_op jit(solution)/shard_map/ppermute | solution.py:109
  11.0 1.9 %copy-start.5 = (s32[2]{0:T(128)S(1)}, s32[2]{0:T(128)}, u32[]{:S(2)}) copy-start(s32[2]{0:T(128)} %param.4) | copy-start | bytes 28
  12.6 11.4 %copy-start.6 = (s32[4,4]{1,0:T(4,128)S(1)}, s32[4,4]{1,0:T(4,128)}, u32[]{:S(2)}) copy-start(s32[4,4]{1,0:T(4,128)} %param.5) | copy-start | bytes 196
  17.9 16.3 %collective-permute-start.4 = (bf16[8,2,256,64]{2,3,1,0:T(8,128)(2,1)S(1)}, bf16[8,2,256,64]{2,3,1,0:T(8,128)(2,1)S(1)}, u32[]{:S(2)}, u32[]{:S(2)}) collective-permute-start(bf16[8,2,256,64]{2,3,1,0:T(8,128)(2,1)S(1)} %copy.48), channel_id=1, source_target_pairs={{0,12},{4,0},{8,4},{12,8},{1,13},{5,1},{9,5},{13,9},{2,14},{6,2},{... | collective-permute-start | bytes 1572872 | tf_op jit(solution)/shard_map/ppermute | solution.py:119
  21.8 45.2 %collective-permute-start.3 = (bf16[8,2,256,64]{2,3,1,0:T(8,128)(2,1)S(1)}, bf16[8,2,256,64]{2,3,1,0:T(8,128)(2,1)}, u32[]{:S(2)}, u32[]{:S(2)}) collective-permute-start(bf16[8,2,256,64]{2,3,1,0:T(8,128)(2,1)S(1)} %copy.48), channel_id=1, source_target_pairs={{0,8},{4,12},{8,0},{12,4},{1,9},{5,13},{9,1},{13,5},{2,10},{6,14},... | collective-permute-start | bytes 1572872 | tf_op jit(solution)/shard_map/ppermute | solution.py:119
  21.8 45.2 %collective-permute-start.2 = (bf16[8,2,256,64]{2,3,1,0:T(8,128)(2,1)S(1)}, bf16[8,2,256,64]{2,3,1,0:T(8,128)(2,1)}, u32[]{:S(2)}, u32[]{:S(2)}) collective-permute-start(bf16[8,2,256,64]{2,3,1,0:T(8,128)(2,1)S(1)} %copy.48), channel_id=1, source_target_pairs={{0,4},{4,8},{8,12},{12,0},{1,5},{5,9},{9,13},{13,1},{2,6},{6,10},{... | collective-permute-start | bytes 1572872 | tf_op jit(solution)/shard_map/ppermute | solution.py:119
  72.5 1.0 %copy-start.1 = (bf16[8,1,256,64]{3,0,2,1:T(8,128)(2,1)S(1)}, bf16[8,1,256,64]{3,0,2,1:T(8,128)(2,1)}, u32[]{:S(2)}) copy-start(bf16[8,1,256,64]{3,0,2,1:T(8,128)(2,1)} %copy.69) | copy-start | bytes 786436
  76.6 2.9 %copy-start.2 = (f32[128,256,1]{1,0,2:T(8,128)S(1)}, f32[128,256,1]{1,0,2:T(8,128)}, u32[]{:S(2)}) copy-start(f32[128,256,1]{1,0,2:T(8,128)} %get-tuple-element.32) | copy-start | bytes 393220
  76.6 2.9 %copy-start.4 = (f32[64,128]{1,0:T(8,128)S(1)}, f32[64,128]{1,0:T(8,128)}, u32[]{:S(2)}) copy-start(f32[64,128]{1,0:T(8,128)} %get-tuple-element.34) | copy-start | bytes 98308
  79.5 5.4 %copy-start.3 = (f32[64,128]{1,0:T(8,128)S(1)}, f32[64,128]{1,0:T(8,128)}, u32[]{:S(2)}) copy-start(f32[64,128]{1,0:T(8,128)} %get-tuple-element.33) | copy-start | bytes 98308

commit v16 on v15

--- a/solution.py
+++ b/solution.py
@@ -70,9 +70,7 @@
     half_sources = SRC // lax.axis_size("seg")
     if lax.axis_size("band") == 2:
         first = band_position == 0
-        edge = lax.dynamic_slice_in_dim(
-            spectra, (1 - band_position) * (band_bins - HALF), HALF, 2
-        )
+        edge = jnp.where(first, spectra[:, :, band_bins - HALF :], spectra[:, :, :HALF])
         edge_amplitude = jnp.sqrt(edge[:, 0] ** 2 + edge[:, 1] ** 2)
         swapped = lax.ppermute(edge_amplitude, "band", [(0, 1), (1, 0)])
         held, _ = lax.optimization_barrier((spectra, edge_amplitude))
@@ -118,7 +116,6 @@
         shifted.append(
             lax.ppermute(own_half, "sta", [(i, (i + shift) % sta_count) for i in range(sta_count)])
         )
-    candidates = jnp.stack(shifted, 0)
     plan, pair_mask, _ = lax.optimization_barrier((plan, pair_mask, own_half))
     steps_blocks = [plan[step_number] for step_number in range(STEPS)]
     mask_rows = [pair_mask[block].astype(jnp.float32) for block in steps_blocks]
@@ -132,7 +129,9 @@
         block_number = steps_blocks[step_number]
         owner_position = block_number // blk_dev
         distance = (sta_position - owner_position) % sta_count
-        held = lax.dynamic_index_in_dim(candidates, distance, 0, keepdims=False)
+        held = shifted[0]
+        for shift in range(1, sta_count):
+            held = jnp.where(distance == shift, shifted[shift], held)
         sources = lax.dynamic_slice_in_dim(
             held, (block_number % blk_dev) * half_sources, half_sources, 3
         )

time: 95.8 us -> 98.5 us (1.028)
  local copies, waits for them, and re-layouts: 11.5 us -> 15.5 us
  other arithmetic: 9.19 us -> 6.88 us
  waiting for transfers between devices: 43.5 us -> 44.5 us
    ppermute x0 -> x3, local copies, waits for them, and re-layouts: none -> 6.64 us  [local(): lax.ppermute(own_half, 'sta', [(i, (i + shift) % sta_count) for i in rang...]
    unnamed x18 -> x6, local copies, waits for them, and re-layouts: 3.83 us -> 0.02 us
    select_n x0 -> x2, other arithmetic: none -> 2.59 us  [the longest x1 2.56 us: local(): held = jnp.where(distance == shift, shifted[shift], held)]
    another operation x1 -> x0, other arithmetic: 1.46 us -> none  [local(): candidates = jnp.stack(shifted, 0)]
    sqrt x1, other arithmetic: 1.37 us -> 0.17 us  [local(): amplitude = jnp.sqrt(held[:, 0] ** 2 + held[:, 1] ** 2)]
    ppermute x1, waiting for transfers between devices: 2.09 us -> 3.29 us  [local(): swapped = lax.ppermute(edge_amplitude, 'band', [(0, 1), (1, 0)])]
  transfers between devices with their start and end apart: 5 -> 5, of which waited for: 4 -> 4; matrix products, arithmetic and copies ran while one was open for 4% -> 5% of each run, Pallas kernels for 0% -> 0%
where the time goes in v16:
time: 98.5 us; the launch traced here: 98.1 us
  waiting for transfers between devices  44.5 us (45%)
  matrix products  16.8 us (17%)
  local copies, waits for them, and re-layouts  15.5 us (16%)
  starting transfers between devices  7.97 us (8%)
  other arithmetic  6.88 us (7%)
  between operations  6.38 us (6%)
    ppermute x3, waiting for transfers between devices, local(): lax.ppermute(own_half, 'sta', [(i, (i + shift) % sta_count) for i in rang...  40 us
    dot_general x2, matrix products, local(): lax.dot_general(lag_weights, cross_spectra, (((1, 2), (0, 1)), ((), ())),...  10.8 us
    ppermute x3, local copies, waits for them, and re-layouts, local(): lax.ppermute(own_half, 'sta', [(i, (i + shift) % sta_count) for i in rang...  6.64 us
    dot_general x2, matrix products, cross_terms(): jnp.einsum('ctfs,tfn->fcsn', left_stack, right_stack, preferred_element_t...  5.47 us
    ppermute x3, starting transfers between devices, local(): lax.ppermute(own_half, 'sta', [(i, (i + shift) % sta_count) for i in rang...  4.86 us
    another operation x1, local copies, waits for them, and re-layouts, local(): return jnp.stack(results, 0)  4.71 us
    ppermute x1, waiting for transfers between devices, local(): swapped = lax.ppermute(edge_amplitude, 'band', [(0, 1), (1, 0)])  3.29 us
    ppermute x1, starting transfers between devices, local(): swapped = lax.ppermute(edge_amplitude, 'band', [(0, 1), (1, 0)])  3.03 us
  transfers between devices with their start and end apart: 5, of which 4 were waited for; matrix products, arithmetic and copies ran while one was open for 5% of the time, Pallas kernels for 0%

profile of v16, /device:TPU:0, one launch (start us, length us, event | category | flops | bytes accessed | tf_op | source)
XLA Modules:
  0.0 98.1 jit_solution(11830366789063633185)
XLA Ops:
  0.0 1.2 %fusion.52 = (f32[4,2,64,128]{3,2,1,0:T(8,128)S(1)}, f32[4,2,64,128]{3,2,1,0:T(8,128)S(1)}) fusion(f32[4,2,256,128]{3,2,1,0:T(8,128)} %param.3), kind=kLoop, calls=%fused_computation.100 | loop fusion | bytes 1048576 | tf_op jit(solution)/shard_map/slice | solution.py:73
  1.3 3.0 %collective-permute-start = (f32[4,64,128]{2,1,0:T(8,128)S(1)}, f32[4,64,128]{2,1,0:T(8,128)S(1)}, u32[]{:S(2)}, u32[]{:S(2)}) collective-permute-start(f32[4,64,128]{2,1,0:T(8,128)S(1)} %fusion.31), channel_id=1, source_target_pairs={{0,2},{2,0},{1,3},{3,1},{4,6},{6,4},{5,7},{7,5},{8,10},{10,8},{9,1... | collective-permute-start | bytes 393224 | tf_op jit(solution)/shard_map/ppermute | solution.py:75
  4.5 3.3 %collective-permute-done = f32[4,64,128]{2,1,0:T(8,128)S(1)} collective-permute-done((f32[4,64,128]{2,1,0:T(8,128)S(1)}, f32[4,64,128]{2,1,0:T(8,128)S(1)}, u32[]{:S(2)}, u32[]{:S(2)}) %collective-permute-start) | collective-permute-done | bytes 131104 | tf_op jit(solution)/shard_map/ppermute | solution.py:75
  7.9 0.5 fusion.18
  8.9 0.8 fusion.22
  9.8 0.6 fusion.36
  10.4 1.2 %collective-permute-done.1 = bf16[4,2,256,128]{3,0,2,1:T(4,128)(2,1)S(1)} collective-permute-done((bf16[4,2,256,128]{3,0,2,1:T(4,128)(2,1)S(1)}, bf16[4,2,256,128]{3,0,2,1:T(4,128)(2,1)S(1)}, u32[]{:S(2)}, u32[]{:S(2)}) %collective-permute-start.1) | collective-permute-done | bytes 524320 | tf_op jit(solution)/shard_map/ppermute | solution.py:107
  11.7 0.9 maximum_select_fusion
  13.0 0.6 fusion.53
  17.2 1.5 %copy.22 = bf16[8,2,256,64]{2,3,1,0:T(8,128)(2,1)} copy(bf16[8,2,256,64]{3,0,2,1:T(8,128)(2,1)S(1)} %constant_dynamic-slice_fusion.2) | data formatting | bytes 1048576 | tf_op jit(solution)/shard_map/dynamic_slice | solution.py:113
  18.7 3.9 %collective-permute-start.2 = (bf16[8,2,256,64]{2,3,1,0:T(8,128)(2,1)}, bf16[8,2,256,64]{2,3,1,0:T(8,128)(2,1)}, u32[]{:S(2)}, u32[]{:S(2)}) collective-permute-start(bf16[8,2,256,64]{2,3,1,0:T(8,128)(2,1)} %copy.22), channel_id=1, source_target_pairs={{0,12},{4,0},{8,4},{12,8},{1,13},{5,1},{9,5},{13,9},{2,14},{6,2},{... | collective-permute-start | bytes 1572872 | tf_op jit(solution)/shard_map/ppermute | solution.py:117
  22.6 1.0 %collective-permute-start.4 = (bf16[8,2,256,64]{2,3,1,0:T(8,128)(2,1)}, bf16[8,2,256,64]{2,3,1,0:T(8,128)(2,1)}, u32[]{:S(2)}, u32[]{:S(2)}) collective-permute-start(bf16[8,2,256,64]{2,3,1,0:T(8,128)(2,1)} %copy.22), channel_id=1, source_target_pairs={{0,4},{4,8},{8,12},{12,0},{1,5},{5,9},{9,13},{13,1},{2,6},{6,10},{... | collective-permute-start | bytes 1572872 | tf_op jit(solution)/shard_map/ppermute | solution.py:117
  26.4 8.9 %collective-permute-done.2 = bf16[8,2,256,64]{2,3,1,0:T(8,128)(2,1)} collective-permute-done((bf16[8,2,256,64]{2,3,1,0:T(8,128)(2,1)}, bf16[8,2,256,64]{2,3,1,0:T(8,128)(2,1)}, u32[]{:S(2)}, u32[]{:S(2)}) %collective-permute-start.2) | collective-permute-done | bytes 524320 | tf_op jit(solution)/shard_map/ppermute | solution.py:117
  35.3 1.6 %copy.27 = bf16[8,2,256,64]{3,0,2,1:T(8,128)(2,1)S(1)} copy(bf16[8,2,256,64]{2,3,1,0:T(8,128)(2,1)} %collective-permute-done.2) | data formatting | bytes 1048576 | tf_op jit(solution)/shard_map/ppermute | solution.py:117
  36.9 31.1 %collective-permute-done.3 = bf16[8,2,256,64]{2,3,1,0:T(8,128)(2,1)} collective-permute-done((bf16[8,2,256,64]{2,3,1,0:T(8,128)(2,1)}, bf16[8,2,256,64]{2,3,1,0:T(8,128)(2,1)}, u32[]{:S(2)}, u32[]{:S(2)}) %collective-permute-start.3) | collective-permute-done | bytes 524320 | tf_op jit(solution)/shard_map/ppermute | solution.py:117
  68.0 2.5 %copy.26 = bf16[8,2,256,64]{3,0,2,1:T(8,128)(2,1)} copy(bf16[8,2,256,64]{2,3,1,0:T(8,128)(2,1)} %collective-permute-done.3) | data formatting | bytes 1048576 | tf_op jit(solution)/shard_map/ppermute | solution.py:117
  70.5 2.5 %copy.25 = bf16[8,2,256,64]{3,0,2,1:T(8,128)(2,1)} copy(bf16[8,2,256,64]{2,3,1,0:T(8,128)(2,1)} %collective-permute-done.4) | data formatting | bytes 1048576 | tf_op jit(solution)/shard_map/ppermute | solution.py:117
  73.0 2.6 %select_select_fusion.1 = (bf16[8,2,256,64]{3,0,2,1:T(8,128)(2,1)S(1)}, bf16[8,2,256,64]{3,0,2,1:T(8,128)(2,1)S(1)}) fusion(bf16[8,2,256,64]{3,0,2,1:T(8,128)(2,1)S(1)} %copy.27, bf16[8,2,256,64]{3,0,2,1:T(8,128)(2,1)} %copy.26, bf16[8,2,256,64]{3,0,2,1:T(8,128)(2,1)} %copy.25, pred[]{:T(512)S(6)} %eq.48, pred[]{:T(512)S(6)} %eq.47, pred[]{:T(512)S(6)} %eq.46, ...), kind=kLoop, calls=%fused_computation.29 | loop fusion | flops 1572864 | bytes 3145738 | tf_op jit(solution)/shard_map/jit(_where)/select_n | solution.py:134
  75.9 0.4 maximum_bitcast_fusion.3
  76.7 2.6 %convolution_convert_fusion = bf16[256,2,64,128]{3,2,1,0:T(8,128)(2,1)S(1)} fusion(bf16[8,256,128]{2,0,1:T(8,128)(2,1)S(1)} %get-tuple-element.18, bf16[8,256,128]{2,0,1:T(8,128)(2,1)S(1)} %get-tuple-element.17, bf16[1,16,256,64]{3,1,2,0:T(8,128)(2,1)S(1)} %get-tuple-element.26, bf16[1,16,256,64]{3,1,2,0:T(8,128)(2,1)S(1)} %get-tuple-element.25), kind=kOutput, calls=%fused_computation.4 | convolution fusion | flops 141033472 | bytes 10485760 | tf_op jit(solution)/shard_map/ctfs,tfn->fcsn/dot_general | solution.py:56
  79.4 2.8 %convolution_convert_fusion.1 = bf16[256,2,64,128]{3,2,1,0:T(8,128)(2,1)S(1)} fusion(bf16[8,256,128]{2,0,1:T(8,128)(2,1)S(1)} %get-tuple-element.18, bf16[8,256,128]{2,0,1:T(8,128)(2,1)S(1)} %get-tuple-element.17, bf16[1,16,256,64]{3,1,2,0:T(8,128)(2,1)S(1)} %get-tuple-element.24, bf16[1,16,256,64]{3,1,2,0:T(8,128)(2,1)S(1)} %get-tuple-element.23), kind=kOutput, calls=%fused_computation.5 | convolution fusion | flops 141033472 | bytes 10485760 | tf_op jit(solution)/shard_map/ctfs,tfn->fcsn/dot_general | solution.py:56
  82.2 5.4 %fusion.15 = bf16[1,128,64,128]{3,1,2,0:T(8,128)(2,1)S(1)} fusion(f32[64,128]{1,0:T(8,128)S(1)} %get-tuple-element.36, bf16[256,2,64,128]{3,2,1,0:T(8,128)(2,1)S(1)} %convolution_convert_fusion, f32[128,256,1]{1,0,2:T(8,128)S(1)} %get-tuple-element.34, f32[128,256,1]{1,0,2:T(8,128)S(1)} %get-tuple-element.33), kind=kOutput, calls=%fused_computation.16 | convolution fusion | flops 1076035584 | bytes 10780672 | tf_op jit(solution)/shard_map/dot_general | solution.py:139
  87.6 5.4 %fusion.12 = bf16[1,128,64,128]{3,1,2,0:T(8,128)(2,1)S(1)} fusion(f32[64,128]{1,0:T(8,128)S(1)} %get-tuple-element.35, bf16[256,2,64,128]{3,2,1,0:T(8,128)(2,1)S(1)} %convolution_convert_fusion.1, f32[128,256,1]{1,0,2:T(8,128)S(1)} %get-tuple-element.34, f32[128,256,1]{1,0,2:T(8,128)S(1)} %get-tuple-element.33), kind=kOutput, calls=%fused_computation.15 | convolution fusion | flops 1076035584 | bytes 10780672 | tf_op jit(solution)/shard_map/dot_general | solution.py:139
  93.4 4.7 %copy.35 = bf16[2,128,64,128]{3,2,1,0:T(8,128)(2,1)} copy(bf16[2,128,64,128]{3,1,2,0:T(8,128)(2,1)S(1)} %pad_maximum_fusion) | data formatting | bytes 8388608 | tf_op jit(solution)/shard_map/stack | solution.py:156
  (33 shorter events, 2.6 us)
Async XLA Ops:
  0.0 4.3 %copy-start = (f32[4,2,256,128]{3,2,1,0:T(8,128)S(1)}, f32[4,2,256,128]{3,2,1,0:T(8,128)}, u32[]{:S(2)}) copy-start(f32[4,2,256,128]{3,2,1,0:T(8,128)} %param.3) | copy-start | bytes 3145732
  1.3 6.5 %collective-permute-start = (f32[4,64,128]{2,1,0:T(8,128)S(1)}, f32[4,64,128]{2,1,0:T(8,128)S(1)}, u32[]{:S(2)}, u32[]{:S(2)}) collective-permute-start(f32[4,64,128]{2,1,0:T(8,128)S(1)} %fusion.31), channel_id=1, source_target_pairs={{0,2},{2,0},{1,3},{3,1},{4,6},{6,4},{5,7},{7,5},{8,10},{10,8},{9,1... | collective-permute-start | bytes 393224 | tf_op jit(solution)/shard_map/ppermute | solution.py:75
  9.7 2.0 %collective-permute-start.1 = (bf16[4,2,256,128]{3,0,2,1:T(4,128)(2,1)S(1)}, bf16[4,2,256,128]{3,0,2,1:T(4,128)(2,1)S(1)}, u32[]{:S(2)}, u32[]{:S(2)}) collective-permute-start(bf16[4,2,256,128]{3,0,2,1:T(4,128)(2,1)S(1)} %fusion.22), channel_id=1, source_target_pairs={{0,1},{1,0},{2,3},{3,2},{4,5},{5,4},{6,7},{7,6},{8,9},{9,8},{10,11... | collective-permute-start | bytes 1572872 | tf_op jit(solution)/shard_map/ppermute | solution.py:107
  10.4 2.6 %copy-start.1 = (s32[2]{0:T(128)S(1)}, s32[2]{0:T(128)}, u32[]{:S(2)}) copy-start(s32[2]{0:T(128)} %param.4) | copy-start | bytes 28
  12.6 12.2 %copy-start.2 = (s32[4,4]{1,0:T(4,128)S(1)}, s32[4,4]{1,0:T(4,128)}, u32[]{:S(2)}) copy-start(s32[4,4]{1,0:T(4,128)} %param.5) | copy-start | bytes 196
  18.7 16.6 %collective-permute-start.2 = (bf16[8,2,256,64]{2,3,1,0:T(8,128)(2,1)}, bf16[8,2,256,64]{2,3,1,0:T(8,128)(2,1)}, u32[]{:S(2)}, u32[]{:S(2)}) collective-permute-start(bf16[8,2,256,64]{2,3,1,0:T(8,128)(2,1)} %copy.22), channel_id=1, source_target_pairs={{0,12},{4,0},{8,4},{12,8},{1,13},{5,1},{9,5},{13,9},{2,14},{6,2},{... | collective-permute-start | bytes 1572872 | tf_op jit(solution)/shard_map/ppermute | solution.py:117
  22.6 45.4 %collective-permute-start.3 = (bf16[8,2,256,64]{2,3,1,0:T(8,128)(2,1)}, bf16[8,2,256,64]{2,3,1,0:T(8,128)(2,1)}, u32[]{:S(2)}, u32[]{:S(2)}) collective-permute-start(bf16[8,2,256,64]{2,3,1,0:T(8,128)(2,1)} %copy.22), channel_id=1, source_target_pairs={{0,8},{4,12},{8,0},{12,4},{1,9},{5,13},{9,1},{13,5},{2,10},{6,14},... | collective-permute-start | bytes 1572872 | tf_op jit(solution)/shard_map/ppermute | solution.py:117
  22.6 47.9 %collective-permute-start.4 = (bf16[8,2,256,64]{2,3,1,0:T(8,128)(2,1)}, bf16[8,2,256,64]{2,3,1,0:T(8,128)(2,1)}, u32[]{:S(2)}, u32[]{:S(2)}) collective-permute-start(bf16[8,2,256,64]{2,3,1,0:T(8,128)(2,1)} %copy.22), channel_id=1, source_target_pairs={{0,4},{4,8},{8,12},{12,0},{1,5},{5,9},{9,13},{13,1},{2,6},{6,10},{... | collective-permute-start | bytes 1572872 | tf_op jit(solution)/shard_map/ppermute | solution.py:117
